TPU v7x, 512 devices: a whole 4x4x16 slice. The times are simulated.
512 devices in a mesh: dp: 4 (over y), expert: 128 (over x, z, core).
Axes of the slice: x: 4, y: 4, z: 16, core: 2. Of those that a mesh axis runs over, the one named last changes fastest.
Arguments:
- tokens: bfloat16 [12288, 2048], P(('dp', 'expert')), may hold values from -6 to 6
- cotangent: bfloat16 [12288, 2048], P(('dp', 'expert')), may hold values from -6 to 6
- routes: int32 [12288, 8], P(('dp', 'expert')), may hold values from 0 to 127, all different within a row; in each aligned block of 24 rows (0 to 23, 24 to 47, ...) at most 2 rows name the same one
- gates: bfloat16 [12288, 8], P(('dp', 'expert')), may hold values from 0.029907227 to 0.25
- plan: int32 [128], replicated, may hold values from 0 to 127, as said below
- gate_values: bfloat16 [128, 768, 2048], P('expert', 'dp'), may hold values from -0.125 to 0.125
- up_values: bfloat16 [128, 768, 2048], P('expert', 'dp'), may hold values from -0.125 to 0.125
- down_values: bfloat16 [128, 768, 2048], P('expert', 'dp'), may hold values from -0.21875 to 0.21875
- gate_scales: float32 [128, 12, 16], P('expert', 'dp'), may hold values from 0.5 to 2
- up_scales: float32 [128, 12, 16], P('expert', 'dp'), may hold values from 0.5 to 2
- down_scales: float32 [128, 12, 16], P('expert', 'dp'), may hold values from 0.5 to 2
Outputs:
- token_grads: bfloat16 [12288, 2048], P(('dp', 'expert'))
- gate_grads: bfloat16 [128, 768, 2048], P('expert', 'dp')
- up_grads: bfloat16 [128, 768, 2048], P('expert', 'dp')
- down_grads: bfloat16 [128, 768, 2048], P('expert', 'dp')
Inputs may be any that keep to these rules, and one draw needn't show every extreme that they name: `routes`: each token names 8 different experts. Among the 24 tokens of one device no expert is named more than 2 times, and in every draw the tokens of some device name some expert exactly 2 times. plan[plan[s]] = s, and plan[s] is either s or (s + 64) % 128; plan[0] = 64.
All inputs are finite; a program needn't handle non-finite values.
Results may differ from a plain program's by a relative error of at most 0.0082.
Values may be sent and summed in bfloat16 or wider, within the bound.
No kernel may reach another device: no remote copies, remote signals or barrier semaphores. Data moves between devices by JAX's collectives and lax.ppermute only.
A program may use at most 128 MiB of HBM per device.

v0:
```python
import jax
import jax.numpy as jnp
from jax import lax
from jax.sharding import PartitionSpec as P


def swapped(block, axis, stride):
    count = lax.axis_size(axis)
    route = []
    for low in range(count):
        high = low | 1 << stride
        if high != low and high < count:
            route += [(low, high), (high, low)]
    return lax.ppermute(block, axis, route)


def dequantize(values, scales):
    row_block = values.shape[0] // scales.shape[0]
    col_block = values.shape[1] // scales.shape[1]
    spread = jnp.repeat(jnp.repeat(scales, row_block, axis=0), col_block, axis=1)
    return (values.astype(jnp.float32) * spread).astype(jnp.bfloat16)


def slot_choice(route_lists, target, experts, capacity):
    numbers = jnp.arange(experts, dtype=jnp.int32)
    matches = route_lists[..., None] == numbers
    destination = jnp.sum(jnp.where(matches, target, 0), axis=-1)
    flattened = destination.reshape(route_lists.shape[0], -1)
    marked = (flattened[..., None] == numbers).astype(jnp.int32)
    slot_index = jnp.sum((jnp.cumsum(marked, axis=1) - 1) * marked, axis=-1)
    position = flattened * capacity + slot_index
    selected = position[..., None] == jnp.arange(experts * capacity, dtype=jnp.int32)
    return selected.reshape(route_lists.shape + (experts * capacity,))


def contract(left, right, left_dim, right_dim):
    return lax.dot_general(
        left, right, (((left_dim,), (right_dim,)), ((), ())), preferred_element_type=jnp.float32
    )


def expert_work(token_rows, cot_rows, w_gate, w_up, w_down):
    pre_gate = contract(token_rows, w_gate, 1, 1)
    pre_up = contract(token_rows, w_up, 1, 1)
    sigmoid_gate = jax.nn.sigmoid(pre_gate)
    activated = pre_gate * sigmoid_gate
    hidden = (activated * pre_up).astype(jnp.bfloat16)
    grad_hidden = contract(cot_rows, w_down, 1, 1)
    grad_gate = (
        grad_hidden * pre_up * sigmoid_gate * (1.0 + pre_gate * (1.0 - sigmoid_gate))
    ).astype(jnp.bfloat16)
    grad_up = (grad_hidden * activated).astype(jnp.bfloat16)
    gate_grad = contract(grad_gate, token_rows, 0, 0).astype(jnp.bfloat16)
    up_grad = contract(grad_up, token_rows, 0, 0).astype(jnp.bfloat16)
    down_grad = contract(hidden, cot_rows, 0, 0).astype(jnp.bfloat16)
    row_grads = (
        jnp.dot(grad_gate, w_gate, preferred_element_type=jnp.float32)
        + jnp.dot(grad_up, w_up, preferred_element_type=jnp.float32)
    ).astype(jnp.bfloat16)
    return (row_grads, gate_grad, up_grad, down_grad)


def on_device(
    tokens,
    cotangent,
    routes,
    gates,
    plan,
    gate_values,
    up_values,
    down_values,
    gate_scales,
    up_scales,
    down_scales,
):
    tok_count, features = tokens.shape
    top_count = routes.shape[1]
    experts = lax.axis_size("expert")
    replicas = lax.axis_size("dp")
    capacity = max(2, min(tok_count, 5 * tok_count * top_count // (4 * experts)))
    half_bit = experts.bit_length() - 2
    expert_index = lax.axis_index("expert")
    replica_index = lax.axis_index("dp")
    numbers = jnp.arange(experts, dtype=jnp.int32)
    is_moved = jnp.sum(jnp.where(numbers == expert_index, plan, 0)) != expert_index
    w_gate = dequantize(gate_values[0], gate_scales[0])
    w_up = dequantize(up_values[0], up_scales[0])
    w_down = dequantize(down_values[0], down_scales[0])
    all_routes = lax.all_gather(routes[None], "dp", axis=0, tiled=True)
    selected = slot_choice(all_routes, numbers, experts, capacity)
    dispatch = (
        jnp.sum(selected.astype(jnp.int32), axis=2)
        .reshape(replicas, tok_count, experts, capacity)
        .astype(jnp.bfloat16)
    )
    own_dispatch = lax.dynamic_index_in_dim(dispatch, replica_index, 0, keepdims=False)
    own_selected = lax.dynamic_index_in_dim(selected, replica_index, 0, keepdims=False)
    outgoing = jnp.einsum(
        "rec,rd->ecd", own_dispatch, tokens, preferred_element_type=jnp.float32
    ).astype(jnp.bfloat16)
    arrived_tokens = lax.all_to_all(outgoing, "expert", split_axis=0, concat_axis=0, tiled=True)
    token_rows = lax.all_gather(arrived_tokens[None], "dp", axis=0, tiled=True)
    slot_gate = jnp.einsum(
        "rkx,rk->x", own_selected.astype(jnp.float32), gates.astype(jnp.float32)
    ).reshape(experts, capacity)
    lifted = jnp.einsum("rec,rd->ecd", own_dispatch, cotangent, preferred_element_type=jnp.float32)
    cot_out = (lifted * slot_gate[..., None]).astype(jnp.bfloat16)
    arrived_cot = lax.all_to_all(cot_out, "expert", split_axis=0, concat_axis=0, tiled=True)
    cot_rows = lax.all_gather(arrived_cot[None], "dp", axis=0, tiled=True)
    row_grads, gate_grad, up_grad, down_grad = expert_work(
        token_rows.reshape(-1, features), cot_rows.reshape(-1, features), w_gate, w_up, w_down
    )
    row_grads = row_grads.reshape(token_rows.shape)
    returned = lax.all_to_all(row_grads, "expert", split_axis=1, concat_axis=1, tiled=True)
    partial_sums = jnp.einsum(
        "qrec,qecd->qrd", dispatch, returned, preferred_element_type=jnp.float32
    )
    token_grads = lax.psum_scatter(
        partial_sums.reshape(replicas * tok_count, features), "dp", scatter_dimension=0, tiled=True
    ).astype(jnp.bfloat16)
    arrived_grads = swapped((gate_grad, up_grad, down_grad), "expert", half_bit)
    gate_grad = jnp.where(is_moved, arrived_grads[0], gate_grad)
    up_grad = jnp.where(is_moved, arrived_grads[1], up_grad)
    down_grad = jnp.where(is_moved, arrived_grads[2], down_grad)
    return (token_grads, gate_grad[None], up_grad[None], down_grad[None])


def solution(mesh):
    return jax.shard_map(
        on_device,
        mesh=mesh,
        in_specs=(
            P(("dp", "expert"), None),
            P(("dp", "expert"), None),
            P(("dp", "expert"), None),
            P(("dp", "expert"), None),
            P(),
            P("expert", "dp", None),
            P("expert", "dp", None),
            P("expert", "dp", None),
            P("expert", "dp", None),
            P("expert", "dp", None),
            P("expert", "dp", None),
        ),
        out_specs=(
            P(("dp", "expert"), None),
            P("expert", "dp", None),
            P("expert", "dp", None),
            P("expert", "dp", None),
        ),
        check_vma=False,
    )
```

profile of v0, /device:TPU:34, one launch (start us, length us, event | category | flops | bytes accessed | tf_op | source)
XLA Modules:
  0.0 497.3 jit_solution(3561114083639992525)
XLA Ops:
  7.2 0.0 all-gather.9.cloned.1.call-start
  7.2 12.7 %all-gather.3 = s32[4,24,8]{1,2,0:T(8,128)S(1)} all-gather(s32[1,24,8]{1,2,0:T(8,128)} %bitcast.136), channel_id=2, replica_groups=mesh['dp'=4,'expert'=128] {'dp'}, dimensions={0}, use_global_device_ids=true | all-gather | bytes 3840 | tf_op jit(solution)/shard_map/all_gather | solution.py:89
  19.9 0.1 copy.46
  20.0 1.8 select_reduce_fusion.1
  21.8 0.1 eq.58
  21.9 0.2 iota_compare_fusion.1
  22.1 0.4 fusion.23
  22.6 0.2 broadcast_add_fusion
  22.8 0.4 fusion.26
  23.2 0.1 reduce_sum.40
  23.3 0.1 copy.49
  23.4 1.5 convert_reduce_fusion
  25.0 0.1 constant_dynamic-slice_fusion.1
  25.1 0.1 copy.50
  25.2 0.4 convolution_convert_fusion
  25.6 1.1 copy.52
  26.7 74.4 %all_to_all.15 = bf16[128,2,2048]{2,1,0:T(2,128)(2,1)} all-to-all(bf16[128,2,2048]{2,1,0:T(2,128)(2,1)S(1)} %copy.52), channel_id=1, replica_groups=mesh['dp'=4,'expert'=128] {'expert'}, dimensions={0} | all-to-all | bytes 2097152 | tf_op jit(solution)/shard_map/all_to_all | solution.py:101
  101.1 0.0 all-gather.9.cloned.1.call-update
  101.2 0.0 all-gather.7.cloned.1.call-start
  101.2 0.5 iota_compare_fusion
  101.8 0.5 select_reduce_fusion
  102.4 0.1 copy.62
  102.5 0.5 fusion.2
  102.9 1.1 copy.51
  104.0 62.8 %all_to_all.16 = bf16[128,2,2048]{2,1,0:T(2,128)(2,1)} all-to-all(bf16[128,2,2048]{2,1,0:T(2,128)(2,1)S(1)} %copy.51), channel_id=1, replica_groups=mesh['dp'=4,'expert'=128] {'expert'}, dimensions={0} | all-to-all | bytes 2097152 | tf_op jit(solution)/shard_map/all_to_all | solution.py:108
  166.9 0.0 all-gather.7.cloned.1.call-update
  167.0 0.2 convert_bitcast_fusion.4
  167.2 0.3 copy.68
  167.5 0.2 convert_bitcast_fusion.1
  167.6 0.3 copy.72
  167.9 0.4 copy-done.5
  168.3 0.2 convert_bitcast_fusion.3
  168.5 0.3 copy.70
  168.8 1.4 fusion.9
  170.2 1.4 fusion.7
  171.6 1.4 fusion.8
  173.0 7.4 %reshape.125 = bf16[1024,2048]{1,0:T(8,128)(2,1)} reshape(bf16[512,2,2048]{2,1,0:T(2,128)(2,1)} %all-gather.9.cloned.1.call-done) | data formatting | bytes 8388608 | tf_op jit(solution)/shard_map/reshape | solution.py:111
  180.4 5.0 fusion.13
  185.4 2.4 fusion.16
  187.8 26.9 %all-gather.7.cloned.1.call-done = bf16[512,2,2048]{2,1,0:T(2,128)(2,1)} async-done(((bf16[128,2,2048]{2,1,0:T(2,128)(2,1)}), bf16[512,2,2048]{2,1,0:T(2,128)(2,1)}) %all-gather.7.cloned.1.call-update) | async-done | bytes 4194320 | tf_op jit(solution)/shard_map/all_gather | solution.py:109
  214.7 7.2 %reshape.123 = bf16[1024,2048]{1,0:T(8,128)(2,1)} reshape(bf16[512,2,2048]{2,1,0:T(2,128)(2,1)} %all-gather.7.cloned.1.call-done) | data formatting | bytes 8388608 | tf_op jit(solution)/shard_map/reshape | solution.py:111
  221.8 4.5 multiply_convert_fusion.1
  226.4 0.5 broadcast_in_dim.63
  226.9 1.4 fusion.10
  228.3 0.5 broadcast_in_dim.61
  228.7 3.4 add_convert_fusion
  232.1 7.8 %reshape.130 = bf16[4,128,2,2048]{3,2,1,0:T(2,128)(2,1)} reshape(bf16[1024,2048]{1,0:T(8,128)(2,1)} %add_convert_fusion) | data formatting | bytes 8388608 | tf_op jit(solution)/shard_map/reshape | solution.py:113
  240.0 9.3 %copy.53 = bf16[4,128,2,2048]{3,2,0,1:T(2,128)(2,1)} copy(bf16[4,128,2,2048]{3,2,1,0:T(2,128)(2,1)} %reshape.130) | data formatting | bytes 8388608 | tf_op jit(solution)/shard_map/reshape | solution.py:113
  249.3 17.1 %all-to-all-start.2 = ((bf16[4,128,2,2048]{3,2,0,1:T(2,128)(2,1)}), bf16[4,128,2,2048]{3,2,0,1:T(2,128)(2,1)}, u32[]{:S(2)}, u32[]{:S(2)}) async-start(bf16[4,128,2,2048]{3,2,0,1:T(2,128)(2,1)} %copy.53), calls=%async_computation.2 | async-start | bytes 8388608 | tf_op jit(solution)/shard_map/all_to_all | solution.py:114
  266.4 0.0 reduce-scatter.2.cloned.1.call-start
  266.4 0.6 fusion.33
  267.7 3.3 convolution_convert_fusion.3
  271.1 4.4 collective-permute-start
  275.5 1.0 convolution_convert_fusion.2
  276.5 3.1 collective-permute-start.1
  279.7 175.7 %all-to-all-done.2 = bf16[4,128,2,2048]{3,2,0,1:T(2,128)(2,1)} async-done(((bf16[4,128,2,2048]{3,2,0,1:T(2,128)(2,1)}), bf16[4,128,2,2048]{3,2,0,1:T(2,128)(2,1)}, u32[]{:S(2)}, u32[]{:S(2)}) %all-to-all-start.2) | async-done | bytes 4194336 | tf_op jit(solution)/shard_map/all_to_all | solution.py:114
  455.4 7.6 %fusion = f32[4,24,2048,1]{2,1,3,0:T(8,128)} fusion(bf16[4,128,2,2048]{3,2,0,1:T(2,128)(2,1)} %all-to-all-done.2, bf16[4,24,128,2]{1,3,2,0:T(2,128)(2,1)S(1)} %bitcast.122), kind=kOutput, calls=%fused_computation.1 | convolution fusion | flops 100663296 | bytes 5029888 | tf_op jit(solution)/shard_map/qrec,qecd->qrd/dot_general | solution.py:115
  463.0 3.7 convolution_convert_fusion.1
  466.7 2.8 collective-permute-start.2
  469.6 1.0 select_bitcast_fusion.2
  470.5 2.1 select_bitcast_fusion.1
  472.6 15.4 %collective-permute-done.2 = bf16[192,2048]{1,0:T(8,128)(2,1)S(1)} collective-permute-done((bf16[192,2048]{1,0:T(8,128)(2,1)S(1)}, bf16[192,2048]{1,0:T(8,128)(2,1)S(1)}, u32[]{:S(2)}, u32[]{:S(2)}) %collective-permute-start.2) | collective-permute-done | bytes 786464 | tf_op jit(solution)/shard_map/ppermute | solution.py:14
  488.0 1.0 select_bitcast_fusion
  489.0 1.6 convert_element_type.158
  (47 shorter events, 0.3 us)
Async XLA Ops:
  7.2 18.0 %copy-start = (bf16[24,2048]{1,0:T(8,128)(2,1)S(1)}, bf16[24,2048]{1,0:T(8,128)(2,1)}, u32[]{:S(2)}) copy-start(bf16[24,2048]{1,0:T(8,128)(2,1)} %param.11) | copy-start | bytes 294916
  7.2 165.8 %all-gather.9.cloned.1.call-start = ((), (), s32[]{:S(2)}) async-start(), calls=%async_computation.6 | async-start | bytes 5242880 | tf_op jit(solution)/shard_map/all_gather | solution.py:102
  25.0 76.8 %copy-start.9 = (bf16[24,8]{0,1:T(8,128)(2,1)S(1)}, bf16[24,8]{0,1:T(8,128)(2,1)}, u32[]{:S(2)}) copy-start(bf16[24,8]{0,1:T(8,128)(2,1)} %param.14) | copy-start | bytes 1156
  25.1 77.3 %copy-start.8 = (bf16[24,2048]{1,0:T(8,128)(2,1)S(1)}, bf16[24,2048]{1,0:T(8,128)(2,1)}, u32[]{:S(2)}) copy-start(bf16[24,2048]{1,0:T(8,128)(2,1)} %param.12) | copy-start | bytes 294916
  101.1 65.8 %copy-start.10 = (f32[1,3,16]{2,0,1:T(1,128)S(1)}, f32[1,3,16]{2,0,1:T(1,128)}, u32[]{:S(2)}) copy-start(f32[1,3,16]{2,0,1:T(1,128)} %param.19) | copy-start | bytes 580
  101.2 65.8 %copy-start.11 = (f32[1,3,16]{2,0,1:T(1,128)S(1)}, f32[1,3,16]{2,0,1:T(1,128)}, u32[]{:S(2)}) copy-start(f32[1,3,16]{2,0,1:T(1,128)} %param.20) | copy-start | bytes 580
  101.2 65.8 %copy-start.12 = (f32[1,3,16]{2,0,1:T(1,128)S(1)}, f32[1,3,16]{2,0,1:T(1,128)}, u32[]{:S(2)}) copy-start(f32[1,3,16]{2,0,1:T(1,128)} %param.21) | copy-start | bytes 580
  101.2 65.8 %copy-start.6 = (bf16[1,192,2048]{2,1,0:T(8,128)(2,1)S(1)}, bf16[1,192,2048]{2,1,0:T(8,128)(2,1)}, u32[]{:S(2)}) copy-start(bf16[1,192,2048]{2,1,0:T(8,128)(2,1)} %param.18) | copy-start | bytes 2359300
  101.2 113.5 %all-gather.7.cloned.1.call-start = ((), (), s32[]{:S(2)}) async-start(), calls=%async_computation.5 | async-start | bytes 5242880 | tf_op jit(solution)/shard_map/all_gather | solution.py:109
  104.0 63.4 %copy-start.4 = (bf16[1,192,2048]{2,1,0:T(8,128)(2,1)S(1)}, bf16[1,192,2048]{2,1,0:T(8,128)(2,1)}, u32[]{:S(2)}) copy-start(bf16[1,192,2048]{2,1,0:T(8,128)(2,1)} %param.16) | copy-start | bytes 2359300
  167.2 1.1 copy-start.5
  180.4 5.0 %copy-start.2 = (bf16[1024,2048]{1,0:T(8,128)(2,1)S(1)}, bf16[1024,2048]{1,0:T(8,128)(2,1)}, u32[]{:S(2)}) copy-start(bf16[1024,2048]{1,0:T(8,128)(2,1)} %reshape.125) | copy-start | bytes 12582916
  180.4 5.0 %copy-start.7 = (bf16[192,16,128]{2,1,0:T(8,128)(2,1)S(1)}, bf16[192,16,128]{2,1,0:T(8,128)(2,1)}, u32[]{:S(2)}) copy-start(bf16[192,16,128]{2,1,0:T(8,128)(2,1)} %fusion.8) | copy-start | bytes 2359300
  249.3 17.2 %copy-start.13 = (s32[128]{0:T(128)S(1)}, s32[128]{0:T(128)}, u32[]{:S(2)}) copy-start(s32[128]{0:T(128)} %param.15) | copy-start | bytes 1540
  249.3 206.1 %all-to-all-start.2 = ((bf16[4,128,2,2048]{3,2,0,1:T(2,128)(2,1)}), bf16[4,128,2,2048]{3,2,0,1:T(2,128)(2,1)}, u32[]{:S(2)}, u32[]{:S(2)}) async-start(bf16[4,128,2,2048]{3,2,0,1:T(2,128)(2,1)} %copy.53), calls=%async_computation.2 | async-start | bytes 8388608 | tf_op jit(solution)/shard_map/all_to_all | solution.py:114
  266.4 222.6 %reduce-scatter.2.cloned.1.call-start = ((), (), s32[]{:S(2)}) async-start(), calls=%async_computation.4 | async-start | bytes 983040 | tf_op jit(solution)/shard_map/reduce_scatter | solution.py:118
  267.7 7.8 %copy-start.3 = (bf16[1024,2048]{1,0:T(8,128)(2,1)S(1)}, bf16[1024,2048]{1,0:T(8,128)(2,1)}, u32[]{:S(2)}) copy-start(bf16[1024,2048]{1,0:T(8,128)(2,1)} %reshape.125) | copy-start | bytes 12582916
  271.1 198.5 %collective-permute-start = (bf16[192,2048]{1,0:T(8,128)(2,1)S(1)}, bf16[192,2048]{1,0:T(8,128)(2,1)S(1)}, u32[]{:S(2)}, u32[]{:S(2)}) collective-permute-start(bf16[192,2048]{1,0:T(8,128)(2,1)S(1)} %convolution_convert_fusion.3), channel_id=1, source_target_pairs={{0,64},{64,0},{1,65},{65,1},{2,66},{66,2},{3,67},{67,3},{4,68},{68... | collective-permute-start | bytes 2359304 | tf_op jit(solution)/shard_map/ppermute | solution.py:14
  276.5 194.0 %collective-permute-start.1 = (bf16[192,2048]{1,0:T(8,128)(2,1)S(1)}, bf16[192,2048]{1,0:T(8,128)(2,1)}, u32[]{:S(2)}, u32[]{:S(2)}) collective-permute-start(bf16[192,2048]{1,0:T(8,128)(2,1)S(1)} %convolution_convert_fusion.2), channel_id=1, source_target_pairs={{0,64},{64,0},{1,65},{65,1},{2,66},{66,2},{3,67},{67,3},{4,68},{68... | collective-permute-start | bytes 2359304 | tf_op jit(solution)/shard_map/ppermute | solution.py:14
  463.0 27.6 %copy-start.1 = (bf16[24,2048]{1,0:T(8,128)(2,1)S(1)}, bf16[24,2048]{1,0:T(8,128)(2,1)}, u32[]{:S(2)}) copy-start(bf16[24,2048]{1,0:T(8,128)(2,1)} %param.11) | copy-start | bytes 294916
  466.7 21.3 %collective-permute-start.2 = (bf16[192,2048]{1,0:T(8,128)(2,1)S(1)}, bf16[192,2048]{1,0:T(8,128)(2,1)S(1)}, u32[]{:S(2)}, u32[]{:S(2)}) collective-permute-start(bf16[192,2048]{1,0:T(8,128)(2,1)S(1)} %convolution_convert_fusion.1), channel_id=1, source_target_pairs={{0,64},{64,0},{1,65},{65,1},{2,66},{66,2},{3,67},{67,3},{4,68},{68... | collective-permute-start | bytes 2359304 | tf_op jit(solution)/shard_map/ppermute | solution.py:14
Sparse Core Ops, SparseCore 0:
  101.3 47.5 all-gather.8
  167.0 47.5 all-gather.6
  463.1 22.4 reduce-scatter.1
where the time goes:
time: 506 us; the launch traced here: 497 us
  waiting for transfers between devices  218 us (43%)
  blocking collectives  150 us (30%)
  local copies, waits for them, and re-layouts  36.7 us (7%)
  matrix products  33.3 us (7%)
  starting transfers between devices  27.6 us (5%)
  other arithmetic  16.7 us (3%)
  between operations  15.1 us (3%)
    all_to_all x1, waiting for transfers between devices, on_device(): lax.all_to_all(row_grads, 'expert', split_axis=1, concat_axis=1, tiled=True)  176 us
    all_to_all x1, blocking collectives, on_device(): lax.all_to_all(outgoing, 'expert', split_axis=0, concat_axis=0, tiled=True)  74.4 us
    all_to_all x1, blocking collectives, on_device(): lax.all_to_all(cot_out, 'expert', split_axis=0, concat_axis=0, tiled=True)  62.8 us
    all_gather x1, waiting for transfers between devices, on_device(): cot_rows = lax.all_gather(arrived_cot[None], 'dp', axis=0, tiled=True)  26.9 us
    dot_general x6, matrix products, contract(): lax.dot_general(left, right, (((left_dim,), (right_dim,)), ((), ())), pre...  20 us
    reshape x2, local copies, waits for them, and re-layouts, on_device(): row_grads = row_grads.reshape(token_rows.shape)  17.1 us
    all_to_all x1, starting transfers between devices, on_device(): lax.all_to_all(row_grads, 'expert', split_axis=1, concat_axis=1, tiled=True)  17.1 us
    ppermute x3, waiting for transfers between devices, swapped(): return lax.ppermute(block, axis, route)  15.4 us
  transfers between devices with their start and end apart: 7, of which 3 were waited for; matrix products, arithmetic and copies ran while one was open for 9% of the time, Pallas kernels for 0%

commit v1 on v0

--- a/solution.py
+++ b/solution.py
@@ -21,15 +21,13 @@
     return (values.astype(jnp.float32) * spread).astype(jnp.bfloat16)
 
 
-def slot_choice(route_lists, target, experts, capacity):
+def slot_choice(route_lists, experts, capacity):
     numbers = jnp.arange(experts, dtype=jnp.int32)
-    matches = route_lists[..., None] == numbers
-    destination = jnp.sum(jnp.where(matches, target, 0), axis=-1)
-    flattened = destination.reshape(route_lists.shape[0], -1)
-    marked = (flattened[..., None] == numbers).astype(jnp.int32)
-    slot_index = jnp.sum((jnp.cumsum(marked, axis=1) - 1) * marked, axis=-1)
+    flattened = route_lists.reshape(-1)
+    marked = (flattened[:, None] == numbers).astype(jnp.int32)
+    slot_index = jnp.sum((jnp.cumsum(marked, axis=0) - 1) * marked, axis=-1)
     position = flattened * capacity + slot_index
-    selected = position[..., None] == jnp.arange(experts * capacity, dtype=jnp.int32)
+    selected = position[:, None] == jnp.arange(experts * capacity, dtype=jnp.int32)
     return selected.reshape(route_lists.shape + (experts * capacity,))
 
 
@@ -74,49 +72,42 @@
     down_scales,
 ):
     tok_count, features = tokens.shape
-    top_count = routes.shape[1]
     experts = lax.axis_size("expert")
     replicas = lax.axis_size("dp")
-    capacity = max(2, min(tok_count, 5 * tok_count * top_count // (4 * experts)))
+    capacity = 2
     half_bit = experts.bit_length() - 2
     expert_index = lax.axis_index("expert")
-    replica_index = lax.axis_index("dp")
     numbers = jnp.arange(experts, dtype=jnp.int32)
     is_moved = jnp.sum(jnp.where(numbers == expert_index, plan, 0)) != expert_index
     w_gate = dequantize(gate_values[0], gate_scales[0])
     w_up = dequantize(up_values[0], up_scales[0])
     w_down = dequantize(down_values[0], down_scales[0])
-    all_routes = lax.all_gather(routes[None], "dp", axis=0, tiled=True)
-    selected = slot_choice(all_routes, numbers, experts, capacity)
-    dispatch = (
-        jnp.sum(selected.astype(jnp.int32), axis=2)
-        .reshape(replicas, tok_count, experts, capacity)
-        .astype(jnp.bfloat16)
+    selected = slot_choice(routes, experts, capacity)
+    dispatch = jnp.sum(selected.astype(jnp.int32), axis=1).reshape(
+        tok_count, experts, capacity
+    ).astype(jnp.bfloat16)
+    outgoing = jnp.einsum(
+        "rec,rd->ecd", dispatch, tokens, preferred_element_type=jnp.float32
+    ).astype(jnp.bfloat16)
+    slot_gate = jnp.einsum(
+        "rkx,rk->x", selected.astype(jnp.float32), gates.astype(jnp.float32)
+    ).reshape(experts, capacity)
+    lifted = jnp.einsum("rec,rd->ecd", dispatch, cotangent, preferred_element_type=jnp.float32)
+    cot_out = (lifted * slot_gate[..., None]).astype(jnp.bfloat16)
+    both = jnp.stack([outgoing, cot_out], axis=0)
+    arrived = lax.all_to_all(both, "expert", split_axis=1, concat_axis=1, tiled=True)
+    gathered = lax.all_gather(arrived, "dp", axis=1, tiled=True)
+    token_rows = gathered[0].reshape(-1, features)
+    cot_rows = gathered[1].reshape(-1, features)
+    row_grads, gate_grad, up_grad, down_grad = expert_work(
+        token_rows, cot_rows, w_gate, w_up, w_down
     )
-    own_dispatch = lax.dynamic_index_in_dim(dispatch, replica_index, 0, keepdims=False)
-    own_selected = lax.dynamic_index_in_dim(selected, replica_index, 0, keepdims=False)
-    outgoing = jnp.einsum(
-        "rec,rd->ecd", own_dispatch, tokens, preferred_element_type=jnp.float32
-    ).astype(jnp.bfloat16)
-    arrived_tokens = lax.all_to_all(outgoing, "expert", split_axis=0, concat_axis=0, tiled=True)
-    token_rows = lax.all_gather(arrived_tokens[None], "dp", axis=0, tiled=True)
-    slot_gate = jnp.einsum(
-        "rkx,rk->x", own_selected.astype(jnp.float32), gates.astype(jnp.float32)
-    ).reshape(experts, capacity)
-    lifted = jnp.einsum("rec,rd->ecd", own_dispatch, cotangent, preferred_element_type=jnp.float32)
-    cot_out = (lifted * slot_gate[..., None]).astype(jnp.bfloat16)
-    arrived_cot = lax.all_to_all(cot_out, "expert", split_axis=0, concat_axis=0, tiled=True)
-    cot_rows = lax.all_gather(arrived_cot[None], "dp", axis=0, tiled=True)
-    row_grads, gate_grad, up_grad, down_grad = expert_work(
-        token_rows.reshape(-1, features), cot_rows.reshape(-1, features), w_gate, w_up, w_down
+    summed_rows = lax.psum_scatter(
+        row_grads.reshape(replicas, experts, capacity, features), "dp", scatter_dimension=0, tiled=True
     )
-    row_grads = row_grads.reshape(token_rows.shape)
-    returned = lax.all_to_all(row_grads, "expert", split_axis=1, concat_axis=1, tiled=True)
-    partial_sums = jnp.einsum(
-        "qrec,qecd->qrd", dispatch, returned, preferred_element_type=jnp.float32
-    )
-    token_grads = lax.psum_scatter(
-        partial_sums.reshape(replicas * tok_count, features), "dp", scatter_dimension=0, tiled=True
+    returned = lax.all_to_all(summed_rows[0], "expert", split_axis=0, concat_axis=0, tiled=True)
+    token_grads = jnp.einsum(
+        "rec,ecd->rd", dispatch, returned, preferred_element_type=jnp.float32
     ).astype(jnp.bfloat16)
     arrived_grads = swapped((gate_grad, up_grad, down_grad), "expert", half_bit)
     gate_grad = jnp.where(is_moved, arrived_grads[0], gate_grad)

time: 506 us -> 427 us (0.84)
  the two profiles are of different devices: /device:TPU:34 before, /device:TPU:1 now
where the time goes in v1:
time: 427 us; the launch traced here: 426 us
  waiting for transfers between devices  179 us (42%)
  blocking collectives  119 us (28%)
  local copies, waits for them, and re-layouts  48.3 us (11%)
  starting transfers between devices  28.9 us (7%)
  matrix products  26.6 us (6%)
  between operations  15 us (4%)
  other arithmetic  8.66 us (2%)
    all_to_all x1, blocking collectives, on_device(): lax.all_to_all(both, 'expert', split_axis=1, concat_axis=1, tiled=True)  119 us
    all_gather x1, waiting for transfers between devices, on_device(): gathered = lax.all_gather(arrived, 'dp', axis=1, tiled=True)  77.3 us
    reduce_scatter x1, waiting for transfers between devices, on_device(): lax.psum_scatter(row_grads.reshape(replicas, experts, capacity, features)...  55.8 us
    ppermute x3, waiting for transfers between devices, swapped(): return lax.ppermute(block, axis, route)  46.3 us
    dot_general x6, matrix products, contract(): lax.dot_general(left, right, (((left_dim,), (right_dim,)), ((), ())), pre...  19.5 us
    all_to_all x1, starting transfers between devices, on_device(): lax.all_to_all(summed_rows[0], 'expert', split_axis=0, concat_axis=0, til...  16.9 us
    reshape x2, local copies, waits for them, and re-layouts, on_device(): row_grads.reshape(replicas, experts, capacity, features)  13.7 us
    ppermute x3, starting transfers between devices, swapped(): return lax.ppermute(block, axis, route)  11.9 us
  transfers between devices with their start and end apart: 6, of which 5 were waited for; matrix products, arithmetic and copies ran while one was open for 4% of the time, Pallas kernels for 0%

profile of v1, /device:TPU:1, one launch (start us, length us, event | category | flops | bytes accessed | tf_op | source)
XLA Modules:
  0.0 426.3 jit_solution(17713711811344199833)
XLA Ops:
  7.3 0.8 copy.50
  8.0 0.1 eq.62
  8.1 0.1 iota_compare_fusion.1
  8.3 0.1 fusion.26
  8.5 0.2 fusion.29
  8.7 0.1 reduce_sum.30
  8.8 0.1 convert_reduce_fusion
  8.9 0.1 copy.54
  9.1 0.1 copy.61
  9.1 0.1 copy.57
  9.2 0.7 bitcast_convert_fusion
  9.9 0.7 select_reduce_fusion
  10.6 0.1 copy.69
  10.7 0.5 fusion.2
  11.2 0.5 fusion.1
  11.6 0.2 pad_maximum_fusion
  11.9 2.2 copy.58
  14.0 119.5 %all_to_all.10 = bf16[2,128,2,2048]{3,2,0,1:T(2,128)(2,1)} all-to-all(bf16[2,128,2,2048]{3,2,0,1:T(2,128)(2,1)S(1)} %copy.58), channel_id=1, replica_groups=mesh['dp'=4,'expert'=128] {'expert'}, dimensions={1} | all-to-all | bytes 4194304 | tf_op jit(solution)/shard_map/all_to_all | solution.py:98
  133.5 0.0 reduce-scatter.2.cloned.1.call-start
  133.6 0.6 copy-done.9
  134.2 0.5 copy-done.4
  134.7 0.2 convert_bitcast_fusion.1
  134.9 0.3 copy.78
  135.2 0.4 copy-done.10
  135.5 0.5 copy-done.5
  136.0 0.2 convert_bitcast_fusion.3
  136.2 0.3 copy.76
  136.5 0.8 copy-done.6
  137.3 0.2 convert_bitcast_fusion.4
  137.5 0.3 copy.74
  137.8 0.4 copy-done.11
  138.2 0.5 fusion.8
  138.7 1.4 fusion.9
  140.1 0.5 fusion.10
  140.6 77.3 %all-gather.2.cloned.1.call-done = bf16[2,512,2,2048]{3,2,0,1:T(2,128)(2,1)} async-done(((bf16[2,128,2,2048]{3,2,0,1:T(2,128)(2,1)}), bf16[2,512,2,2048]{3,2,0,1:T(2,128)(2,1)}) %all-gather.2.cloned.1.call-update) | async-done | bytes 8388624 | tf_op jit(solution)/shard_map/all_gather | solution.py:99
  217.9 8.4 %fusion.34 = (bf16[1,512,2,2048]{3,2,0,1:T(2,128)(2,1)}, bf16[1,512,2,2048]{3,2,0,1:T(2,128)(2,1)}) fusion(bf16[2,512,2,2048]{3,2,0,1:T(2,128)(2,1)} %all-gather.2.cloned.1.call-done), kind=kLoop, calls=%fused_computation.70 | loop fusion | bytes 16777216 | tf_op jit(solution)/shard_map/slice | solution.py:101
  226.3 7.2 %reshape_squeeze.7 = bf16[1024,2048]{1,0:T(8,128)(2,1)} reshape(bf16[1,512,2,2048]{3,2,0,1:T(2,128)(2,1)} %get-tuple-element.5) | data formatting | bytes 8388608 | tf_op jit(solution)/shard_map/reshape;squeeze | solution.py:100
  233.5 4.8 %fusion.15 = f32[1024,192]{0,1:T(8,128)} fusion(bf16[1024,2048]{1,0:T(8,128)(2,1)} %reshape_squeeze.7, bf16[24,8,16,128]{3,2,1,0:T(8,128)(2,1)S(1)} %bitcast.130), kind=kOutput, calls=%fused_computation.30 | convolution fusion | flops 805306368 | bytes 5767168 | tf_op jit(solution)/shard_map/dot_general | solution.py:35
  238.2 2.4 fusion.18
  240.7 7.2 %reshape_squeeze.6 = bf16[1024,2048]{1,0:T(8,128)(2,1)} reshape(bf16[1,512,2,2048]{3,2,0,1:T(2,128)(2,1)} %get-tuple-element.4) | data formatting | bytes 8388608 | tf_op jit(solution)/shard_map/reshape;squeeze | solution.py:101
  247.9 4.3 %multiply_convert_fusion.1 = (bf16[1024,192]{0,1:T(8,128)(2,1)S(1)}, bf16[1024,192]{0,1:T(8,128)(2,1)S(1)}) fusion(f32[1024,192]{0,1:T(8,128)} %fusion.15, f32[1024,192]{0,1:T(8,128)} %fusion.18, bf16[1024,2048]{1,0:T(8,128)(2,1)} %reshape_squeeze.6, bf16[24,8,16,128]{3,2,1,0:T(8,128)(2,1)S(1)} %bitcast.129), kind=kOutput, calls=%fused_computation.43 | convolution fusion | flops 807862272 | bytes 7340032 | tf_op jit(solution)/shard_map/dot_general | solution.py:35
  252.2 0.5 broadcast_in_dim.39
  252.7 1.4 fusion.12
  254.1 0.5 broadcast_in_dim.37
  254.5 3.4 add_convert_fusion
  258.0 7.7 %reshape.126 = bf16[4,128,2,2048]{3,2,1,0:T(2,128)(2,1)} reshape(bf16[1024,2048]{1,0:T(8,128)(2,1)} %add_convert_fusion) | data formatting | bytes 8388608 | tf_op jit(solution)/shard_map/reshape | solution.py:106
  265.6 6.0 %copy.59 = bf16[4,128,2,2048]{3,1,2,0:T(8,128)(2,1)} copy(bf16[4,128,2,2048]{3,2,1,0:T(2,128)(2,1)} %reshape.126) | data formatting | bytes 8388608 | tf_op jit(solution)/shard_map/reshape | solution.py:106
  271.7 55.8 %reduce-scatter.2.cloned.1.call-done = bf16[1,128,2,2048]{3,1,2,0:T(8,128)(2,1)} async-done(((bf16[4,128,2,2048]{3,1,2,0:T(8,128)(2,1)}), bf16[1,128,2,2048]{3,1,2,0:T(8,128)(2,1)}) %reduce-scatter.2.cloned.1.call-update) | async-done | bytes 1048592 | tf_op jit(solution)/shard_map/reduce_scatter | solution.py:105
  327.5 3.3 copy.60
  330.8 16.9 %all-to-all-start.1 = ((bf16[128,2,2048]{2,1,0:T(2,128)(2,1)}), bf16[128,2,2048]{2,1,0:T(2,128)(2,1)S(1)}, u32[]{:S(2)}, u32[]{:S(2)}) async-start(bf16[128,2,2048]{2,1,0:T(2,128)(2,1)} %copy.60), calls=%async_computation.2 | async-start | bytes 2097152 | tf_op jit(solution)/shard_map/all_to_all | solution.py:108
  347.7 3.7 convolution_convert_fusion.1
  351.4 5.1 %collective-permute-start.2 = (bf16[192,2048]{1,0:T(8,128)(2,1)S(1)}, bf16[192,2048]{1,0:T(8,128)(2,1)}, u32[]{:S(2)}, u32[]{:S(2)}) collective-permute-start(bf16[192,2048]{1,0:T(8,128)(2,1)S(1)} %convolution_convert_fusion.1), channel_id=1, source_target_pairs={{0,64},{64,0},{1,65},{65,1},{2,66},{66,2},{3,67},{67,3},{4,68},{68... | collective-permute-start | bytes 2359304 | tf_op jit(solution)/shard_map/ppermute | solution.py:14
  356.5 0.6 fusion.32
  357.8 3.3 convolution_convert_fusion.2
  361.2 1.9 collective-permute-start.1
  363.1 1.0 convolution_convert_fusion.3
  364.1 4.9 %collective-permute-start = (bf16[192,2048]{1,0:T(8,128)(2,1)S(1)}, bf16[192,2048]{1,0:T(8,128)(2,1)S(1)}, u32[]{:S(2)}, u32[]{:S(2)}) collective-permute-start(bf16[192,2048]{1,0:T(8,128)(2,1)S(1)} %convolution_convert_fusion.3), channel_id=1, source_target_pairs={{0,64},{64,0},{1,65},{65,1},{2,66},{66,2},{3,67},{67,3},{4,68},{68... | collective-permute-start | bytes 2359304 | tf_op jit(solution)/shard_map/ppermute | solution.py:14
  369.0 9.6 %collective-permute-done.2 = bf16[192,2048]{1,0:T(8,128)(2,1)} collective-permute-done((bf16[192,2048]{1,0:T(8,128)(2,1)S(1)}, bf16[192,2048]{1,0:T(8,128)(2,1)}, u32[]{:S(2)}, u32[]{:S(2)}) %collective-permute-start.2) | collective-permute-done | bytes 786464 | tf_op jit(solution)/shard_map/ppermute | solution.py:14
  378.6 1.0 select_bitcast_fusion
  379.6 20.6 %collective-permute-done.1 = bf16[192,2048]{1,0:T(8,128)(2,1)S(1)} collective-permute-done((bf16[192,2048]{1,0:T(8,128)(2,1)S(1)}, bf16[192,2048]{1,0:T(8,128)(2,1)S(1)}, u32[]{:S(2)}, u32[]{:S(2)}) %collective-permute-start.1) | collective-permute-done | bytes 786464 | tf_op jit(solution)/shard_map/ppermute | solution.py:14
  400.2 1.0 select_bitcast_fusion.1
  401.1 16.1 %collective-permute-done = bf16[192,2048]{1,0:T(8,128)(2,1)S(1)} collective-permute-done((bf16[192,2048]{1,0:T(8,128)(2,1)S(1)}, bf16[192,2048]{1,0:T(8,128)(2,1)S(1)}, u32[]{:S(2)}, u32[]{:S(2)}) %collective-permute-start) | collective-permute-done | bytes 786464 | tf_op jit(solution)/shard_map/ppermute | solution.py:14
  417.2 1.0 select_bitcast_fusion.2
  418.2 1.3 fusion.3
  (40 shorter events, 0.3 us)
Async XLA Ops:
  7.2 3.5 copy-start
  7.2 4.0 copy-start.8
  7.2 210.7 %all-gather.2.cloned.1.call-start = ((), (), s32[]{:S(2)}) async-start(), calls=%async_computation.3 | async-start | bytes 10485760 | tf_op jit(solution)/shard_map/all_gather | solution.py:99
  133.5 0.7 copy-start.9
  133.5 1.1 copy-start.4
  133.5 193.9 %reduce-scatter.2.cloned.1.call-start = ((), (), s32[]{:S(2)}) async-start(), calls=%async_computation.4 | async-start | bytes 5242880 | tf_op jit(solution)/shard_map/reduce_scatter | solution.py:105
  134.8 0.7 copy-start.10
  134.9 1.1 copy-start.5
  136.2 1.1 copy-start.6
  137.5 0.7 copy-start.11
  233.5 4.8 %copy-start.2 = (bf16[1024,2048]{1,0:T(8,128)(2,1)S(1)}, bf16[1024,2048]{1,0:T(8,128)(2,1)}, u32[]{:S(2)}) copy-start(bf16[1024,2048]{1,0:T(8,128)(2,1)} %reshape_squeeze.7) | copy-start | bytes 12582916
  233.5 4.8 %copy-start.7 = (bf16[192,16,128]{2,1,0:T(8,128)(2,1)S(1)}, bf16[192,16,128]{2,1,0:T(8,128)(2,1)}, u32[]{:S(2)}) copy-start(bf16[192,16,128]{2,1,0:T(8,128)(2,1)} %fusion.9) | copy-start | bytes 2359300
  330.8 87.4 %all-to-all-start.1 = ((bf16[128,2,2048]{2,1,0:T(2,128)(2,1)}), bf16[128,2,2048]{2,1,0:T(2,128)(2,1)S(1)}, u32[]{:S(2)}, u32[]{:S(2)}) async-start(bf16[128,2,2048]{2,1,0:T(2,128)(2,1)} %copy.60), calls=%async_computation.2 | async-start | bytes 2097152 | tf_op jit(solution)/shard_map/all_to_all | solution.py:108
  347.7 8.8 %copy-start.12 = (s32[128]{0:T(128)S(1)}, s32[128]{0:T(128)}, u32[]{:S(2)}) copy-start(s32[128]{0:T(128)} %param.15) | copy-start | bytes 1540
  351.4 27.2 %collective-permute-start.2 = (bf16[192,2048]{1,0:T(8,128)(2,1)S(1)}, bf16[192,2048]{1,0:T(8,128)(2,1)}, u32[]{:S(2)}, u32[]{:S(2)}) collective-permute-start(bf16[192,2048]{1,0:T(8,128)(2,1)S(1)} %convolution_convert_fusion.1), channel_id=1, source_target_pairs={{0,64},{64,0},{1,65},{65,1},{2,66},{66,2},{3,67},{67,3},{4,68},{68... | collective-permute-start | bytes 2359304 | tf_op jit(solution)/shard_map/ppermute | solution.py:14
  357.8 5.3 %copy-start.3 = (bf16[1024,2048]{1,0:T(8,128)(2,1)S(1)}, bf16[1024,2048]{1,0:T(8,128)(2,1)}, u32[]{:S(2)}) copy-start(bf16[1024,2048]{1,0:T(8,128)(2,1)} %reshape_squeeze.7) | copy-start | bytes 12582916
  361.2 39.0 %collective-permute-start.1 = (bf16[192,2048]{1,0:T(8,128)(2,1)S(1)}, bf16[192,2048]{1,0:T(8,128)(2,1)S(1)}, u32[]{:S(2)}, u32[]{:S(2)}) collective-permute-start(bf16[192,2048]{1,0:T(8,128)(2,1)S(1)} %convolution_convert_fusion.2), channel_id=1, source_target_pairs={{0,64},{64,0},{1,65},{65,1},{2,66},{66,2},{3,67},{67,3},{4,68},{68... | collective-permute-start | bytes 2359304 | tf_op jit(solution)/shard_map/ppermute | solution.py:14
  364.1 53.1 %collective-permute-start = (bf16[192,2048]{1,0:T(8,128)(2,1)S(1)}, bf16[192,2048]{1,0:T(8,128)(2,1)S(1)}, u32[]{:S(2)}, u32[]{:S(2)}) collective-permute-start(bf16[192,2048]{1,0:T(8,128)(2,1)S(1)} %convolution_convert_fusion.3), channel_id=1, source_target_pairs={{0,64},{64,0},{1,65},{65,1},{2,66},{66,2},{3,67},{67,3},{4,68},{68... | collective-permute-start | bytes 2359304 | tf_op jit(solution)/shard_map/ppermute | solution.py:14
  400.2 19.3 %copy-start.1 = (bf16[24,2048]{1,0:T(8,128)(2,1)S(1)}, bf16[24,2048]{1,0:T(8,128)(2,1)}, u32[]{:S(2)}) copy-start(bf16[24,2048]{1,0:T(8,128)(2,1)} %param.11) | copy-start | bytes 294916
Sparse Core Ops, SparseCore 0:
  133.7 84.1 all-gather.1
  271.8 55.6 reduce-scatter.1

commit v2 on v1

--- a/solution.py
+++ b/solution.py
@@ -48,9 +48,9 @@
         grad_hidden * pre_up * sigmoid_gate * (1.0 + pre_gate * (1.0 - sigmoid_gate))
     ).astype(jnp.bfloat16)
     grad_up = (grad_hidden * activated).astype(jnp.bfloat16)
-    gate_grad = contract(grad_gate, token_rows, 0, 0).astype(jnp.bfloat16)
-    up_grad = contract(grad_up, token_rows, 0, 0).astype(jnp.bfloat16)
-    down_grad = contract(hidden, cot_rows, 0, 0).astype(jnp.bfloat16)
+    gate_grad = contract(grad_gate, token_rows, 0, 0)
+    up_grad = contract(grad_up, token_rows, 0, 0)
+    down_grad = contract(hidden, cot_rows, 0, 0)
     row_grads = (
         jnp.dot(grad_gate, w_gate, preferred_element_type=jnp.float32)
         + jnp.dot(grad_up, w_up, preferred_element_type=jnp.float32)
@@ -79,10 +79,15 @@
     expert_index = lax.axis_index("expert")
     numbers = jnp.arange(experts, dtype=jnp.int32)
     is_moved = jnp.sum(jnp.where(numbers == expert_index, plan, 0)) != expert_index
-    w_gate = dequantize(gate_values[0], gate_scales[0])
-    w_up = dequantize(up_values[0], up_scales[0])
-    w_down = dequantize(down_values[0], down_scales[0])
-    selected = slot_choice(routes, experts, capacity)
+    own = (
+        jnp.concatenate([gate_values, up_values, down_values], axis=0),
+        jnp.concatenate([gate_scales, up_scales, down_scales], axis=0),
+    )
+    partner = swapped(own, "expert", half_bit)
+    values, scales = (jnp.where(is_moved, b, a) for a, b in zip(own, partner))
+    w_gate, w_up, w_down = (dequantize(values[i], scales[i]) for i in range(3))
+    destination = jnp.take(plan, routes, axis=0)
+    selected = slot_choice(destination, experts, capacity)
     dispatch = jnp.sum(selected.astype(jnp.int32), axis=1).reshape(
         tok_count, experts, capacity
     ).astype(jnp.bfloat16)
@@ -94,25 +99,26 @@
     ).reshape(experts, capacity)
     lifted = jnp.einsum("rec,rd->ecd", dispatch, cotangent, preferred_element_type=jnp.float32)
     cot_out = (lifted * slot_gate[..., None]).astype(jnp.bfloat16)
-    both = jnp.stack([outgoing, cot_out], axis=0)
-    arrived = lax.all_to_all(both, "expert", split_axis=1, concat_axis=1, tiled=True)
-    gathered = lax.all_gather(arrived, "dp", axis=1, tiled=True)
-    token_rows = gathered[0].reshape(-1, features)
-    cot_rows = gathered[1].reshape(-1, features)
-    row_grads, gate_grad, up_grad, down_grad = expert_work(
-        token_rows, cot_rows, w_gate, w_up, w_down
-    )
-    summed_rows = lax.psum_scatter(
-        row_grads.reshape(replicas, experts, capacity, features), "dp", scatter_dimension=0, tiled=True
-    )
-    returned = lax.all_to_all(summed_rows[0], "expert", split_axis=0, concat_axis=0, tiled=True)
-    token_grads = jnp.einsum(
-        "rec,ecd->rd", dispatch, returned, preferred_element_type=jnp.float32
-    ).astype(jnp.bfloat16)
-    arrived_grads = swapped((gate_grad, up_grad, down_grad), "expert", half_bit)
-    gate_grad = jnp.where(is_moved, arrived_grads[0], gate_grad)
-    up_grad = jnp.where(is_moved, arrived_grads[1], up_grad)
-    down_grad = jnp.where(is_moved, arrived_grads[2], down_grad)
+    token_sum = jnp.zeros((tok_count, features), jnp.float32)
+    sums = None
+    for chunk in range(capacity):
+        both = jnp.stack([outgoing[:, chunk], cot_out[:, chunk]], axis=0)
+        arrived = lax.all_to_all(both, "expert", split_axis=1, concat_axis=1, tiled=True)
+        gathered = lax.all_gather(arrived, "dp", axis=1, tiled=True)
+        row_grads, gate_grad, up_grad, down_grad = expert_work(
+            gathered[0], gathered[1], w_gate, w_up, w_down
+        )
+        part = (gate_grad, up_grad, down_grad)
+        sums = part if sums is None else tuple(a + b for a, b in zip(sums, part))
+        summed_rows = lax.psum_scatter(
+            row_grads.reshape(replicas, experts, features), "dp", scatter_dimension=0, tiled=True
+        )
+        returned = lax.all_to_all(summed_rows[0], "expert", split_axis=0, concat_axis=0, tiled=True)
+        token_sum = token_sum + jnp.einsum(
+            "re,ed->rd", dispatch[:, :, chunk], returned, preferred_element_type=jnp.float32
+        )
+    token_grads = token_sum.astype(jnp.bfloat16)
+    gate_grad, up_grad, down_grad = (x.astype(jnp.bfloat16) for x in sums)
     return (token_grads, gate_grad[None], up_grad[None], down_grad[None])
 
 

time: 427 us -> 365 us (0.85)
  blocking collectives: 119 us -> 74.6 us
  local copies, waits for them, and re-layouts: 48.3 us -> 21.4 us
  starting transfers between devices: 28.9 us -> 39.7 us
  waiting for transfers between devices: 179 us -> 172 us
    all_gather x1 -> x2, waiting for transfers between devices: 77.3 us -> 0.02 us  [on_device(): gathered = lax.all_gather(arrived, 'dp', axis=1, tiled=True)]
    all_to_all x0 -> x1, waiting for transfers between devices: none -> 51.8 us  [on_device(): lax.all_to_all(both, 'expert', split_axis=1, concat_axis=1, tiled=True)]
    all_to_all x1, blocking collectives: 119 us -> 74.6 us  [on_device(): lax.all_to_all(both, 'expert', split_axis=1, concat_axis=1, tiled=True)]
    all_to_all x1 -> x2, waiting for transfers between devices: 0.01 us -> 32.5 us  [on_device(): lax.all_to_all(summed_rows[0], 'expert', split_axis=0, concat_axis=0, til...]
    reduce_scatter x1 -> x2, waiting for transfers between devices: 55.8 us -> 41.7 us  [on_device(): lax.psum_scatter(row_grads.reshape(replicas, experts, features), 'dp', sc...]
    reshape x2 -> x0, local copies, waits for them, and re-layouts: 13.7 us -> none  [on_device(): row_grads.reshape(replicas, experts, capacity, features)]
    another operation x6, local copies, waits for them, and re-layouts: 16.6 us -> 3.38 us  [the longest x3 3.35 us: on_device(): both = jnp.stack([outgoing[:, chunk], cot_out[:, chunk]], axis=0)]
    all_to_all x0 -> x1, starting transfers between devices: none -> 8.4 us  [on_device(): lax.all_to_all(both, 'expert', split_axis=1, concat_axis=1, tiled=True)]
  transfers between devices with their start and end apart: 6 -> 9, of which waited for: 5 -> 6; matrix products, arithmetic and copies ran while one was open for 4% -> 14% of each run, Pallas kernels for 0% -> 0%
where the time goes in v2:
time: 365 us; the launch traced here: 364 us
  waiting for transfers between devices  172 us (47%)
  blocking collectives  74.6 us (20%)
  starting transfers between devices  39.7 us (11%)
  matrix products  28.9 us (8%)
  local copies, waits for them, and re-layouts  21.4 us (6%)
  between operations  15.1 us (4%)
  other arithmetic  12.1 us (3%)
    all_to_all x1, blocking collectives, on_device(): lax.all_to_all(both, 'expert', split_axis=1, concat_axis=1, tiled=True)  74.6 us
    all_to_all x1, waiting for transfers between devices, on_device(): lax.all_to_all(both, 'expert', split_axis=1, concat_axis=1, tiled=True)  51.8 us
    ppermute x2, waiting for transfers between devices, swapped(): return lax.ppermute(block, axis, route)  46.4 us
    reduce_scatter x2, waiting for transfers between devices, on_device(): lax.psum_scatter(row_grads.reshape(replicas, experts, features), 'dp', sc...  41.7 us
    all_to_all x2, waiting for transfers between devices, on_device(): lax.all_to_all(summed_rows[0], 'expert', split_axis=0, concat_axis=0, til...  32.5 us
    all_to_all x2, starting transfers between devices, on_device(): lax.all_to_all(summed_rows[0], 'expert', split_axis=0, concat_axis=0, til...  23.9 us
    dot_general x12, matrix products, contract(): lax.dot_general(left, right, (((left_dim,), (right_dim,)), ((), ())), pre...  19.9 us
    unnamed x75, local copies, waits for them, and re-layouts  10.2 us
  transfers between devices with their start and end apart: 9, of which 6 were waited for; matrix products, arithmetic and copies ran while one was open for 14% of the time, Pallas kernels for 0%

profile of v2, /device:TPU:1, one launch (start us, length us, event | category | flops | bytes accessed | tf_op | source)
XLA Modules:
  0.0 364.2 jit_solution(2799810068516038705)
XLA Ops:
  7.3 0.8 copy.62
  8.1 1.6 gather_fusion
  11.0 0.7 select_reduce_fusion
  11.8 0.5 convolution_convert_fusion
  12.3 0.5 fusion
  13.1 1.1 copy.72
  14.2 74.6 %all_to_all.34 = bf16[2,128,2048]{2,0,1:T(2,128)(2,1)S(1)} all-to-all(bf16[2,128,2048]{2,0,1:T(2,128)(2,1)S(1)} %copy.72), channel_id=1, replica_groups=mesh['dp'=4,'expert'=128] {'expert'}, dimensions={1} | all-to-all | bytes 2097152 | tf_op jit(solution)/shard_map/all_to_all | solution.py:106
  88.7 1.4 copy.73
  90.2 2.1 copy.76
  92.3 8.4 %all-to-all-start.2 = ((bf16[2,128,2048]{2,0,1:T(2,128)(2,1)}), bf16[2,128,2048]{2,0,1:T(2,128)(2,1)S(1)}, u32[]{:S(2)}, u32[]{:S(2)}) async-start(bf16[2,128,2048]{2,0,1:T(2,128)(2,1)} %copy.76), calls=%async_computation.3 | async-start | bytes 2097152 | tf_op jit(solution)/shard_map/all_to_all | solution.py:106
  100.8 1.3 constant_dynamic-update-slice_fusion.2
  102.1 1.2 constant_dynamic-update-slice_fusion.1
  103.3 51.8 %all-to-all-done.2 = bf16[2,128,2048]{2,0,1:T(2,128)(2,1)S(1)} async-done(((bf16[2,128,2048]{2,0,1:T(2,128)(2,1)}), bf16[2,128,2048]{2,0,1:T(2,128)(2,1)S(1)}, u32[]{:S(2)}, u32[]{:S(2)}) %all-to-all-start.2) | async-done | bytes 1048608 | tf_op jit(solution)/shard_map/all_to_all | solution.py:106
  155.1 1.3 copy.77
  156.5 1.2 constant_dynamic-update-slice_fusion
  157.7 4.4 %collective-permute-start = (bf16[3,192,2048]{2,1,0:T(8,128)(2,1)S(1)}, bf16[3,192,2048]{2,1,0:T(8,128)(2,1)}, u32[]{:S(2)}, u32[]{:S(2)}) collective-permute-start(bf16[3,192,2048]{2,1,0:T(8,128)(2,1)S(1)} %constant_dynamic-update-slice_fusion), channel_id=1, source_target_pairs={{0,64},{64,0},{1,65},{65,1},{2,66},{66,2},{3,67},{67,3},{4,68},{68... | collective-permute-start | bytes 7077896 | tf_op jit(solution)/shard_map/ppermute | solution.py:14
  162.2 2.5 collective-permute-start.1
  164.8 0.6 fusion.53
  166.1 46.4 %collective-permute-done.1 = f32[3,3,16]{2,0,1:T(4,128)S(1)} collective-permute-done((f32[3,3,16]{2,0,1:T(4,128)S(1)}, f32[3,3,16]{2,0,1:T(4,128)S(1)}, u32[]{:S(2)}, u32[]{:S(2)}) %collective-permute-start.1) | collective-permute-done | bytes 608 | tf_op jit(solution)/shard_map/ppermute | solution.py:14
  212.5 1.9 broadcast_select_fusion
  214.5 0.6 convert_bitcast_fusion.3
  215.1 0.3 copy.94
  215.4 0.3 copy.96
  215.6 0.3 copy.92
  215.9 0.5 fusion.16
  216.5 1.4 fusion.15
  217.9 1.4 fusion.17
  219.2 2.6 fusion.21
  222.1 2.1 fusion.20
  224.1 0.9 multiply_convert_fusion.4
  225.1 0.5 broadcast_in_dim.50
  225.6 0.9 fusion.58
  226.7 0.5 broadcast_in_dim.48
  227.2 2.4 add_convert_fusion.1
  229.9 2.8 fusion.22
  233.0 0.8 fusion.23
  233.8 0.4 copy-done.15
  234.3 0.9 multiply_convert_fusion.2
  235.2 0.6 copy-done.4
  235.8 0.9 fusion.56
  236.7 0.5 copy-done.6
  237.2 2.4 add_convert_fusion
  239.6 22.5 %reduce-scatter.3.cloned.1.call-done = bf16[1,128,2048]{2,1,0:T(8,128)(2,1)} async-done(((bf16[4,128,2048]{2,1,0:T(8,128)(2,1)}), bf16[1,128,2048]{2,1,0:T(8,128)(2,1)}) %reduce-scatter.3.cloned.1.call-update) | async-done | bytes 524304 | tf_op jit(solution)/shard_map/reduce_scatter | solution.py:113
  262.2 0.5 broadcast.82
  262.7 2.0 reduce.2
  264.7 1.2 reshape.200
  265.8 16.8 %all-to-all-start.1 = ((bf16[128,2,1024]{2,1,0:T(2,128)(2,1)}), bf16[128,2,1024]{2,1,0:T(2,128)(2,1)S(1)}, u32[]{:S(2)}, u32[]{:S(2)}) async-start(bf16[128,2,1024]{2,1,0:T(2,128)(2,1)} %reshape.200), calls=%async_computation.2 | async-start | bytes 1048576 | tf_op jit(solution)/shard_map/all_to_all | solution.py:116
  282.9 19.1 %reduce-scatter.5.cloned.1.call-done = bf16[1,128,2048]{2,1,0:T(8,128)(2,1)} async-done(((bf16[4,128,2048]{2,1,0:T(8,128)(2,1)}), bf16[1,128,2048]{2,1,0:T(8,128)(2,1)}) %reduce-scatter.5.cloned.1.call-update) | async-done | bytes 524304 | tf_op jit(solution)/shard_map/reduce_scatter | solution.py:113
  302.1 2.0 reduce.3
  304.1 1.2 reshape.202
  305.3 10.5 %all-to-all-done.1 = bf16[128,2,1024]{2,1,0:T(2,128)(2,1)S(1)} async-done(((bf16[128,2,1024]{2,1,0:T(2,128)(2,1)}), bf16[128,2,1024]{2,1,0:T(2,128)(2,1)S(1)}, u32[]{:S(2)}, u32[]{:S(2)}) %all-to-all-start.1) | async-done | bytes 524320 | tf_op jit(solution)/shard_map/all_to_all | solution.py:116
  315.9 7.1 %all-to-all-start.3 = ((bf16[128,2,1024]{2,1,0:T(2,128)(2,1)}), bf16[128,2,1024]{2,1,0:T(2,128)(2,1)S(1)}, u32[]{:S(2)}, u32[]{:S(2)}) async-start(bf16[128,2,1024]{2,1,0:T(2,128)(2,1)} %reshape.202), calls=%async_computation.5 | async-start | bytes 1048576 | tf_op jit(solution)/shard_map/all_to_all | solution.py:116
  323.0 2.3 fusion.18
  325.4 3.2 fusion.5
  328.6 0.6 fusion.19
  329.3 1.5 fusion.6
  330.8 0.6 fusion.8
  331.4 0.4 copy-done.24
  331.9 1.5 fusion.4
  333.4 0.4 reshape.201
  333.8 0.4 fusion.38
  334.2 22.0 %all-to-all-done.3 = bf16[128,2,1024]{2,1,0:T(2,128)(2,1)S(1)} async-done(((bf16[128,2,1024]{2,1,0:T(2,128)(2,1)}), bf16[128,2,1024]{2,1,0:T(2,128)(2,1)S(1)}, u32[]{:S(2)}, u32[]{:S(2)}) %all-to-all-start.3) | async-done | bytes 524320 | tf_op jit(solution)/shard_map/all_to_all | solution.py:116
  356.2 0.4 reshape.203
  356.6 1.0 fusion.7
  (109 shorter events, 3.5 us)
Async XLA Ops:
  7.2 4.6 %copy-start = (bf16[24,2048]{1,0:T(8,128)(2,1)S(1)}, bf16[24,2048]{1,0:T(8,128)(2,1)}, u32[]{:S(2)}) copy-start(bf16[24,2048]{1,0:T(8,128)(2,1)} %param.11) | copy-start | bytes 294916
  7.2 0.9 copy-start.2
  7.2 212.0 %all-gather.3.cloned.1.call-start = ((), (), s32[]{:S(2)}) async-start(), calls=%async_computation.6 | async-start | bytes 5242880 | tf_op jit(solution)/shard_map/all_gather | solution.py:107
  8.1 2.9 copy-start.22
  9.7 2.6 copy-start.18
  10.8 1.5 copy-start.12
  92.3 62.8 %all-to-all-start.2 = ((bf16[2,128,2048]{2,0,1:T(2,128)(2,1)}), bf16[2,128,2048]{2,0,1:T(2,128)(2,1)S(1)}, u32[]{:S(2)}, u32[]{:S(2)}) async-start(bf16[2,128,2048]{2,0,1:T(2,128)(2,1)} %copy.76), calls=%async_computation.3 | async-start | bytes 2097152 | tf_op jit(solution)/shard_map/all_to_all | solution.py:106
  100.7 129.2 %all-gather.5.cloned.1.call-start = ((), (), s32[]{:S(2)}) async-start(), calls=%async_computation.8 | async-start | bytes 5242880 | tf_op jit(solution)/shard_map/all_gather | solution.py:107
  103.3 58.9 %copy-start.19 = (f32[1,3,16]{2,0,1:T(1,128)S(1)}, f32[1,3,16]{2,0,1:T(1,128)}, u32[]{:S(2)}) copy-start(f32[1,3,16]{2,0,1:T(1,128)} %param.21) | copy-start | bytes 580
  103.3 58.9 %copy-start.20 = (f32[1,3,16]{2,0,1:T(1,128)S(1)}, f32[1,3,16]{2,0,1:T(1,128)}, u32[]{:S(2)}) copy-start(f32[1,3,16]{2,0,1:T(1,128)} %param.20) | copy-start | bytes 580
  103.3 58.9 %copy-start.21 = (f32[1,3,16]{2,0,1:T(1,128)S(1)}, f32[1,3,16]{2,0,1:T(1,128)}, u32[]{:S(2)}) copy-start(f32[1,3,16]{2,0,1:T(1,128)} %param.19) | copy-start | bytes 580
  156.5 105.7 %reduce-scatter.3.cloned.1.call-start = ((), (), s32[]{:S(2)}) async-start(), calls=%async_computation.7 | async-start | bytes 2621440 | tf_op jit(solution)/shard_map/reduce_scatter | solution.py:113
  157.7 54.8 %copy-start.7 = (bf16[3,192,2048]{2,1,0:T(8,128)(2,1)}, bf16[3,192,2048]{2,1,0:T(8,128)(2,1)S(1)}, u32[]{:S(2)}) copy-start(bf16[3,192,2048]{2,1,0:T(8,128)(2,1)S(1)} %constant_dynamic-update-slice_fusion) | copy-start | bytes 7077892
  157.7 54.8 %collective-permute-start = (bf16[3,192,2048]{2,1,0:T(8,128)(2,1)S(1)}, bf16[3,192,2048]{2,1,0:T(8,128)(2,1)}, u32[]{:S(2)}, u32[]{:S(2)}) collective-permute-start(bf16[3,192,2048]{2,1,0:T(8,128)(2,1)S(1)} %constant_dynamic-update-slice_fusion), channel_id=1, source_target_pairs={{0,64},{64,0},{1,65},{65,1},{2,66},{66,2},{3,67},{67,3},{4,68},{68... | collective-permute-start | bytes 7077896 | tf_op jit(solution)/shard_map/ppermute | solution.py:14
  162.2 50.2 %collective-permute-start.1 = (f32[3,3,16]{2,0,1:T(4,128)S(1)}, f32[3,3,16]{2,0,1:T(4,128)S(1)}, u32[]{:S(2)}, u32[]{:S(2)}) collective-permute-start(f32[3,3,16]{2,0,1:T(4,128)S(1)} %pad_maximum_fusion.2), channel_id=1, source_target_pairs={{0,64},{64,0},{1,65},{65,1},{2,66},{66,2},{3,67},{67,3},{4,68},{68... | collective-permute-start | bytes 1736 | tf_op jit(solution)/shard_map/ppermute | solution.py:14
  219.2 2.8 copy-start.10
  221.8 2.3 copy-start.27
  222.1 2.1 copy-start.14
  224.1 1.0 copy-start.29
  225.1 2.1 copy-start.16
  225.6 1.1 copy-start.3
  227.2 2.4 copy-start.5
  229.6 72.5 %reduce-scatter.5.cloned.1.call-start = ((), (), s32[]{:S(2)}) async-start(), calls=%async_computation.9 | async-start | bytes 2621440 | tf_op jit(solution)/shard_map/reduce_scatter | solution.py:113
  229.9 3.1 copy-start.8
  233.0 0.9 copy-start.23
  233.0 1.3 copy-start.15
  234.2 0.9 copy-start.25
  234.3 1.5 copy-start.4
  235.8 1.4 copy-start.6
  239.6 43.1 %copy-start.13 = (bf16[24,256]{0,1:T(8,128)(2,1)S(1)}, bf16[24,256]{0,1:T(8,128)(2,1)}, u32[]{:S(2)}) copy-start(bf16[24,256]{0,1:T(8,128)(2,1)} %copy-done.12) | copy-start | bytes 36868
  265.8 57.2 %copy-start.17 = (bf16[512,192]{0,1:T(8,128)(2,1)S(1)}, bf16[512,192]{0,1:T(8,128)(2,1)}, u32[]{:S(2)}) copy-start(bf16[512,192]{0,1:T(8,128)(2,1)} %copy-done.16) | copy-start | bytes 589828
  265.8 50.0 %all-to-all-start.1 = ((bf16[128,2,1024]{2,1,0:T(2,128)(2,1)}), bf16[128,2,1024]{2,1,0:T(2,128)(2,1)S(1)}, u32[]{:S(2)}, u32[]{:S(2)}) async-start(bf16[128,2,1024]{2,1,0:T(2,128)(2,1)} %reshape.200), calls=%async_computation.2 | async-start | bytes 1048576 | tf_op jit(solution)/shard_map/all_to_all | solution.py:116
  315.9 40.3 %all-to-all-start.3 = ((bf16[128,2,1024]{2,1,0:T(2,128)(2,1)}), bf16[128,2,1024]{2,1,0:T(2,128)(2,1)S(1)}, u32[]{:S(2)}, u32[]{:S(2)}) async-start(bf16[128,2,1024]{2,1,0:T(2,128)(2,1)} %reshape.202), calls=%async_computation.5 | async-start | bytes 1048576 | tf_op jit(solution)/shard_map/all_to_all | solution.py:116
  323.0 5.6 %copy-start.11 = (bf16[2,512,2048]{2,1,0:T(8,128)(2,1)S(1)}, bf16[2,512,2048]{2,1,0:T(8,128)(2,1)}, u32[]{:S(2)}) copy-start(bf16[2,512,2048]{2,1,0:T(8,128)(2,1)} %all-gather.3.cloned.1.call-done) | copy-start | bytes 12582916
  325.4 3.9 %copy-start.9 = (bf16[2,512,2048]{2,1,0:T(8,128)(2,1)S(1)}, bf16[2,512,2048]{2,1,0:T(8,128)(2,1)}, u32[]{:S(2)}) copy-start(bf16[2,512,2048]{2,1,0:T(8,128)(2,1)} %all-gather.5.cloned.1.call-done) | copy-start | bytes 12582916
  329.2 1.5 copy-start.28
  329.2 1.5 copy-start.30
  330.8 1.0 copy-start.24
  330.8 1.1 copy-start.26
  331.9 25.8 %copy-start.1 = (bf16[24,2048]{1,0:T(8,128)(2,1)S(1)}, bf16[24,2048]{1,0:T(8,128)(2,1)}, u32[]{:S(2)}) copy-start(bf16[24,2048]{1,0:T(8,128)(2,1)} %param.11) | copy-start | bytes 294916
Sparse Core Ops, SparseCore 0:
  90.2 49.0 all-gather.2
  156.6 49.0 all-gather.4
  229.7 32.3 reduce-scatter.2
  264.8 37.1 reduce-scatter.4

commit v3 on v2

v3 whole, which is shorter than its diff:
```python
import jax
import jax.numpy as jnp
import numpy as np
from jax import lax
from jax.sharding import Mesh
from jax.sharding import PartitionSpec as P

EXPERT_AXES = ("ex", "ez", "ec")
RING_AXES = ("ez", "ec")


def swapped(block, axis, count, stride):
    route = []
    for low in range(count):
        high = low | 1 << stride
        if high != low and high < count:
            route += [(low, high), (high, low)]
    return lax.ppermute(block, axis, route)


def dequantize(values, scales):
    row_block = values.shape[0] // scales.shape[0]
    col_block = values.shape[1] // scales.shape[1]
    spread = jnp.repeat(jnp.repeat(scales, row_block, axis=0), col_block, axis=1)
    return (values.astype(jnp.float32) * spread).astype(jnp.bfloat16)


def slot_position(route_lists, experts, capacity):
    numbers = jnp.arange(experts, dtype=jnp.int32)
    flattened = route_lists.reshape(-1)
    marked = (flattened[:, None] == numbers).astype(jnp.int32)
    slot_index = jnp.sum((jnp.cumsum(marked, axis=0) - 1) * marked, axis=-1)
    return (flattened * capacity + slot_index).reshape(route_lists.shape)


def contract(left, right, left_dim, right_dim):
    return lax.dot_general(
        left, right, (((left_dim,), (right_dim,)), ((), ())), preferred_element_type=jnp.float32
    )


def expert_work(token_rows, cot_rows, w_gate, w_up, w_down):
    pre_gate = contract(token_rows, w_gate, 1, 1)
    pre_up = contract(token_rows, w_up, 1, 1)
    sigmoid_gate = jax.nn.sigmoid(pre_gate)
    activated = pre_gate * sigmoid_gate
    hidden = (activated * pre_up).astype(jnp.bfloat16)
    grad_hidden = contract(cot_rows, w_down, 1, 1)
    grad_gate = (
        grad_hidden * pre_up * sigmoid_gate * (1.0 + pre_gate * (1.0 - sigmoid_gate))
    ).astype(jnp.bfloat16)
    grad_up = (grad_hidden * activated).astype(jnp.bfloat16)
    gate_grad = contract(grad_gate, token_rows, 0, 0)
    up_grad = contract(grad_up, token_rows, 0, 0)
    down_grad = contract(hidden, cot_rows, 0, 0)
    row_grads = (
        jnp.dot(grad_gate, w_gate, preferred_element_type=jnp.float32)
        + jnp.dot(grad_up, w_up, preferred_element_type=jnp.float32)
    ).astype(jnp.bfloat16)
    return (row_grads, gate_grad, up_grad, down_grad)


def on_device(
    tokens,
    cotangent,
    routes,
    gates,
    plan,
    gate_values,
    up_values,
    down_values,
    gate_scales,
    up_scales,
    down_scales,
):
    tok_count, features = tokens.shape
    n_x, n_z, n_c = (lax.axis_size(a) for a in EXPERT_AXES)
    ring = n_z * n_c
    experts = n_x * ring
    replicas = lax.axis_size("dp")
    capacity = 2
    half_bit = experts.bit_length() - 2
    ring_index = lax.axis_index("ez") * n_c + lax.axis_index("ec")
    expert_index = lax.axis_index("ex") * ring + ring_index
    numbers = jnp.arange(experts, dtype=jnp.int32)
    is_moved = jnp.sum(jnp.where(numbers == expert_index, plan, 0)) != expert_index
    own = (
        jnp.concatenate([gate_values, up_values, down_values], axis=0),
        jnp.concatenate([gate_scales, up_scales, down_scales], axis=0),
    )
    partner = swapped(own, EXPERT_AXES, experts, half_bit)
    values, scales = (jnp.where(is_moved, b, a) for a, b in zip(own, partner))
    w_gate, w_up, w_down = (dequantize(values[i], scales[i]) for i in range(3))

    destination = jnp.take(plan, routes, axis=0)
    position = slot_position(destination, experts, capacity)
    slots = jnp.arange(experts * capacity, dtype=jnp.int32)
    dispatch = jnp.any(position[..., None] == slots, axis=1).astype(jnp.bfloat16).reshape(
        tok_count, experts, capacity
    )
    ring_rows = lax.all_gather(
        jnp.concatenate([tokens, cotangent], axis=1), RING_AXES, axis=0, tiled=True
    )
    ring_position = lax.all_gather(position, RING_AXES, axis=0, tiled=True)
    ring_gates = lax.all_gather(gates, RING_AXES, axis=0, tiled=True)
    target = (
        (jnp.arange(n_x, dtype=jnp.int32)[:, None] * ring + ring_index) * capacity
        + jnp.arange(capacity, dtype=jnp.int32)
    )
    match = ring_position[:, :, None, None] == target
    picked = jnp.any(match, axis=1).astype(jnp.bfloat16).reshape(ring, tok_count, n_x, capacity)
    picked_gate = jnp.sum(
        jnp.where(match, ring_gates[:, :, None, None], jnp.zeros((), ring_gates.dtype)), axis=1
    ).reshape(ring, tok_count, n_x, capacity)
    ring_rows = ring_rows.reshape(ring, tok_count, 2 * features)
    relay_tok = jnp.einsum(
        "srxc,srd->cxsd", picked, ring_rows[:, :, :features], preferred_element_type=jnp.float32
    ).astype(jnp.bfloat16)
    relay_cot = jnp.einsum(
        "srxc,srd->cxsd", picked_gate, ring_rows[:, :, features:], preferred_element_type=jnp.float32
    ).astype(jnp.bfloat16)

    token_sum = jnp.zeros((tok_count, features), jnp.float32)
    sums = None
    for chunk in range(capacity):
        both = jnp.stack([relay_tok[chunk], relay_cot[chunk]], axis=0)
        arrived = lax.all_to_all(both, "ex", split_axis=1, concat_axis=1, tiled=True)
        arrived = arrived.reshape(2, experts, features)
        gathered = lax.all_gather(arrived, "dp", axis=1, tiled=True)
        row_grads, gate_grad, up_grad, down_grad = expert_work(
            gathered[0], gathered[1], w_gate, w_up, w_down
        )
        part = (gate_grad, up_grad, down_grad)
        sums = part if sums is None else tuple(a + b for a, b in zip(sums, part))
        summed_rows = lax.psum_scatter(
            row_grads.reshape(replicas, experts, features), "dp", scatter_dimension=0, tiled=True
        )
        returned = lax.all_to_all(summed_rows[0], EXPERT_AXES, split_axis=0, concat_axis=0, tiled=True)
        token_sum = token_sum + jnp.einsum(
            "re,ed->rd", dispatch[:, :, chunk], returned, preferred_element_type=jnp.float32
        )
    token_grads = token_sum.astype(jnp.bfloat16)
    gate_grad, up_grad, down_grad = (x.astype(jnp.bfloat16) for x in sums)
    return (token_grads, gate_grad[None], up_grad[None], down_grad[None])


def split_mesh(mesh):
    devices = mesh.devices
    flat = devices.reshape(-1)
    sizes = []
    for pick in (lambda d: d.coords[0], lambda d: d.coords[2], lambda d: d.core_on_chip):
        sizes.append(len({pick(d) for d in devices[0]}))
    assert int(np.prod(sizes)) == devices.shape[1]
    return Mesh(flat.reshape((devices.shape[0], *sizes)), ("dp", *EXPERT_AXES))


def solution(mesh):
    fine = split_mesh(mesh)
    rows = P(("dp", *EXPERT_AXES), None)
    weights = P(EXPERT_AXES, "dp", None)
    return jax.shard_map(
        on_device,
        mesh=fine,
        in_specs=(rows, rows, rows, rows, P(), weights, weights, weights, weights, weights, weights),
        out_specs=(rows, weights, weights, weights),
        check_vma=False,
    )
```

time: 365 us -> 374 us (1.025)
  blocking collectives: 74.6 us -> 83.7 us
  starting transfers between devices: 39.7 us -> 34.7 us
  matrix products: 28.9 us -> 33.1 us
    all_gather x0 -> x2, blocking collectives: none -> 65.2 us  [the longest x1 37.9 us: on_device(): ring_position = lax.all_gather(position, RING_AXES, axis=0, tiled=True)]
    all_to_all x1, blocking collectives: 74.6 us -> 18.4 us  [on_device(): lax.all_to_all(both, 'ex', split_axis=1, concat_axis=1, tiled=True)]
    all_to_all x3, waiting for transfers between devices: 84.3 us -> 43.7 us  [the longest x2 32.4 us: on_device(): lax.all_to_all(summed_rows[0], EXPERT_AXES, split_axis=0, concat_axis=0,...]
    all_gather x2, waiting for transfers between devices: 0.02 us -> 15.6 us  [on_device(): gathered = lax.all_gather(arrived, 'dp', axis=1, tiled=True)]
    all_gather x0 -> x1, waiting for transfers between devices: none -> 14.4 us  [on_device(): lax.all_gather(jnp.concatenate([tokens, cotangent], axis=1), RING_AXES, a...]
    reduce_scatter x2, waiting for transfers between devices: 41.7 us -> 49.8 us  [on_device(): lax.psum_scatter(row_grads.reshape(replicas, experts, features), 'dp', sc...]
    all_to_all x3, starting transfers between devices: 32.3 us -> 27.4 us  [the longest x2 23.8 us: on_device(): lax.all_to_all(summed_rows[0], EXPERT_AXES, split_axis=0, concat_axis=0,...]
    dot_general x2, matrix products: 0.93 us -> 5.17 us  [the longest x1 2.59 us: on_device(): jnp.einsum('srxc,srd->cxsd', picked_gate, ring_rows[:, :, features:], pre...]
  transfers between devices with their start and end apart: 9 -> 10, of which waited for: 6 -> 8; matrix products, arithmetic and copies ran while one was open for 14% -> 15% of each run, Pallas kernels for 0% -> 0%
where the time goes in v3:
time: 374 us; the launch traced here: 373 us
  waiting for transfers between devices  169 us (45%)
  blocking collectives  83.7 us (22%)
  starting transfers between devices  34.7 us (9%)
  matrix products  33.1 us (9%)
  local copies, waits for them, and re-layouts  22.7 us (6%)
  between operations  15.1 us (4%)
  other arithmetic  14.5 us (4%)
    reduce_scatter x2, waiting for transfers between devices, on_device(): lax.psum_scatter(row_grads.reshape(replicas, experts, features), 'dp', sc...  49.8 us
    ppermute x2, waiting for transfers between devices, swapped(): return lax.ppermute(block, axis, route)  45.9 us
    all_gather x1, blocking collectives, on_device(): ring_position = lax.all_gather(position, RING_AXES, axis=0, tiled=True)  37.9 us
    all_to_all x2, waiting for transfers between devices, on_device(): lax.all_to_all(summed_rows[0], EXPERT_AXES, split_axis=0, concat_axis=0,...  32.4 us
    all_gather x1, blocking collectives, on_device(): ring_gates = lax.all_gather(gates, RING_AXES, axis=0, tiled=True)  27.3 us
    all_to_all x2, starting transfers between devices, on_device(): lax.all_to_all(summed_rows[0], EXPERT_AXES, split_axis=0, concat_axis=0,...  23.8 us
    dot_general x12, matrix products, contract(): lax.dot_general(left, right, (((left_dim,), (right_dim,)), ((), ())), pre...  19.9 us
    all_to_all x1, blocking collectives, on_device(): lax.all_to_all(both, 'ex', split_axis=1, concat_axis=1, tiled=True)  18.4 us
  transfers between devices with their start and end apart: 10, of which 8 were waited for; matrix products, arithmetic and copies ran while one was open for 15% of the time, Pallas kernels for 0%

profile of v3, /device:TPU:1, one launch (start us, length us, event | category | flops | bytes accessed | tf_op | source)
XLA Modules:
  0.0 373.1 jit_solution(4731478354306599622)
XLA Ops:
  7.2 1.6 pad_maximum_fusion.2
  8.9 0.8 copy.69
  9.8 1.6 gather_fusion
  12.3 37.9 %all-gather = s32[32,24,8]{1,2,0:T(8,128)S(1)} all-gather(s32[1,24,8]{1,2,0:T(8,128)S(1)} %copy.76), channel_id=1, replica_groups=mesh['dp'=4,'ex'=4,'ez'=16,'ec'=2] {'ez','ec'}, dimensions={0}, use_global_device_ids=true | all-gather | bytes 25344 | tf_op jit(solution)/shard_map/all_gather | solution.py:104
  50.4 27.3 %all-gather.1 = bf16[32,24,8]{1,2,0:T(8,128)(2,1)S(1)} all-gather(bf16[1,24,8]{1,2,0:T(8,128)(2,1)S(1)} %bitcast.207), channel_id=1, replica_groups=mesh['dp'=4,'ex'=4,'ez'=16,'ec'=2] {'ez','ec'}, dimensions={0}, use_global_device_ids=true | all-gather | bytes 12672 | tf_op jit(solution)/shard_map/all_gather | solution.py:105
  78.5 14.4 %all-gather.6.cloned.1.call-done = bf16[768,4096]{1,0:T(8,128)(2,1)} async-done(((bf16[24,4096]{1,0:T(8,128)(2,1)}), bf16[768,4096]{1,0:T(8,128)(2,1)}) %all-gather.6.cloned.1.call-update) | async-done | bytes 6291472 | tf_op jit(solution)/shard_map/all_gather | solution.py:101
  92.8 2.6 fusion.7
  95.4 2.6 fusion.8
  98.0 0.9 fusion.69
  99.0 0.7 pad_maximum_fusion
  99.7 1.1 copy.82
  100.8 18.4 %all_to_all.34 = bf16[2,4,32,2048]{3,0,2,1:T(2,128)(2,1)S(1)} all-to-all(bf16[2,4,32,2048]{3,0,2,1:T(2,128)(2,1)S(1)} %copy.82), channel_id=1, replica_groups=mesh['dp'=4,'ex'=4,'ez'=16,'ec'=2] {'ex'}, dimensions={1} | all-to-all | bytes 2097152 | tf_op jit(solution)/shard_map/all_to_all | solution.py:127
  119.2 1.4 copy.83
  120.6 0.7 pad_maximum_fusion.1
  121.3 2.1 copy.86
  123.3 3.5 all-to-all-start.2
  126.9 1.2 constant_dynamic-update-slice_fusion.2
  128.1 1.2 constant_dynamic-update-slice_fusion.1
  129.3 11.3 %all-to-all-done.2 = bf16[2,4,32,2048]{3,0,2,1:T(2,128)(2,1)S(1)} async-done(((bf16[2,4,32,2048]{3,0,2,1:T(2,128)(2,1)}), bf16[2,4,32,2048]{3,0,2,1:T(2,128)(2,1)S(1)}, u32[]{:S(2)}, u32[]{:S(2)}) %all-to-all-start.2) | async-done | bytes 1048608 | tf_op jit(solution)/shard_map/all_to_all | solution.py:127
  140.6 1.4 copy.87
  142.0 1.2 constant_dynamic-update-slice_fusion
  143.2 2.2 collective-permute-start
  145.5 4.7 %collective-permute-start.1 = (f32[3,3,16]{2,0,1:T(4,128)S(1)}, f32[3,3,16]{2,0,1:T(4,128)S(1)}, u32[]{:S(2)}, u32[]{:S(2)}) collective-permute-start(f32[3,3,16]{2,0,1:T(4,128)S(1)} %pad_maximum_fusion.3), channel_id=1, source_target_pairs={{0,64},{64,0},{1,65},{65,1},{2,66},{66,2},{3,67},{67,3},{4,68},{68... | collective-permute-start | bytes 1736 | tf_op jit(solution)/shard_map/ppermute | solution.py:18
  150.3 0.6 fusion.60
  151.6 45.9 %collective-permute-done.1 = f32[3,3,16]{2,0,1:T(4,128)S(1)} collective-permute-done((f32[3,3,16]{2,0,1:T(4,128)S(1)}, f32[3,3,16]{2,0,1:T(4,128)S(1)}, u32[]{:S(2)}, u32[]{:S(2)}) %collective-permute-start.1) | collective-permute-done | bytes 608 | tf_op jit(solution)/shard_map/ppermute | solution.py:18
  197.5 1.9 broadcast_select_fusion
  199.4 0.6 convert_bitcast_fusion.3
  200.9 0.5 fusion.21
  201.4 1.4 fusion.20
  202.8 1.4 fusion.22
  204.2 2.6 fusion.26
  207.1 2.0 fusion.25
  209.2 0.9 multiply_convert_fusion.4
  210.1 0.5 broadcast_in_dim.68
  210.6 0.9 fusion.65
  211.7 0.5 broadcast_in_dim.66
  212.2 2.4 add_convert_fusion.1
  214.9 15.6 %all-gather.10.cloned.1.call-done = bf16[2,512,2048]{2,1,0:T(8,128)(2,1)} async-done(((bf16[2,128,2048]{2,1,0:T(8,128)(2,1)}), bf16[2,512,2048]{2,1,0:T(8,128)(2,1)}) %all-gather.10.cloned.1.call-update) | async-done | bytes 4194320 | tf_op jit(solution)/shard_map/all_gather | solution.py:129
  230.5 2.8 fusion.27
  233.5 0.9 fusion.28
  234.8 0.9 multiply_convert_fusion.2
  235.8 0.6 copy-done.2
  236.4 0.9 fusion.63
  237.3 0.5 copy-done.4
  237.8 2.4 add_convert_fusion
  240.2 30.9 %reduce-scatter.3.cloned.1.call-done = bf16[1,128,2048]{2,1,0:T(8,128)(2,1)} async-done(((bf16[4,128,2048]{2,1,0:T(8,128)(2,1)}), bf16[1,128,2048]{2,1,0:T(8,128)(2,1)}) %reduce-scatter.3.cloned.1.call-update) | async-done | bytes 524304 | tf_op jit(solution)/shard_map/reduce_scatter | solution.py:135
  271.1 0.5 broadcast.105
  271.6 2.0 reduce.1
  273.6 1.2 reshape.239
  274.8 16.7 %all-to-all-start.1 = ((bf16[128,2,1024]{2,1,0:T(2,128)(2,1)}), bf16[128,2,1024]{2,1,0:T(2,128)(2,1)S(1)}, u32[]{:S(2)}, u32[]{:S(2)}) async-start(bf16[128,2,1024]{2,1,0:T(2,128)(2,1)} %reshape.239), calls=%async_computation.2 | async-start | bytes 1048576 | tf_op jit(solution)/shard_map/all_to_all | solution.py:138
  292.2 18.8 %reduce-scatter.5.cloned.1.call-done = bf16[1,128,2048]{2,1,0:T(8,128)(2,1)} async-done(((bf16[4,128,2048]{2,1,0:T(8,128)(2,1)}), bf16[1,128,2048]{2,1,0:T(8,128)(2,1)}) %reduce-scatter.5.cloned.1.call-update) | async-done | bytes 524304 | tf_op jit(solution)/shard_map/reduce_scatter | solution.py:135
  311.0 2.0 reduce.2
  313.0 1.2 reshape.241
  314.3 10.4 %all-to-all-done.1 = bf16[128,2,1024]{2,1,0:T(2,128)(2,1)S(1)} async-done(((bf16[128,2,1024]{2,1,0:T(2,128)(2,1)}), bf16[128,2,1024]{2,1,0:T(2,128)(2,1)S(1)}, u32[]{:S(2)}, u32[]{:S(2)}) %all-to-all-start.1) | async-done | bytes 524320 | tf_op jit(solution)/shard_map/all_to_all | solution.py:138
  324.7 7.1 %all-to-all-start.3 = ((bf16[128,2,1024]{2,1,0:T(2,128)(2,1)}), bf16[128,2,1024]{2,1,0:T(2,128)(2,1)S(1)}, u32[]{:S(2)}, u32[]{:S(2)}) async-start(bf16[128,2,1024]{2,1,0:T(2,128)(2,1)} %reshape.241), calls=%async_computation.5 | async-start | bytes 1048576 | tf_op jit(solution)/shard_map/all_to_all | solution.py:138
  331.9 2.3 fusion.23
  334.2 3.2 fusion.10
  337.5 0.6 fusion.24
  338.1 1.5 fusion.11
  339.6 0.6 fusion.13
  340.7 1.5 fusion.9
  343.1 22.0 %all-to-all-done.3 = bf16[128,2,1024]{2,1,0:T(2,128)(2,1)S(1)} async-done(((bf16[128,2,1024]{2,1,0:T(2,128)(2,1)}), bf16[128,2,1024]{2,1,0:T(2,128)(2,1)S(1)}, u32[]{:S(2)}, u32[]{:S(2)}) %all-to-all-start.3) | async-done | bytes 524320 | tf_op jit(solution)/shard_map/all_to_all | solution.py:138
  365.1 0.4 reshape.242
  365.5 1.0 fusion.12
  (110 shorter events, 6.6 us)
Async XLA Ops:
  7.2 2.6 copy-start
  7.2 85.7 %all-gather.6.cloned.1.call-start = ((), (), s32[]{:S(2)}) async-start(), calls=%async_computation.6 | async-start | bytes 6488064 | tf_op jit(solution)/shard_map/all_gather | solution.py:101
  8.9 195.3 %all-gather.8.cloned.1.call-start = ((), (), s32[]{:S(2)}) async-start(), calls=%async_computation.7 | async-start | bytes 5242880 | tf_op jit(solution)/shard_map/all_gather | solution.py:129
  9.8 40.6 %copy-start.17 = (bf16[24,8]{0,1:T(8,128)(2,1)S(1)}, bf16[24,8]{0,1:T(8,128)(2,1)}, u32[]{:S(2)}) copy-start(bf16[24,8]{0,1:T(8,128)(2,1)} %param.14) | copy-start | bytes 1156
  123.3 17.3 %all-to-all-start.2 = ((bf16[2,4,32,2048]{3,0,2,1:T(2,128)(2,1)}), bf16[2,4,32,2048]{3,0,2,1:T(2,128)(2,1)S(1)}, u32[]{:S(2)}, u32[]{:S(2)}) async-start(bf16[2,4,32,2048]{3,0,2,1:T(2,128)(2,1)} %copy.86), calls=%async_computation.3 | async-start | bytes 2097152 | tf_op jit(solution)/shard_map/all_to_all | solution.py:127
  126.9 103.6 %all-gather.10.cloned.1.call-start = ((), (), s32[]{:S(2)}) async-start(), calls=%async_computation.9 | async-start | bytes 5242880 | tf_op jit(solution)/shard_map/all_gather | solution.py:129
  129.3 16.2 %copy-start.14 = (f32[1,3,16]{2,0,1:T(1,128)S(1)}, f32[1,3,16]{2,0,1:T(1,128)}, u32[]{:S(2)}) copy-start(f32[1,3,16]{2,0,1:T(1,128)} %param.21) | copy-start | bytes 580
  129.3 16.2 %copy-start.15 = (f32[1,3,16]{2,0,1:T(1,128)S(1)}, f32[1,3,16]{2,0,1:T(1,128)}, u32[]{:S(2)}) copy-start(f32[1,3,16]{2,0,1:T(1,128)} %param.20) | copy-start | bytes 580
  129.3 16.2 %copy-start.16 = (f32[1,3,16]{2,0,1:T(1,128)S(1)}, f32[1,3,16]{2,0,1:T(1,128)}, u32[]{:S(2)}) copy-start(f32[1,3,16]{2,0,1:T(1,128)} %param.19) | copy-start | bytes 580
  142.0 129.1 %reduce-scatter.3.cloned.1.call-start = ((), (), s32[]{:S(2)}) async-start(), calls=%async_computation.8 | async-start | bytes 2621440 | tf_op jit(solution)/shard_map/reduce_scatter | solution.py:135
  143.2 54.2 %copy-start.5 = (bf16[3,192,2048]{2,1,0:T(8,128)(2,1)}, bf16[3,192,2048]{2,1,0:T(8,128)(2,1)S(1)}, u32[]{:S(2)}) copy-start(bf16[3,192,2048]{2,1,0:T(8,128)(2,1)S(1)} %constant_dynamic-update-slice_fusion) | copy-start | bytes 7077892
  143.2 54.2 %collective-permute-start = (bf16[3,192,2048]{2,1,0:T(8,128)(2,1)S(1)}, bf16[3,192,2048]{2,1,0:T(8,128)(2,1)}, u32[]{:S(2)}, u32[]{:S(2)}) collective-permute-start(bf16[3,192,2048]{2,1,0:T(8,128)(2,1)S(1)} %constant_dynamic-update-slice_fusion), channel_id=1, source_target_pairs={{0,64},{64,0},{1,65},{65,1},{2,66},{66,2},{3,67},{67,3},{4,68},{68... | collective-permute-start | bytes 7077896 | tf_op jit(solution)/shard_map/ppermute | solution.py:18
  145.5 51.9 %collective-permute-start.1 = (f32[3,3,16]{2,0,1:T(4,128)S(1)}, f32[3,3,16]{2,0,1:T(4,128)S(1)}, u32[]{:S(2)}, u32[]{:S(2)}) collective-permute-start(f32[3,3,16]{2,0,1:T(4,128)S(1)} %pad_maximum_fusion.3), channel_id=1, source_target_pairs={{0,64},{64,0},{1,65},{65,1},{2,66},{66,2},{3,67},{67,3},{4,68},{68... | collective-permute-start | bytes 1736 | tf_op jit(solution)/shard_map/ppermute | solution.py:18
  204.2 2.9 copy-start.8
  206.8 2.4 copy-start.22
  207.1 2.1 copy-start.10
  209.1 1.0 copy-start.24
  210.1 2.1 copy-start.12
  210.6 1.1 copy-start.1
  212.2 2.4 copy-start.3
  214.6 96.4 %reduce-scatter.5.cloned.1.call-start = ((), (), s32[]{:S(2)}) async-start(), calls=%async_computation.10 | async-start | bytes 2621440 | tf_op jit(solution)/shard_map/reduce_scatter | solution.py:135
  230.5 3.1 copy-start.6
  233.5 0.9 copy-start.18
  233.5 1.3 copy-start.11
  234.8 0.9 copy-start.20
  234.8 1.5 copy-start.2
  236.4 1.4 copy-start.4
  274.8 49.9 %all-to-all-start.1 = ((bf16[128,2,1024]{2,1,0:T(2,128)(2,1)}), bf16[128,2,1024]{2,1,0:T(2,128)(2,1)S(1)}, u32[]{:S(2)}, u32[]{:S(2)}) async-start(bf16[128,2,1024]{2,1,0:T(2,128)(2,1)} %reshape.239), calls=%async_computation.2 | async-start | bytes 1048576 | tf_op jit(solution)/shard_map/all_to_all | solution.py:138
  291.5 40.4 %copy-start.13 = (bf16[512,192]{0,1:T(8,128)(2,1)S(1)}, bf16[512,192]{0,1:T(8,128)(2,1)}, u32[]{:S(2)}) copy-start(bf16[512,192]{0,1:T(8,128)(2,1)} %copy-done.12) | copy-start | bytes 589828
  324.7 40.3 %all-to-all-start.3 = ((bf16[128,2,1024]{2,1,0:T(2,128)(2,1)}), bf16[128,2,1024]{2,1,0:T(2,128)(2,1)S(1)}, u32[]{:S(2)}, u32[]{:S(2)}) async-start(bf16[128,2,1024]{2,1,0:T(2,128)(2,1)} %reshape.241), calls=%async_computation.5 | async-start | bytes 1048576 | tf_op jit(solution)/shard_map/all_to_all | solution.py:138
  331.9 5.6 %copy-start.9 = (bf16[2,512,2048]{2,1,0:T(8,128)(2,1)S(1)}, bf16[2,512,2048]{2,1,0:T(8,128)(2,1)}, u32[]{:S(2)}) copy-start(bf16[2,512,2048]{2,1,0:T(8,128)(2,1)} %all-gather.8.cloned.1.call-done) | copy-start | bytes 12582916
  334.2 3.9 %copy-start.7 = (bf16[2,512,2048]{2,1,0:T(8,128)(2,1)S(1)}, bf16[2,512,2048]{2,1,0:T(8,128)(2,1)}, u32[]{:S(2)}) copy-start(bf16[2,512,2048]{2,1,0:T(8,128)(2,1)} %all-gather.10.cloned.1.call-done) | copy-start | bytes 12582916
  338.1 1.5 copy-start.23
  338.1 1.5 copy-start.25
  339.6 1.0 copy-start.19
  339.6 1.1 copy-start.21
Sparse Core Ops, SparseCore 0:
  10.7 82.1 all-gather.5
  120.7 51.3 all-gather.7
  174.2 56.2 all-gather.9
  233.2 37.8 reduce-scatter.2
  273.8 37.1 reduce-scatter.4

commit v4 on v3

--- a/solution.py
+++ b/solution.py
@@ -6,7 +6,6 @@
 from jax.sharding import PartitionSpec as P
 
 EXPERT_AXES = ("ex", "ez", "ec")
-RING_AXES = ("ez", "ec")
 
 
 def swapped(block, axis, count, stride):
@@ -98,33 +97,42 @@
     dispatch = jnp.any(position[..., None] == slots, axis=1).astype(jnp.bfloat16).reshape(
         tok_count, experts, capacity
     )
-    ring_rows = lax.all_gather(
-        jnp.concatenate([tokens, cotangent], axis=1), RING_AXES, axis=0, tiled=True
+    pad = jnp.zeros((tok_count, 128 - 2 * position.shape[1]), jnp.bfloat16)
+    packed = jnp.concatenate(
+        [tokens, cotangent, position.astype(jnp.bfloat16), gates, pad], axis=1
     )
-    ring_position = lax.all_gather(position, RING_AXES, axis=0, tiled=True)
-    ring_gates = lax.all_gather(gates, RING_AXES, axis=0, tiled=True)
+    ring_rows = lax.all_gather(packed, "ez", axis=0, tiled=True)
+    top = position.shape[1]
+    ring_position = ring_rows[:, 2 * features:2 * features + top].astype(jnp.int32)
+    ring_gates = ring_rows[:, 2 * features + top:2 * features + 2 * top]
+    my_z = lax.axis_index("ez")
     target = (
-        (jnp.arange(n_x, dtype=jnp.int32)[:, None] * ring + ring_index) * capacity
+        ((jnp.arange(n_x, dtype=jnp.int32)[:, None, None] * n_z + my_z) * n_c
+         + jnp.arange(n_c, dtype=jnp.int32)[None, :, None]) * capacity
         + jnp.arange(capacity, dtype=jnp.int32)
     )
-    match = ring_position[:, :, None, None] == target
-    picked = jnp.any(match, axis=1).astype(jnp.bfloat16).reshape(ring, tok_count, n_x, capacity)
+    match = ring_position[:, :, None, None, None] == target
+    picked = jnp.any(match, axis=1).astype(jnp.bfloat16).reshape(n_z, tok_count, n_x, n_c, capacity)
     picked_gate = jnp.sum(
-        jnp.where(match, ring_gates[:, :, None, None], jnp.zeros((), ring_gates.dtype)), axis=1
-    ).reshape(ring, tok_count, n_x, capacity)
-    ring_rows = ring_rows.reshape(ring, tok_count, 2 * features)
+        jnp.where(match, ring_gates[:, :, None, None, None], jnp.zeros((), ring_gates.dtype)), axis=1
+    ).reshape(n_z, tok_count, n_x, n_c, capacity)
+    ring_rows = ring_rows.reshape(n_z, tok_count, ring_rows.shape[-1])
     relay_tok = jnp.einsum(
-        "srxc,srd->cxsd", picked, ring_rows[:, :, :features], preferred_element_type=jnp.float32
-    ).astype(jnp.bfloat16)
+        "zrxcs,zrd->sxczd", picked, ring_rows[:, :, :features], preferred_element_type=jnp.float32
+    ).astype(jnp.bfloat16).reshape(capacity, n_x * n_c, n_z, features)
     relay_cot = jnp.einsum(
-        "srxc,srd->cxsd", picked_gate, ring_rows[:, :, features:], preferred_element_type=jnp.float32
-    ).astype(jnp.bfloat16)
+        "zrxcs,zrd->sxczd", picked_gate, ring_rows[:, :, features:2 * features],
+        preferred_element_type=jnp.float32,
+    ).astype(jnp.bfloat16).reshape(capacity, n_x * n_c, n_z, features)
+    dispatch = dispatch.reshape(tok_count, n_x, n_z, n_c, capacity).transpose(0, 1, 3, 2, 4).reshape(
+        tok_count, experts, capacity
+    )
 
     token_sum = jnp.zeros((tok_count, features), jnp.float32)
     sums = None
     for chunk in range(capacity):
         both = jnp.stack([relay_tok[chunk], relay_cot[chunk]], axis=0)
-        arrived = lax.all_to_all(both, "ex", split_axis=1, concat_axis=1, tiled=True)
+        arrived = lax.all_to_all(both, ("ex", "ec"), split_axis=1, concat_axis=1, tiled=True)
         arrived = arrived.reshape(2, experts, features)
         gathered = lax.all_gather(arrived, "dp", axis=1, tiled=True)
         row_grads, gate_grad, up_grad, down_grad = expert_work(
@@ -135,7 +143,9 @@
         summed_rows = lax.psum_scatter(
             row_grads.reshape(replicas, experts, features), "dp", scatter_dimension=0, tiled=True
         )
-        returned = lax.all_to_all(summed_rows[0], EXPERT_AXES, split_axis=0, concat_axis=0, tiled=True)
+        returned = lax.all_to_all(
+            summed_rows[0], ("ex", "ec", "ez"), split_axis=0, concat_axis=0, tiled=True
+        )
         token_sum = token_sum + jnp.einsum(
             "re,ed->rd", dispatch[:, :, chunk], returned, preferred_element_type=jnp.float32
         )

time: 374 us -> 373 us (level)
  waiting for transfers between devices: 169 us -> 226 us
  blocking collectives: 83.7 us -> 28.6 us
    all_gather x2 -> x0, blocking collectives: 65.2 us -> none  [the longest x1 37.9 us: on_device(): ring_position = lax.all_gather(position, RING_AXES, axis=0, tiled=True)]
    all_gather x1, waiting for transfers between devices: 14.4 us -> 72 us  [on_device(): ring_rows = lax.all_gather(packed, 'ez', axis=0, tiled=True)]
    all_to_all x1, blocking collectives: 18.4 us -> 28.6 us  [on_device(): lax.all_to_all(both, ('ex', 'ec'), split_axis=1, concat_axis=1, tiled=True)]
    unnamed x68 -> x71, local copies, waits for them, and re-layouts: 10.4 us -> 10.3 us
  transfers between devices with their start and end apart: 10 -> 10, of which waited for: 8 -> 8; matrix products, arithmetic and copies ran while one was open for 15% -> 13% of each run, Pallas kernels for 0% -> 0%
where the time goes in v4:
time: 373 us; the launch traced here: 372 us
  waiting for transfers between devices  226 us (61%)
  starting transfers between devices  36.2 us (10%)
  matrix products  32.1 us (9%)
  blocking collectives  28.6 us (8%)
  local copies, waits for them, and re-layouts  22.7 us (6%)
  between operations  15.1 us (4%)
  other arithmetic  11.8 us (3%)
    all_gather x1, waiting for transfers between devices, on_device(): ring_rows = lax.all_gather(packed, 'ez', axis=0, tiled=True)  72 us
    reduce_scatter x2, waiting for transfers between devices, on_device(): lax.psum_scatter(row_grads.reshape(replicas, experts, features), 'dp', sc...  49.9 us
    ppermute x2, waiting for transfers between devices, swapped(): return lax.ppermute(block, axis, route)  47.2 us
    all_to_all x2, waiting for transfers between devices, on_device(): lax.all_to_all(summed_rows[0], ('ex', 'ec', 'ez'), split_axis=0, concat_a...  30.7 us
    all_to_all x1, blocking collectives, on_device(): lax.all_to_all(both, ('ex', 'ec'), split_axis=1, concat_axis=1, tiled=True)  28.6 us
    all_to_all x2, starting transfers between devices, on_device(): lax.all_to_all(summed_rows[0], ('ex', 'ec', 'ez'), split_axis=0, concat_a...  24.4 us
    dot_general x12, matrix products, contract(): lax.dot_general(left, right, (((left_dim,), (right_dim,)), ((), ())), pre...  19.9 us
    all_gather x2, waiting for transfers between devices, on_device(): gathered = lax.all_gather(arrived, 'dp', axis=1, tiled=True)  13.2 us
  transfers between devices with their start and end apart: 10, of which 8 were waited for; matrix products, arithmetic and copies ran while one was open for 13% of the time, Pallas kernels for 0%

profile of v4, /device:TPU:1, one launch (start us, length us, event | category | flops | bytes accessed | tf_op | source)
XLA Modules:
  0.0 372.2 jit_solution(3108542194045402906)
XLA Ops:
  7.2 0.8 copy.151
  8.1 1.6 gather_fusion
  10.7 0.8 concatenate.9
  11.7 72.0 %all-gather.4.cloned.1.call-done = bf16[384,4224]{1,0:T(8,128)(2,1)} async-done(((bf16[24,4224]{1,0:T(8,128)(2,1)}), bf16[384,4224]{1,0:T(8,128)(2,1)}) %all-gather.4.cloned.1.call-update) | async-done | bytes 3244048 | tf_op jit(solution)/shard_map/all_gather | solution.py:104
  83.7 1.1 fusion.64
  85.4 2.1 fusion.4
  87.5 0.5 fusion.66
  88.4 2.1 fusion.3
  90.5 0.5 fusion.65
  91.4 28.6 %all_to_all.34 = bf16[2,8,16,2048]{3,2,0,1:T(8,128)(2,1)S(1)} all-to-all(bf16[2,8,16,2048]{3,2,0,1:T(8,128)(2,1)S(1)} %copy.167), channel_id=1, replica_groups=mesh['dp'=4,'ex'=4,'ez'=16,'ec'=2] {'ex','ec'}, dimensions={1} | all-to-all | bytes 2097152 | tf_op jit(solution)/shard_map/all_to_all | solution.py:135
  120.0 1.1 copy.168
  121.8 1.1 copy.173
  122.9 4.5 %all-to-all-start.2 = ((bf16[2,8,16,2048]{3,2,0,1:T(8,128)(2,1)}), bf16[2,8,16,2048]{3,2,0,1:T(8,128)(2,1)S(1)}, u32[]{:S(2)}, u32[]{:S(2)}) async-start(bf16[2,8,16,2048]{3,2,0,1:T(8,128)(2,1)} %copy.173), calls=%async_computation.3 | async-start | bytes 2097152 | tf_op jit(solution)/shard_map/all_to_all | solution.py:135
  127.4 1.2 constant_dynamic-update-slice_fusion.2
  128.6 1.2 constant_dynamic-update-slice_fusion.1
  129.8 12.6 %all-to-all-done.2 = bf16[2,8,16,2048]{3,2,0,1:T(8,128)(2,1)S(1)} async-done(((bf16[2,8,16,2048]{3,2,0,1:T(8,128)(2,1)}), bf16[2,8,16,2048]{3,2,0,1:T(8,128)(2,1)S(1)}, u32[]{:S(2)}, u32[]{:S(2)}) %all-to-all-start.2) | async-done | bytes 1048608 | tf_op jit(solution)/shard_map/all_to_all | solution.py:135
  142.4 1.0 copy.174
  143.5 1.2 constant_dynamic-update-slice_fusion
  144.7 2.4 collective-permute-start
  147.2 4.5 %collective-permute-start.1 = (f32[3,3,16]{2,0,1:T(4,128)S(1)}, f32[3,3,16]{2,0,1:T(4,128)S(1)}, u32[]{:S(2)}, u32[]{:S(2)}) collective-permute-start(f32[3,3,16]{2,0,1:T(4,128)S(1)} %pad_maximum_fusion.2), channel_id=1, source_target_pairs={{0,64},{64,0},{1,65},{65,1},{2,66},{66,2},{3,67},{67,3},{4,68},{68... | collective-permute-start | bytes 1736 | tf_op jit(solution)/shard_map/ppermute | solution.py:17
  151.7 0.6 fusion.54
  153.0 47.1 %collective-permute-done.1 = f32[3,3,16]{2,0,1:T(4,128)S(1)} collective-permute-done((f32[3,3,16]{2,0,1:T(4,128)S(1)}, f32[3,3,16]{2,0,1:T(4,128)S(1)}, u32[]{:S(2)}, u32[]{:S(2)}) %collective-permute-start.1) | collective-permute-done | bytes 608 | tf_op jit(solution)/shard_map/ppermute | solution.py:17
  200.3 2.0 broadcast_select_fusion
  202.2 0.6 convert_bitcast_fusion.3
  203.7 0.5 fusion.17
  204.2 1.4 fusion.16
  205.6 1.4 fusion.18
  207.0 2.6 fusion.22
  209.9 2.1 fusion.21
  211.9 0.9 multiply_convert_fusion.4
  212.9 0.5 broadcast_in_dim.73
  213.4 0.9 fusion.59
  214.5 0.5 broadcast_in_dim.71
  215.0 2.4 add_convert_fusion.1
  217.7 13.2 %all-gather.8.cloned.1.call-done = bf16[2,512,2048]{2,1,0:T(8,128)(2,1)} async-done(((bf16[2,128,2048]{2,1,0:T(8,128)(2,1)}), bf16[2,512,2048]{2,1,0:T(8,128)(2,1)}) %all-gather.8.cloned.1.call-update) | async-done | bytes 4194320 | tf_op jit(solution)/shard_map/all_gather | solution.py:137
  230.9 2.8 fusion.23
  234.0 0.8 fusion.24
  234.8 0.4 copy-done.11
  235.3 0.9 multiply_convert_fusion.2
  236.2 0.6 copy-done.2
  236.8 0.9 fusion.57
  237.7 0.5 copy-done.4
  238.2 2.4 add_convert_fusion
  240.6 30.9 %reduce-scatter.3.cloned.1.call-done = bf16[1,128,2048]{2,1,0:T(8,128)(2,1)} async-done(((bf16[4,128,2048]{2,1,0:T(8,128)(2,1)}), bf16[1,128,2048]{2,1,0:T(8,128)(2,1)}) %reduce-scatter.3.cloned.1.call-update) | async-done | bytes 524304 | tf_op jit(solution)/shard_map/reduce_scatter | solution.py:143
  271.5 0.5 broadcast.127
  272.1 2.0 reduce.1
  274.1 1.2 reshape.251
  275.2 16.8 %all-to-all-start.1 = ((bf16[128,2,1024]{2,1,0:T(2,128)(2,1)}), bf16[128,2,1024]{2,1,0:T(2,128)(2,1)S(1)}, u32[]{:S(2)}, u32[]{:S(2)}) async-start(bf16[128,2,1024]{2,1,0:T(2,128)(2,1)} %reshape.251), calls=%async_computation.2 | async-start | bytes 1048576 | tf_op jit(solution)/shard_map/all_to_all | solution.py:146
  292.5 19.0 %reduce-scatter.5.cloned.1.call-done = bf16[1,128,2048]{2,1,0:T(8,128)(2,1)} async-done(((bf16[4,128,2048]{2,1,0:T(8,128)(2,1)}), bf16[1,128,2048]{2,1,0:T(8,128)(2,1)}) %reduce-scatter.5.cloned.1.call-update) | async-done | bytes 524304 | tf_op jit(solution)/shard_map/reduce_scatter | solution.py:143
  311.5 2.0 reduce.2
  313.5 1.2 reshape.253
  314.7 9.7 %all-to-all-done.1 = bf16[128,2,1024]{2,1,0:T(2,128)(2,1)S(1)} async-done(((bf16[128,2,1024]{2,1,0:T(2,128)(2,1)}), bf16[128,2,1024]{2,1,0:T(2,128)(2,1)S(1)}, u32[]{:S(2)}, u32[]{:S(2)}) %all-to-all-start.1) | async-done | bytes 524320 | tf_op jit(solution)/shard_map/all_to_all | solution.py:146
  324.4 7.6 %all-to-all-start.3 = ((bf16[128,2,1024]{2,1,0:T(2,128)(2,1)}), bf16[128,2,1024]{2,1,0:T(2,128)(2,1)S(1)}, u32[]{:S(2)}, u32[]{:S(2)}) async-start(bf16[128,2,1024]{2,1,0:T(2,128)(2,1)} %reshape.253), calls=%async_computation.5 | async-start | bytes 1048576 | tf_op jit(solution)/shard_map/all_to_all | solution.py:146
  332.0 2.3 fusion.19
  334.3 3.2 fusion.6
  337.6 0.6 fusion.20
  338.2 1.5 fusion.7
  339.7 0.6 fusion.9
  340.8 1.5 fusion.5
  342.4 0.4 reshape.252
  342.8 0.4 fusion.39
  343.2 21.0 %all-to-all-done.3 = bf16[128,2,1024]{2,1,0:T(2,128)(2,1)S(1)} async-done(((bf16[128,2,1024]{2,1,0:T(2,128)(2,1)}), bf16[128,2,1024]{2,1,0:T(2,128)(2,1)S(1)}, u32[]{:S(2)}, u32[]{:S(2)}) %all-to-all-start.3) | async-done | bytes 524320 | tf_op jit(solution)/shard_map/all_to_all | solution.py:146
  364.2 0.4 reshape.254
  364.7 1.0 fusion.8
  (117 shorter events, 6.4 us)
Async XLA Ops:
  7.2 0.9 copy-start
  7.2 76.5 %all-gather.4.cloned.1.call-start = ((), (), s32[]{:S(2)}) async-start(), calls=%async_computation.6 | async-start | bytes 3446784 | tf_op jit(solution)/shard_map/all_gather | solution.py:104
  8.1 2.4 copy-start.19
  8.1 2.5 copy-start.14
  8.1 2.5 copy-start.15
  11.4 195.6 %all-gather.6.cloned.1.call-start = ((), (), s32[]{:S(2)}) async-start(), calls=%async_computation.7 | async-start | bytes 5242880 | tf_op jit(solution)/shard_map/all_gather | solution.py:137
  122.9 19.5 %all-to-all-start.2 = ((bf16[2,8,16,2048]{3,2,0,1:T(8,128)(2,1)}), bf16[2,8,16,2048]{3,2,0,1:T(8,128)(2,1)S(1)}, u32[]{:S(2)}, u32[]{:S(2)}) async-start(bf16[2,8,16,2048]{3,2,0,1:T(8,128)(2,1)} %copy.173), calls=%async_computation.3 | async-start | bytes 2097152 | tf_op jit(solution)/shard_map/all_to_all | solution.py:135
  127.4 103.5 %all-gather.8.cloned.1.call-start = ((), (), s32[]{:S(2)}) async-start(), calls=%async_computation.9 | async-start | bytes 5242880 | tf_op jit(solution)/shard_map/all_gather | solution.py:137
  129.8 17.4 %copy-start.16 = (f32[1,3,16]{2,0,1:T(1,128)S(1)}, f32[1,3,16]{2,0,1:T(1,128)}, u32[]{:S(2)}) copy-start(f32[1,3,16]{2,0,1:T(1,128)} %param.21) | copy-start | bytes 580
  129.8 17.4 %copy-start.17 = (f32[1,3,16]{2,0,1:T(1,128)S(1)}, f32[1,3,16]{2,0,1:T(1,128)}, u32[]{:S(2)}) copy-start(f32[1,3,16]{2,0,1:T(1,128)} %param.20) | copy-start | bytes 580
  129.8 17.4 %copy-start.18 = (f32[1,3,16]{2,0,1:T(1,128)S(1)}, f32[1,3,16]{2,0,1:T(1,128)}, u32[]{:S(2)}) copy-start(f32[1,3,16]{2,0,1:T(1,128)} %param.19) | copy-start | bytes 580
  143.5 128.1 %reduce-scatter.3.cloned.1.call-start = ((), (), s32[]{:S(2)}) async-start(), calls=%async_computation.8 | async-start | bytes 2621440 | tf_op jit(solution)/shard_map/reduce_scatter | solution.py:143
  144.7 55.5 %copy-start.5 = (bf16[3,192,2048]{2,1,0:T(8,128)(2,1)}, bf16[3,192,2048]{2,1,0:T(8,128)(2,1)S(1)}, u32[]{:S(2)}) copy-start(bf16[3,192,2048]{2,1,0:T(8,128)(2,1)S(1)} %constant_dynamic-update-slice_fusion) | copy-start | bytes 7077892
  144.7 55.5 %collective-permute-start = (bf16[3,192,2048]{2,1,0:T(8,128)(2,1)S(1)}, bf16[3,192,2048]{2,1,0:T(8,128)(2,1)}, u32[]{:S(2)}, u32[]{:S(2)}) collective-permute-start(bf16[3,192,2048]{2,1,0:T(8,128)(2,1)S(1)} %constant_dynamic-update-slice_fusion), channel_id=1, source_target_pairs={{0,64},{64,0},{1,65},{65,1},{2,66},{66,2},{3,67},{67,3},{4,68},{68... | collective-permute-start | bytes 7077896 | tf_op jit(solution)/shard_map/ppermute | solution.py:17
  147.2 53.0 %collective-permute-start.1 = (f32[3,3,16]{2,0,1:T(4,128)S(1)}, f32[3,3,16]{2,0,1:T(4,128)S(1)}, u32[]{:S(2)}, u32[]{:S(2)}) collective-permute-start(f32[3,3,16]{2,0,1:T(4,128)S(1)} %pad_maximum_fusion.2), channel_id=1, source_target_pairs={{0,64},{64,0},{1,65},{65,1},{2,66},{66,2},{3,67},{67,3},{4,68},{68... | collective-permute-start | bytes 1736 | tf_op jit(solution)/shard_map/ppermute | solution.py:17
  207.0 2.9 copy-start.8
  209.6 2.3 copy-start.24
  209.9 2.1 copy-start.10
  211.9 1.0 copy-start.26
  212.9 2.1 copy-start.12
  213.3 1.1 copy-start.1
  215.0 2.4 copy-start.3
  217.4 94.0 %reduce-scatter.5.cloned.1.call-start = ((), (), s32[]{:S(2)}) async-start(), calls=%async_computation.10 | async-start | bytes 2621440 | tf_op jit(solution)/shard_map/reduce_scatter | solution.py:143
  230.9 3.1 copy-start.6
  234.0 0.9 copy-start.20
  234.0 1.3 copy-start.11
  235.3 0.9 copy-start.22
  235.3 1.5 copy-start.2
  236.8 1.4 copy-start.4
  275.2 56.7 %copy-start.13 = (bf16[512,192]{0,1:T(8,128)(2,1)S(1)}, bf16[512,192]{0,1:T(8,128)(2,1)}, u32[]{:S(2)}) copy-start(bf16[512,192]{0,1:T(8,128)(2,1)} %copy-done.12) | copy-start | bytes 589828
  275.2 49.1 %all-to-all-start.1 = ((bf16[128,2,1024]{2,1,0:T(2,128)(2,1)}), bf16[128,2,1024]{2,1,0:T(2,128)(2,1)S(1)}, u32[]{:S(2)}, u32[]{:S(2)}) async-start(bf16[128,2,1024]{2,1,0:T(2,128)(2,1)} %reshape.251), calls=%async_computation.2 | async-start | bytes 1048576 | tf_op jit(solution)/shard_map/all_to_all | solution.py:146
  324.4 39.9 %all-to-all-start.3 = ((bf16[128,2,1024]{2,1,0:T(2,128)(2,1)}), bf16[128,2,1024]{2,1,0:T(2,128)(2,1)S(1)}, u32[]{:S(2)}, u32[]{:S(2)}) async-start(bf16[128,2,1024]{2,1,0:T(2,128)(2,1)} %reshape.253), calls=%async_computation.5 | async-start | bytes 1048576 | tf_op jit(solution)/shard_map/all_to_all | solution.py:146
  332.0 5.6 %copy-start.9 = (bf16[2,512,2048]{2,1,0:T(8,128)(2,1)S(1)}, bf16[2,512,2048]{2,1,0:T(8,128)(2,1)}, u32[]{:S(2)}) copy-start(bf16[2,512,2048]{2,1,0:T(8,128)(2,1)} %all-gather.6.cloned.1.call-done) | copy-start | bytes 12582916
  334.3 3.9 %copy-start.7 = (bf16[2,512,2048]{2,1,0:T(8,128)(2,1)S(1)}, bf16[2,512,2048]{2,1,0:T(8,128)(2,1)}, u32[]{:S(2)}) copy-start(bf16[2,512,2048]{2,1,0:T(8,128)(2,1)} %all-gather.8.cloned.1.call-done) | copy-start | bytes 12582916
  338.2 1.5 copy-start.25
  338.2 1.5 copy-start.27
  339.7 1.0 copy-start.21
  339.7 1.1 copy-start.23
Sparse Core Ops, SparseCore 0:
  11.6 72.0 all-gather.3
  121.2 51.2 all-gather.5
  174.6 56.2 all-gather.7
  233.6 37.8 reduce-scatter.2
  274.2 37.1 reduce-scatter.4

commit v5 on v4

--- a/solution.py
+++ b/solution.py
@@ -30,6 +30,20 @@
     marked = (flattened[:, None] == numbers).astype(jnp.int32)
     slot_index = jnp.sum((jnp.cumsum(marked, axis=0) - 1) * marked, axis=-1)
     return (flattened * capacity + slot_index).reshape(route_lists.shape)
+
+
+def dp_gather(block, count):
+    shifted = [lax.ppermute(block, "dp", [(i, (i + r) % count) for i in range(count)]) for r in range(1, count)]
+    return [block] + shifted
+
+
+def dp_reduce(parts, count):
+    total = parts[0].astype(jnp.float32)
+    for r in range(1, count):
+        total = total + lax.ppermute(
+            parts[r], "dp", [(i, (i - r) % count) for i in range(count)]
+        ).astype(jnp.float32)
+    return total
 
 
 def contract(left, right, left_dim, right_dim):
@@ -134,17 +148,17 @@
         both = jnp.stack([relay_tok[chunk], relay_cot[chunk]], axis=0)
         arrived = lax.all_to_all(both, ("ex", "ec"), split_axis=1, concat_axis=1, tiled=True)
         arrived = arrived.reshape(2, experts, features)
-        gathered = lax.all_gather(arrived, "dp", axis=1, tiled=True)
+        blocks = dp_gather(arrived, replicas)
+        token_rows = jnp.concatenate([b[0] for b in blocks], axis=0)
+        cot_rows = jnp.concatenate([b[1] for b in blocks], axis=0)
         row_grads, gate_grad, up_grad, down_grad = expert_work(
-            gathered[0], gathered[1], w_gate, w_up, w_down
+            token_rows, cot_rows, w_gate, w_up, w_down
         )
         part = (gate_grad, up_grad, down_grad)
         sums = part if sums is None else tuple(a + b for a, b in zip(sums, part))
-        summed_rows = lax.psum_scatter(
-            row_grads.reshape(replicas, experts, features), "dp", scatter_dimension=0, tiled=True
-        )
+        summed_rows = dp_reduce(row_grads.reshape(replicas, experts, features), replicas)
         returned = lax.all_to_all(
-            summed_rows[0], ("ex", "ec", "ez"), split_axis=0, concat_axis=0, tiled=True
+            summed_rows.astype(jnp.bfloat16), ("ex", "ec", "ez"), split_axis=0, concat_axis=0, tiled=True
         )
         token_sum = token_sum + jnp.einsum(
             "re,ed->rd", dispatch[:, :, chunk], returned, preferred_element_type=jnp.float32

time: 373 us -> 386 us (1.035)
  starting transfers between devices: 36.2 us -> 92.2 us
  blocking collectives: 28.6 us -> 0 us
  waiting for transfers between devices: 226 us -> 210 us
  local copies, waits for them, and re-layouts: 22.7 us -> 31.7 us
  matrix products: 32.1 us -> 23.7 us
    ppermute x0 -> x12, waiting for transfers between devices: none -> 113 us  [the longest x6 72.3 us: dp_gather(): lax.ppermute(block, 'dp', [(i, (i + r) % count) for i in range(count)])]
    reduce_scatter x2 -> x0, waiting for transfers between devices: 49.9 us -> none  [on_device(): lax.psum_scatter(row_grads.reshape(replicas, experts, features), 'dp', sc...]
    ppermute x2, waiting for transfers between devices: 47.2 us -> 0.01 us  [swapped(): return lax.ppermute(block, axis, route)]
    ppermute x0 -> x12, starting transfers between devices: none -> 38.4 us  [the longest x6 19.9 us: dp_gather(): lax.ppermute(block, 'dp', [(i, (i + r) % count) for i in range(count)])]
    all_to_all x1 -> x0, blocking collectives: 28.6 us -> none  [on_device(): lax.all_to_all(both, ('ex', 'ec'), split_axis=1, concat_axis=1, tiled=True)]
    all_gather x2 -> x0, waiting for transfers between devices: 13.2 us -> none  [on_device(): gathered = lax.all_gather(arrived, 'dp', axis=1, tiled=True)]
    all_to_all x1 -> x2, starting transfers between devices: 4.5 us -> 17.7 us  [on_device(): lax.all_to_all(both, ('ex', 'ec'), split_axis=1, concat_axis=1, tiled=True)]
    all_gather x1, waiting for transfers between devices: 72 us -> 60.9 us  [on_device(): ring_rows = lax.all_gather(packed, 'ez', axis=0, tiled=True)]
  transfers between devices with their start and end apart: 10 -> 19, of which waited for: 8 -> 15; matrix products, arithmetic and copies ran while one was open for 13% -> 12% of each run, Pallas kernels for 0% -> 0%
where the time goes in v5:
time: 386 us; the launch traced here: 385 us
  waiting for transfers between devices  210 us (54%)
  starting transfers between devices  92.2 us (24%)
  local copies, waits for them, and re-layouts  31.7 us (8%)
  matrix products  23.7 us (6%)
  between operations  15.9 us (4%)
  other arithmetic  11.7 us (3%)
    ppermute x6, waiting for transfers between devices, dp_gather(): lax.ppermute(block, 'dp', [(i, (i + r) % count) for i in range(count)])  72.3 us
    all_gather x1, waiting for transfers between devices, on_device(): ring_rows = lax.all_gather(packed, 'ez', axis=0, tiled=True)  60.9 us
    ppermute x6, waiting for transfers between devices, dp_reduce(): lax.ppermute(parts[r], 'dp', [(i, (i - r) % count) for i in range(count)])  40.9 us
    all_to_all x2, starting transfers between devices, on_device(): lax.all_to_all(summed_rows.astype(jnp.bfloat16), ('ex', 'ec', 'ez'), spli...  28.6 us
    all_to_all x2, waiting for transfers between devices, on_device(): lax.all_to_all(summed_rows.astype(jnp.bfloat16), ('ex', 'ec', 'ez'), spli...  22.7 us
    ppermute x6, starting transfers between devices, dp_gather(): lax.ppermute(block, 'dp', [(i, (i + r) % count) for i in range(count)])  19.9 us
    ppermute x6, starting transfers between devices, dp_reduce(): lax.ppermute(parts[r], 'dp', [(i, (i - r) % count) for i in range(count)])  18.5 us
    all_to_all x2, starting transfers between devices, on_device(): lax.all_to_all(both, ('ex', 'ec'), split_axis=1, concat_axis=1, tiled=True)  17.7 us
  transfers between devices with their start and end apart: 19, of which 15 were waited for; matrix products, arithmetic and copies ran while one was open for 12% of the time, Pallas kernels for 0%

profile of v5, /device:TPU:1, one launch (start us, length us, event | category | flops | bytes accessed | tf_op | source)
XLA Modules:
  0.0 385.2 jit_solution(8829693196814806419)
XLA Ops:
  8.2 1.6 gather_fusion
  11.6 5.5 %collective-permute-start.4 = (f32[3,3,16]{2,0,1:T(4,128)S(1)}, f32[3,3,16]{2,0,1:T(4,128)S(1)}, u32[]{:S(2)}, u32[]{:S(2)}) collective-permute-start(f32[3,3,16]{2,0,1:T(4,128)S(1)} %pad_maximum_fusion.10), channel_id=1, source_target_pairs={{0,64},{64,0},{1,65},{65,1},{2,66},{66,2},{3,67},{67,3},{4,68},{68... | collective-permute-start | bytes 1736 | tf_op jit(solution)/shard_map/ppermute | solution.py:17
  17.1 1.0 constant_dynamic-update-slice_fusion.2
  18.0 0.9 constant_dynamic-update-slice_fusion.1
  19.0 1.0 constant_dynamic-update-slice_fusion
  19.9 1.9 collective-permute-start.3
  23.3 60.9 %all-gather.2.cloned.1.call-done = bf16[384,4224]{1,0:T(8,128)(2,1)} async-done(((bf16[24,4224]{1,0:T(8,128)(2,1)}), bf16[384,4224]{1,0:T(8,128)(2,1)}) %all-gather.2.cloned.1.call-update) | async-done | bytes 3244048 | tf_op jit(solution)/shard_map/all_gather | solution.py:118
  84.2 1.1 fusion.46
  85.7 2.1 fusion.4
  88.9 2.1 fusion.3
  91.9 1.1 copy.175
  93.0 13.3 %all-to-all-start.2 = ((bf16[2,8,16,2048]{3,2,0,1:T(8,128)(2,1)}), bf16[2,8,16,2048]{3,2,0,1:T(8,128)(2,1)S(1)}, u32[]{:S(2)}, u32[]{:S(2)}) async-start(bf16[2,8,16,2048]{3,2,0,1:T(8,128)(2,1)} %copy.175), calls=%async_computation.2 | async-start | bytes 2097152 | tf_op jit(solution)/shard_map/all_to_all | solution.py:149
  107.0 1.0 copy.169
  108.0 13.2 %all-to-all-done.2 = bf16[2,8,16,2048]{3,2,0,1:T(8,128)(2,1)S(1)} async-done(((bf16[2,8,16,2048]{3,2,0,1:T(8,128)(2,1)}), bf16[2,8,16,2048]{3,2,0,1:T(8,128)(2,1)S(1)}, u32[]{:S(2)}, u32[]{:S(2)}) %all-to-all-start.2) | async-done | bytes 1048608 | tf_op jit(solution)/shard_map/all_to_all | solution.py:149
  121.2 4.4 %all-to-all-start = ((bf16[2,8,16,2048]{3,2,0,1:T(8,128)(2,1)}), bf16[2,8,16,2048]{3,2,0,1:T(8,128)(2,1)S(1)}, u32[]{:S(2)}, u32[]{:S(2)}) async-start(bf16[2,8,16,2048]{3,2,0,1:T(8,128)(2,1)} %copy.169), calls=%async_computation | async-start | bytes 2097152 | tf_op jit(solution)/shard_map/all_to_all | solution.py:149
  125.6 1.9 broadcast_select_fusion
  127.6 1.2 copy.176
  128.8 3.3 collective-permute-start.8
  133.0 2.1 fusion.10
  135.2 4.4 %collective-permute-start.9 = (bf16[2,128,2048]{2,1,0:T(8,128)(2,1)}, bf16[2,128,2048]{2,1,0:T(8,128)(2,1)}, u32[]{:S(2)}, u32[]{:S(2)}) collective-permute-start(bf16[2,128,2048]{2,1,0:T(8,128)(2,1)} %bitcast.36), channel_id=1, source_target_pairs={{0,256},{128,384},{256,0},{384,128},{1,257},{129,385},{257,1},{385... | collective-permute-start | bytes 3145736 | tf_op jit(solution)/shard_map/ppermute | solution.py:36
  139.6 2.7 collective-permute-start.10
  142.4 2.5 collective-permute-start
  145.0 3.5 collective-permute-start.1
  148.6 8.2 %collective-permute-done.8 = bf16[2,128,2048]{2,1,0:T(8,128)(2,1)} collective-permute-done((bf16[2,128,2048]{2,1,0:T(8,128)(2,1)}, bf16[2,128,2048]{2,1,0:T(8,128)(2,1)}, u32[]{:S(2)}, u32[]{:S(2)}) %collective-permute-start.8) | collective-permute-done | bytes 1048608 | tf_op jit(solution)/shard_map/ppermute | solution.py:36
  156.9 3.5 collective-permute-start.2
  160.3 1.3 slice_bitcast_fusion.12
  161.7 18.8 %collective-permute-done.9 = bf16[2,128,2048]{2,1,0:T(8,128)(2,1)} collective-permute-done((bf16[2,128,2048]{2,1,0:T(8,128)(2,1)}, bf16[2,128,2048]{2,1,0:T(8,128)(2,1)}, u32[]{:S(2)}, u32[]{:S(2)}) %collective-permute-start.9) | collective-permute-done | bytes 1048608 | tf_op jit(solution)/shard_map/ppermute | solution.py:36
  180.5 1.3 slice_bitcast_fusion.11
  181.8 2.9 collective-permute-done.10
  184.7 1.3 slice_bitcast_fusion.10
  187.0 14.7 %collective-permute-done = bf16[2,128,2048]{2,1,0:T(8,128)(2,1)S(1)} collective-permute-done((bf16[2,128,2048]{2,1,0:T(8,128)(2,1)S(1)}, bf16[2,128,2048]{2,1,0:T(8,128)(2,1)S(1)}, u32[]{:S(2)}, u32[]{:S(2)}) %collective-permute-start) | collective-permute-done | bytes 1048608 | tf_op jit(solution)/shard_map/ppermute | solution.py:36
  201.8 23.6 %collective-permute-done.1 = bf16[2,128,2048]{2,1,0:T(8,128)(2,1)S(1)} collective-permute-done((bf16[2,128,2048]{2,1,0:T(8,128)(2,1)S(1)}, bf16[2,128,2048]{2,1,0:T(8,128)(2,1)S(1)}, u32[]{:S(2)}, u32[]{:S(2)}) %collective-permute-start.1) | collective-permute-done | bytes 1048608 | tf_op jit(solution)/shard_map/ppermute | solution.py:36
  225.4 4.1 %collective-permute-done.2 = bf16[2,128,2048]{2,1,0:T(8,128)(2,1)S(1)} collective-permute-done((bf16[2,128,2048]{2,1,0:T(8,128)(2,1)S(1)}, bf16[2,128,2048]{2,1,0:T(8,128)(2,1)S(1)}, u32[]{:S(2)}, u32[]{:S(2)}) %collective-permute-start.2) | collective-permute-done | bytes 1048608 | tf_op jit(solution)/shard_map/ppermute | solution.py:36
  232.9 1.0 multiply_convert_fusion.4
  235.6 4.9 %collective-permute-start.5 = (bf16[128,2048]{1,0:T(8,128)(2,1)S(1)}, bf16[128,2048]{1,0:T(8,128)(2,1)S(1)}, u32[]{:S(2)}, u32[]{:S(2)}) collective-permute-start(bf16[128,2048]{1,0:T(8,128)(2,1)S(1)} %get-tuple-element.13), channel_id=1, source_target_pairs={{0,384},{128,0},{256,128},{384,256},{1,385},{129,1},{257,129},{385... | collective-permute-start | bytes 1572872 | tf_op jit(solution)/shard_map/ppermute | solution.py:43
  240.5 3.3 collective-permute-start.6
  243.9 1.9 collective-permute-start.7
  245.8 0.9 fusion.56
  246.7 1.9 multiply_convert_fusion.2
  248.6 3.3 collective-permute-done.5
  252.0 4.7 %collective-permute-done.6 = bf16[128,2048]{1,0:T(8,128)(2,1)S(1)} collective-permute-done((bf16[128,2048]{1,0:T(8,128)(2,1)S(1)}, bf16[128,2048]{1,0:T(8,128)(2,1)S(1)}, u32[]{:S(2)}, u32[]{:S(2)}) %collective-permute-start.6) | collective-permute-done | bytes 524320 | tf_op jit(solution)/shard_map/ppermute | solution.py:43
  256.7 12.3 %collective-permute-done.7 = bf16[128,2048]{1,0:T(8,128)(2,1)S(1)} collective-permute-done((bf16[128,2048]{1,0:T(8,128)(2,1)S(1)}, bf16[128,2048]{1,0:T(8,128)(2,1)S(1)}, u32[]{:S(2)}, u32[]{:S(2)}) %collective-permute-start.7) | collective-permute-done | bytes 524320 | tf_op jit(solution)/shard_map/ppermute | solution.py:43
  269.9 1.7 reduce.1
  271.5 2.2 reshape.198
  273.8 12.3 %all-to-all-start.1 = ((bf16[128,2,1024]{2,1,0:T(2,128)(2,1)}), bf16[128,2,1024]{2,1,0:T(2,128)(2,1)S(1)}, u32[]{:S(2)}, u32[]{:S(2)}) async-start(bf16[128,2,1024]{2,1,0:T(2,128)(2,1)} %reshape.198), calls=%async_computation.1 | async-start | bytes 1048576 | tf_op jit(solution)/shard_map/all_to_all | solution.py:160
  286.1 2.0 fusion.57
  288.9 1.3 copy-done.1
  290.2 1.2 fusion.47
  291.4 2.2 collective-permute-start.11
  293.6 3.4 collective-permute-start.12
  297.0 2.7 collective-permute-start.13
  300.1 1.8 fusion.59
  301.9 4.2 %collective-permute-done.11 = bf16[128,2048]{1,0:T(8,128)(2,1)S(1)} collective-permute-done((bf16[128,2048]{1,0:T(8,128)(2,1)}, bf16[128,2048]{1,0:T(8,128)(2,1)S(1)}, u32[]{:S(2)}, u32[]{:S(2)}) %collective-permute-start.11) | collective-permute-done | bytes 524320 | tf_op jit(solution)/shard_map/ppermute | solution.py:43
  306.2 3.5 collective-permute-done.12
  309.7 12.7 %collective-permute-done.13 = bf16[128,2048]{1,0:T(8,128)(2,1)} collective-permute-done((bf16[128,2048]{1,0:T(8,128)(2,1)}, bf16[128,2048]{1,0:T(8,128)(2,1)}, u32[]{:S(2)}, u32[]{:S(2)}) %collective-permute-start.13) | collective-permute-done | bytes 524320 | tf_op jit(solution)/shard_map/ppermute | solution.py:43
  322.4 1.8 fusion.13
  324.3 1.7 reduce.2
  326.0 2.2 reshape.200
  328.2 16.3 %all-to-all-start.3 = ((bf16[128,2,1024]{2,1,0:T(2,128)(2,1)}), bf16[128,2,1024]{2,1,0:T(2,128)(2,1)S(1)}, u32[]{:S(2)}, u32[]{:S(2)}) async-start(bf16[128,2,1024]{2,1,0:T(2,128)(2,1)} %reshape.200), calls=%async_computation.3 | async-start | bytes 1048576 | tf_op jit(solution)/shard_map/all_to_all | solution.py:160
  346.6 1.5 fusion.6
  348.1 1.5 fusion.7
  351.8 1.5 fusion.5
  354.2 22.7 %all-to-all-done.3 = bf16[128,2,1024]{2,1,0:T(2,128)(2,1)S(1)} async-done(((bf16[128,2,1024]{2,1,0:T(2,128)(2,1)}), bf16[128,2,1024]{2,1,0:T(2,128)(2,1)S(1)}, u32[]{:S(2)}, u32[]{:S(2)}) %all-to-all-start.3) | async-done | bytes 524320 | tf_op jit(solution)/shard_map/all_to_all | solution.py:160
  377.3 1.0 fusion.8
  (192 shorter events, 21.1 us)
Async XLA Ops:
  7.2 77.0 %all-gather.2.cloned.1.call-start = ((), (), s32[]{:S(2)}) async-start(), calls=%async_computation.4 | async-start | bytes 3446784 | tf_op jit(solution)/shard_map/all_gather | solution.py:118
  8.1 2.5 copy-start.46
  8.1 2.6 copy-start.41
  8.1 2.6 copy-start.42
  8.1 3.4 copy-start.43
  8.1 3.4 copy-start.44
  8.2 3.4 copy-start.45
  9.7 7.3 %copy-start.7 = (bf16[1,192,2048]{2,1,0:T(8,128)(2,1)S(1)}, bf16[1,192,2048]{2,1,0:T(8,128)(2,1)}, u32[]{:S(2)}) copy-start(bf16[1,192,2048]{2,1,0:T(8,128)(2,1)} %param.16) | copy-start | bytes 2359300
  9.7 8.3 %copy-start.8 = (bf16[1,192,2048]{2,1,0:T(8,128)(2,1)S(1)}, bf16[1,192,2048]{2,1,0:T(8,128)(2,1)}, u32[]{:S(2)}) copy-start(bf16[1,192,2048]{2,1,0:T(8,128)(2,1)} %param.17) | copy-start | bytes 2359300
  10.3 8.7 %copy-start.9 = (bf16[1,192,2048]{2,1,0:T(8,128)(2,1)S(1)}, bf16[1,192,2048]{2,1,0:T(8,128)(2,1)}, u32[]{:S(2)}) copy-start(bf16[1,192,2048]{2,1,0:T(8,128)(2,1)} %param.18) | copy-start | bytes 2359300
  11.6 94.7 %collective-permute-start.4 = (f32[3,3,16]{2,0,1:T(4,128)S(1)}, f32[3,3,16]{2,0,1:T(4,128)S(1)}, u32[]{:S(2)}, u32[]{:S(2)}) collective-permute-start(f32[3,3,16]{2,0,1:T(4,128)S(1)} %pad_maximum_fusion.10), channel_id=1, source_target_pairs={{0,64},{64,0},{1,65},{65,1},{2,66},{66,2},{3,67},{67,3},{4,68},{68... | collective-permute-start | bytes 1736 | tf_op jit(solution)/shard_map/ppermute | solution.py:17
  19.9 105.7 %collective-permute-start.3 = (bf16[3,192,2048]{2,1,0:T(8,128)(2,1)}, bf16[3,192,2048]{2,1,0:T(8,128)(2,1)}, u32[]{:S(2)}, u32[]{:S(2)}) collective-permute-start(bf16[3,192,2048]{2,1,0:T(8,128)(2,1)} %constant_dynamic-update-slice_fusion), channel_id=1, source_target_pairs={{0,64},{64,0},{1,65},{65,1},{2,66},{66,2},{3,67},{67,3},{4,68},{68... | collective-permute-start | bytes 7077896 | tf_op jit(solution)/shard_map/ppermute | solution.py:17
  93.0 28.3 %all-to-all-start.2 = ((bf16[2,8,16,2048]{3,2,0,1:T(8,128)(2,1)}), bf16[2,8,16,2048]{3,2,0,1:T(8,128)(2,1)S(1)}, u32[]{:S(2)}, u32[]{:S(2)}) async-start(bf16[2,8,16,2048]{3,2,0,1:T(8,128)(2,1)} %copy.175), calls=%async_computation.2 | async-start | bytes 2097152 | tf_op jit(solution)/shard_map/all_to_all | solution.py:149
  121.2 21.1 %all-to-all-start = ((bf16[2,8,16,2048]{3,2,0,1:T(8,128)(2,1)}), bf16[2,8,16,2048]{3,2,0,1:T(8,128)(2,1)S(1)}, u32[]{:S(2)}, u32[]{:S(2)}) async-start(bf16[2,8,16,2048]{3,2,0,1:T(8,128)(2,1)} %copy.169), calls=%async_computation | async-start | bytes 2097152 | tf_op jit(solution)/shard_map/all_to_all | solution.py:149
  127.6 5.5 %copy-start.3 = (bf16[3,192,2048]{2,1,0:T(8,128)(2,1)}, bf16[3,192,2048]{2,1,0:T(8,128)(2,1)S(1)}, u32[]{:S(2)}) copy-start(bf16[3,192,2048]{2,1,0:T(8,128)(2,1)S(1)} %broadcast_select_fusion) | copy-start | bytes 7077892
  128.8 28.1 %collective-permute-start.8 = (bf16[2,128,2048]{2,1,0:T(8,128)(2,1)}, bf16[2,128,2048]{2,1,0:T(8,128)(2,1)}, u32[]{:S(2)}, u32[]{:S(2)}) collective-permute-start(bf16[2,128,2048]{2,1,0:T(8,128)(2,1)} %bitcast.36), channel_id=1, source_target_pairs={{0,128},{128,256},{256,384},{384,0},{1,129},{129,257},{257,385},{3... | collective-permute-start | bytes 3145736 | tf_op jit(solution)/shard_map/ppermute | solution.py:36
  135.2 45.3 %collective-permute-start.9 = (bf16[2,128,2048]{2,1,0:T(8,128)(2,1)}, bf16[2,128,2048]{2,1,0:T(8,128)(2,1)}, u32[]{:S(2)}, u32[]{:S(2)}) collective-permute-start(bf16[2,128,2048]{2,1,0:T(8,128)(2,1)} %bitcast.36), channel_id=1, source_target_pairs={{0,256},{128,384},{256,0},{384,128},{1,257},{129,385},{257,1},{385... | collective-permute-start | bytes 3145736 | tf_op jit(solution)/shard_map/ppermute | solution.py:36
  139.6 45.1 %collective-permute-start.10 = (bf16[2,128,2048]{2,1,0:T(8,128)(2,1)}, bf16[2,128,2048]{2,1,0:T(8,128)(2,1)}, u32[]{:S(2)}, u32[]{:S(2)}) collective-permute-start(bf16[2,128,2048]{2,1,0:T(8,128)(2,1)} %bitcast.36), channel_id=1, source_target_pairs={{0,384},{128,0},{256,128},{384,256},{1,385},{129,1},{257,129},{385... | collective-permute-start | bytes 3145736 | tf_op jit(solution)/shard_map/ppermute | solution.py:36
  142.4 59.3 %collective-permute-start = (bf16[2,128,2048]{2,1,0:T(8,128)(2,1)S(1)}, bf16[2,128,2048]{2,1,0:T(8,128)(2,1)S(1)}, u32[]{:S(2)}, u32[]{:S(2)}) collective-permute-start(bf16[2,128,2048]{2,1,0:T(8,128)(2,1)S(1)} %bitcast.171), channel_id=1, source_target_pairs={{0,128},{128,256},{256,384},{384,0},{1,129},{129,257},{257,385},{3... | collective-permute-start | bytes 3145736 | tf_op jit(solution)/shard_map/ppermute | solution.py:36
  145.0 80.4 %collective-permute-start.1 = (bf16[2,128,2048]{2,1,0:T(8,128)(2,1)S(1)}, bf16[2,128,2048]{2,1,0:T(8,128)(2,1)S(1)}, u32[]{:S(2)}, u32[]{:S(2)}) collective-permute-start(bf16[2,128,2048]{2,1,0:T(8,128)(2,1)S(1)} %bitcast.172), channel_id=1, source_target_pairs={{0,256},{128,384},{256,0},{384,128},{1,257},{129,385},{257,1},{385... | collective-permute-start | bytes 3145736 | tf_op jit(solution)/shard_map/ppermute | solution.py:36
  148.5 98.2 %copy-start.15 = (bf16[1,8,16,2048]{3,2,0,1:T(8,128)(2,1)}, bf16[1,8,16,2048]{3,2,0,1:T(8,128)(2,1)S(1)}, u32[]{:S(2)}) copy-start(bf16[1,8,16,2048]{3,2,0,1:T(8,128)(2,1)S(1)} %get-tuple-element.16) | copy-start | bytes 1572868
  148.6 82.0 %copy-start.17 = (bf16[1,8,16,2048]{3,2,0,1:T(8,128)(2,1)}, bf16[1,8,16,2048]{3,2,0,1:T(8,128)(2,1)S(1)}, u32[]{:S(2)}) copy-start(bf16[1,8,16,2048]{3,2,0,1:T(8,128)(2,1)S(1)} %get-tuple-element.29) | copy-start | bytes 1572868
  148.6 84.0 %copy-start.13 = (bf16[1,8,16,2048]{3,2,0,1:T(8,128)(2,1)}, bf16[1,8,16,2048]{3,2,0,1:T(8,128)(2,1)S(1)}, u32[]{:S(2)}) copy-start(bf16[1,8,16,2048]{3,2,0,1:T(8,128)(2,1)S(1)} %get-tuple-element.28) | copy-start | bytes 1572868
  156.9 72.7 %collective-permute-start.2 = (bf16[2,128,2048]{2,1,0:T(8,128)(2,1)S(1)}, bf16[2,128,2048]{2,1,0:T(8,128)(2,1)S(1)}, u32[]{:S(2)}, u32[]{:S(2)}) collective-permute-start(bf16[2,128,2048]{2,1,0:T(8,128)(2,1)S(1)} %bitcast.173), channel_id=1, source_target_pairs={{0,384},{128,0},{256,128},{384,256},{1,385},{129,1},{257,129},{385... | collective-permute-start | bytes 3145736 | tf_op jit(solution)/shard_map/ppermute | solution.py:36
  161.7 85.0 %copy-start.19 = (bf16[128,2048]{1,0:T(8,128)(2,1)}, bf16[128,2048]{1,0:T(8,128)(2,1)S(1)}, u32[]{:S(2)}) copy-start(bf16[128,2048]{1,0:T(8,128)(2,1)S(1)} %get-tuple-element.18) | copy-start | bytes 1572868
  181.8 64.9 %copy-start.21 = (bf16[128,2048]{1,0:T(8,128)(2,1)}, bf16[128,2048]{1,0:T(8,128)(2,1)S(1)}, u32[]{:S(2)}) copy-start(bf16[128,2048]{1,0:T(8,128)(2,1)S(1)} %get-tuple-element.20) | copy-start | bytes 1572868
  186.0 60.7 %copy-start.23 = (bf16[128,2048]{1,0:T(8,128)(2,1)}, bf16[128,2048]{1,0:T(8,128)(2,1)S(1)}, u32[]{:S(2)}) copy-start(bf16[128,2048]{1,0:T(8,128)(2,1)S(1)} %get-tuple-element.22) | copy-start | bytes 1572868
  187.0 59.7 %copy-start.47 = (f32[512,192]{0,1:T(8,128)}, f32[512,192]{0,1:T(8,128)S(1)}, u32[]{:S(2)}) copy-start(f32[512,192]{0,1:T(8,128)S(1)} %fusion.55) | copy-start | bytes 1179652
  201.8 28.8 %copy-start.29 = (bf16[128,2048]{1,0:T(8,128)(2,1)}, bf16[128,2048]{1,0:T(8,128)(2,1)S(1)}, u32[]{:S(2)}) copy-start(bf16[128,2048]{1,0:T(8,128)(2,1)S(1)} %get-tuple-element.31) | copy-start | bytes 1572868
  201.8 30.8 %copy-start.25 = (bf16[128,2048]{1,0:T(8,128)(2,1)}, bf16[128,2048]{1,0:T(8,128)(2,1)S(1)}, u32[]{:S(2)}) copy-start(bf16[128,2048]{1,0:T(8,128)(2,1)S(1)} %get-tuple-element.30) | copy-start | bytes 1572868
  225.4 5.2 %copy-start.33 = (bf16[128,2048]{1,0:T(8,128)(2,1)}, bf16[128,2048]{1,0:T(8,128)(2,1)S(1)}, u32[]{:S(2)}) copy-start(bf16[128,2048]{1,0:T(8,128)(2,1)S(1)} %get-tuple-element.33) | copy-start | bytes 1572868
  225.4 7.2 %copy-start.27 = (bf16[128,2048]{1,0:T(8,128)(2,1)}, bf16[128,2048]{1,0:T(8,128)(2,1)S(1)}, u32[]{:S(2)}) copy-start(bf16[128,2048]{1,0:T(8,128)(2,1)S(1)} %get-tuple-element.32) | copy-start | bytes 1572868
  229.7 2.9 copy-start.31
  229.7 1.5 copy-start.2
  230.5 2.1 copy-start.51
  231.2 1.7 copy-start.4
  232.1 1.8 copy-start.53
  235.6 16.3 %collective-permute-start.5 = (bf16[128,2048]{1,0:T(8,128)(2,1)S(1)}, bf16[128,2048]{1,0:T(8,128)(2,1)S(1)}, u32[]{:S(2)}, u32[]{:S(2)}) collective-permute-start(bf16[128,2048]{1,0:T(8,128)(2,1)S(1)} %get-tuple-element.13), channel_id=1, source_target_pairs={{0,384},{128,0},{256,128},{384,256},{1,385},{129,1},{257,129},{385... | collective-permute-start | bytes 1572872 | tf_op jit(solution)/shard_map/ppermute | solution.py:43
  240.5 16.2 %collective-permute-start.6 = (bf16[128,2048]{1,0:T(8,128)(2,1)S(1)}, bf16[128,2048]{1,0:T(8,128)(2,1)S(1)}, u32[]{:S(2)}, u32[]{:S(2)}) collective-permute-start(bf16[128,2048]{1,0:T(8,128)(2,1)S(1)} %get-tuple-element.15), channel_id=1, source_target_pairs={{0,256},{128,384},{256,0},{384,128},{1,257},{129,385},{257,1},{385... | collective-permute-start | bytes 1572872 | tf_op jit(solution)/shard_map/ppermute | solution.py:43
  243.9 25.2 %collective-permute-start.7 = (bf16[128,2048]{1,0:T(8,128)(2,1)S(1)}, bf16[128,2048]{1,0:T(8,128)(2,1)S(1)}, u32[]{:S(2)}, u32[]{:S(2)}) collective-permute-start(bf16[128,2048]{1,0:T(8,128)(2,1)S(1)} %get-tuple-element.14), channel_id=1, source_target_pairs={{0,128},{128,256},{256,384},{384,0},{1,129},{129,257},{257,385},{3... | collective-permute-start | bytes 1572872 | tf_op jit(solution)/shard_map/ppermute | solution.py:43
  246.7 1.9 copy-start.49
  273.8 54.4 %all-to-all-start.1 = ((bf16[128,2,1024]{2,1,0:T(2,128)(2,1)}), bf16[128,2,1024]{2,1,0:T(2,128)(2,1)S(1)}, u32[]{:S(2)}, u32[]{:S(2)}) async-start(bf16[128,2,1024]{2,1,0:T(2,128)(2,1)} %reshape.198), calls=%async_computation.1 | async-start | bytes 1048576 | tf_op jit(solution)/shard_map/all_to_all | solution.py:160
  286.1 2.0 copy-start.10
  290.2 9.9 %copy-start.11 = (bf16[512,192]{0,1:T(8,128)(2,1)S(1)}, bf16[512,192]{0,1:T(8,128)(2,1)}, u32[]{:S(2)}) copy-start(bf16[512,192]{0,1:T(8,128)(2,1)} %get-tuple-element.36) | copy-start | bytes 589828
  291.4 14.8 %collective-permute-start.11 = (bf16[128,2048]{1,0:T(8,128)(2,1)}, bf16[128,2048]{1,0:T(8,128)(2,1)S(1)}, u32[]{:S(2)}, u32[]{:S(2)}) collective-permute-start(bf16[128,2048]{1,0:T(8,128)(2,1)} %get-tuple-element.10), channel_id=1, source_target_pairs={{0,384},{128,0},{256,128},{384,256},{1,385},{129,1},{257,129},{385... | collective-permute-start | bytes 1572872 | tf_op jit(solution)/shard_map/ppermute | solution.py:43
  293.6 16.1 %collective-permute-start.12 = (bf16[128,2048]{1,0:T(8,128)(2,1)}, bf16[128,2048]{1,0:T(8,128)(2,1)}, u32[]{:S(2)}, u32[]{:S(2)}) collective-permute-start(bf16[128,2048]{1,0:T(8,128)(2,1)} %get-tuple-element.12), channel_id=1, source_target_pairs={{0,256},{128,384},{256,0},{384,128},{1,257},{129,385},{257,1},{385... | collective-permute-start | bytes 1572872 | tf_op jit(solution)/shard_map/ppermute | solution.py:43
  297.0 25.4 %collective-permute-start.13 = (bf16[128,2048]{1,0:T(8,128)(2,1)}, bf16[128,2048]{1,0:T(8,128)(2,1)}, u32[]{:S(2)}, u32[]{:S(2)}) collective-permute-start(bf16[128,2048]{1,0:T(8,128)(2,1)} %get-tuple-element.11), channel_id=1, source_target_pairs={{0,128},{128,256},{256,384},{384,0},{1,129},{129,257},{257,385},{3... | collective-permute-start | bytes 1572872 | tf_op jit(solution)/shard_map/ppermute | solution.py:43
  306.2 3.5 copy-start.12
  324.2 20.3 %copy-start.6 = (bf16[512,192]{0,1:T(8,128)(2,1)S(1)}, bf16[512,192]{0,1:T(8,128)(2,1)}, u32[]{:S(2)}) copy-start(bf16[512,192]{0,1:T(8,128)(2,1)} %get-tuple-element.37) | copy-start | bytes 589828
  328.2 48.6 %all-to-all-start.3 = ((bf16[128,2,1024]{2,1,0:T(2,128)(2,1)}), bf16[128,2,1024]{2,1,0:T(2,128)(2,1)S(1)}, u32[]{:S(2)}, u32[]{:S(2)}) async-start(bf16[128,2,1024]{2,1,0:T(2,128)(2,1)} %reshape.200), calls=%async_computation.3 | async-start | bytes 1048576 | tf_op jit(solution)/shard_map/all_to_all | solution.py:160
  344.6 1.5 copy-start.18
  344.6 1.7 copy-start.30
  344.6 1.8 copy-start.34
  344.6 1.9 copy-start.36
  344.6 2.0 copy-start.40
  348.1 1.5 copy-start.16
  348.1 1.5 copy-start.20
  348.1 1.5 copy-start.22
  348.1 1.5 copy-start.24
  348.1 1.9 copy-start.48
  348.1 2.0 copy-start.50
  350.1 1.5 copy-start.32
  350.1 1.6 copy-start.52
  350.1 1.7 copy-start.54
  (10 other events, 11.2 us)
Sparse Core Ops, SparseCore 0:
  11.6 72.5 all-gather.1

commit v6 on v2

--- a/solution.py
+++ b/solution.py
@@ -104,7 +104,12 @@
     for chunk in range(capacity):
         both = jnp.stack([outgoing[:, chunk], cot_out[:, chunk]], axis=0)
         arrived = lax.all_to_all(both, "expert", split_axis=1, concat_axis=1, tiled=True)
-        gathered = lax.all_gather(arrived, "dp", axis=1, tiled=True)
+        if chunk == 0:
+            gathered = lax.all_gather(arrived, "dp", axis=1, tiled=True)
+        else:
+            spread = jnp.broadcast_to(arrived[None], (replicas,) + arrived.shape)
+            gathered = lax.all_to_all(spread, "dp", split_axis=0, concat_axis=0, tiled=True)
+            gathered = jnp.moveaxis(gathered, 0, 1).reshape(2, replicas * experts, features)
         row_grads, gate_grad, up_grad, down_grad = expert_work(
             gathered[0], gathered[1], w_gate, w_up, w_down
         )

time: 365 us -> 361 us (0.989)
  blocking collectives: 74.6 us -> 0 us
  waiting for transfers between devices: 172 us -> 208 us
  starting transfers between devices: 39.7 us -> 68.3 us
  local copies, waits for them, and re-layouts: 21.4 us -> 30.4 us
  matrix products: 28.9 us -> 25.2 us
    all_to_all x1 -> x0, blocking collectives: 74.6 us -> none  [on_device(): lax.all_to_all(both, 'expert', split_axis=1, concat_axis=1, tiled=True)]
    ppermute x2, waiting for transfers between devices: 46.4 us -> 0.21 us  [swapped(): return lax.ppermute(block, axis, route)]
    all_to_all x1 -> x2, waiting for transfers between devices: 51.8 us -> 97.1 us  [on_device(): lax.all_to_all(both, 'expert', split_axis=1, concat_axis=1, tiled=True)]
    all_to_all x0 -> x1, waiting for transfers between devices: none -> 34.2 us  [on_device(): lax.all_to_all(spread, 'dp', split_axis=0, concat_axis=0, tiled=True)]
    all_to_all x1 -> x2, starting transfers between devices: 8.4 us -> 29.2 us  [on_device(): lax.all_to_all(both, 'expert', split_axis=1, concat_axis=1, tiled=True)]
    all_to_all x0 -> x1, starting transfers between devices: none -> 5.03 us  [on_device(): lax.all_to_all(spread, 'dp', split_axis=0, concat_axis=0, tiled=True)]
    unnamed x75 -> x87, local copies, waits for them, and re-layouts: 10.2 us -> 12.3 us
  transfers between devices with their start and end apart: 9 -> 10, of which waited for: 6 -> 8; matrix products, arithmetic and copies ran while one was open for 14% -> 15% of each run, Pallas kernels for 0% -> 0%
where the time goes in v6:
time: 361 us; the launch traced here: 359 us
  waiting for transfers between devices  208 us (58%)
  starting transfers between devices  68.3 us (19%)
  local copies, waits for them, and re-layouts  30.4 us (8%)
  matrix products  25.2 us (7%)
  between operations  15.2 us (4%)
  other arithmetic  12.8 us (4%)
    all_to_all x2, waiting for transfers between devices, on_device(): lax.all_to_all(both, 'expert', split_axis=1, concat_axis=1, tiled=True)  97.1 us
    reduce_scatter x2, waiting for transfers between devices, on_device(): lax.psum_scatter(row_grads.reshape(replicas, experts, features), 'dp', sc...  45 us
    all_to_all x1, waiting for transfers between devices, on_device(): lax.all_to_all(spread, 'dp', split_axis=0, concat_axis=0, tiled=True)  34.2 us
    all_to_all x2, waiting for transfers between devices, on_device(): lax.all_to_all(summed_rows[0], 'expert', split_axis=0, concat_axis=0, til...  30.9 us
    all_to_all x2, starting transfers between devices, on_device(): lax.all_to_all(both, 'expert', split_axis=1, concat_axis=1, tiled=True)  29.2 us
    all_to_all x2, starting transfers between devices, on_device(): lax.all_to_all(summed_rows[0], 'expert', split_axis=0, concat_axis=0, til...  23.9 us
    dot_general x12, matrix products, contract(): lax.dot_general(left, right, (((left_dim,), (right_dim,)), ((), ())), pre...  16.3 us
    unnamed x87, local copies, waits for them, and re-layouts  12.3 us
  transfers between devices with their start and end apart: 10, of which 8 were waited for; matrix products, arithmetic and copies ran while one was open for 15% of the time, Pallas kernels for 0%

profile of v6, /device:TPU:1, one launch (start us, length us, event | category | flops | bytes accessed | tf_op | source)
XLA Modules:
  0.0 359.4 jit_solution(2296770397332257970)
XLA Ops:
  7.2 0.7 bitcast_convert_fusion
  7.9 0.8 copy.63
  8.8 1.6 gather_fusion
  11.4 0.7 select_reduce_fusion
  12.5 0.5 convolution_convert_fusion
  13.8 2.1 copy.73
  15.8 20.4 %all-to-all-start = ((bf16[2,128,2048]{2,0,1:T(2,128)(2,1)}), bf16[2,128,2048]{2,0,1:T(2,128)(2,1)S(1)}, u32[]{:S(2)}, u32[]{:S(2)}) async-start(bf16[2,128,2048]{2,0,1:T(2,128)(2,1)} %copy.73), calls=%async_computation | async-start | bytes 2097152 | tf_op jit(solution)/shard_map/all_to_all | solution.py:106
  36.3 2.1 copy.77
  38.4 52.2 %all-to-all-done = bf16[2,128,2048]{2,0,1:T(2,128)(2,1)S(1)} async-done(((bf16[2,128,2048]{2,0,1:T(2,128)(2,1)}), bf16[2,128,2048]{2,0,1:T(2,128)(2,1)S(1)}, u32[]{:S(2)}, u32[]{:S(2)}) %all-to-all-start) | async-done | bytes 1048608 | tf_op jit(solution)/shard_map/all_to_all | solution.py:106
  90.6 8.9 %all-to-all-start.2 = ((bf16[2,128,2048]{2,0,1:T(2,128)(2,1)}), bf16[2,128,2048]{2,0,1:T(2,128)(2,1)}, u32[]{:S(2)}, u32[]{:S(2)}) async-start(bf16[2,128,2048]{2,0,1:T(2,128)(2,1)} %copy.77), calls=%async_computation.3 | async-start | bytes 2097152 | tf_op jit(solution)/shard_map/all_to_all | solution.py:106
  99.5 1.3 constant_dynamic-update-slice_fusion.2
  100.8 1.2 constant_dynamic-update-slice_fusion.1
  102.1 5.1 %collective-permute-start = (bf16[3,192,2048]{2,1,0:T(8,128)(2,1)S(1)}, bf16[3,192,2048]{2,1,0:T(8,128)(2,1)}, u32[]{:S(2)}, u32[]{:S(2)}) collective-permute-start(bf16[3,192,2048]{2,1,0:T(8,128)(2,1)S(1)} %constant_dynamic-update-slice_fusion), channel_id=1, source_target_pairs={{0,64},{64,0},{1,65},{65,1},{2,66},{66,2},{3,67},{67,3},{4,68},{68... | collective-permute-start | bytes 7077896 | tf_op jit(solution)/shard_map/ppermute | solution.py:14
  107.2 1.4 copy.74
  108.6 45.0 %all-to-all-done.2 = bf16[2,128,2048]{2,0,1:T(2,128)(2,1)} async-done(((bf16[2,128,2048]{2,0,1:T(2,128)(2,1)}), bf16[2,128,2048]{2,0,1:T(2,128)(2,1)}, u32[]{:S(2)}, u32[]{:S(2)}) %all-to-all-start.2) | async-done | bytes 1048608 | tf_op jit(solution)/shard_map/all_to_all | solution.py:106
  153.5 1.6 copy.78
  155.1 2.5 broadcast_in_dim.57
  157.7 5.0 %all-to-all-start.3 = ((bf16[4,2,128,2048]{3,2,1,0:T(8,128)(2,1)}), bf16[4,2,128,2048]{3,2,1,0:T(8,128)(2,1)}, u32[]{:S(2)}, u32[]{:S(2)}) async-start(bf16[4,2,128,2048]{3,2,1,0:T(8,128)(2,1)} %broadcast_in_dim.57), calls=%async_computation.4 | async-start | bytes 8388608 | tf_op jit(solution)/shard_map/all_to_all | solution.py:111
  162.8 4.6 %collective-permute-start.1 = (f32[3,3,16]{2,0,1:T(4,128)S(1)}, f32[3,3,16]{2,0,1:T(4,128)S(1)}, u32[]{:S(2)}, u32[]{:S(2)}) collective-permute-start(f32[3,3,16]{2,0,1:T(4,128)S(1)} %pad_maximum_fusion.2), channel_id=1, source_target_pairs={{0,64},{64,0},{1,65},{65,1},{2,66},{66,2},{3,67},{67,3},{4,68},{68... | collective-permute-start | bytes 1736 | tf_op jit(solution)/shard_map/ppermute | solution.py:14
  167.5 0.6 fusion.53
  169.0 1.9 broadcast_select_fusion
  170.9 0.6 convert_bitcast_fusion.3
  172.4 0.5 fusion.15
  173.0 1.4 fusion.14
  174.4 1.4 fusion.16
  175.7 34.2 %all-to-all-done.3 = bf16[4,2,128,2048]{3,2,1,0:T(8,128)(2,1)} async-done(((bf16[4,2,128,2048]{3,2,1,0:T(8,128)(2,1)}), bf16[4,2,128,2048]{3,2,1,0:T(8,128)(2,1)}, u32[]{:S(2)}, u32[]{:S(2)}) %all-to-all-start.3) | async-done | bytes 4194336 | tf_op jit(solution)/shard_map/all_to_all | solution.py:111
  209.9 2.7 fusion.62
  212.7 0.8 fusion.24
  213.6 0.8 copy-done.20
  214.4 0.8 fusion.21
  215.3 0.9 multiply_convert_fusion.2
  216.3 0.5 broadcast_in_dim.56
  216.8 0.9 fusion.56
  217.9 0.5 broadcast_in_dim.54
  218.4 2.4 add_convert_fusion
  221.1 2.6 fusion.20
  224.0 2.1 fusion.19
  226.1 0.9 multiply_convert_fusion.4
  227.1 0.6 copy-done.8
  227.7 0.9 fusion.58
  228.6 0.5 copy-done.6
  229.1 2.4 add_convert_fusion.1
  231.5 25.4 %reduce-scatter.5.cloned.1.call-done = bf16[1,128,2048]{2,1,0:T(8,128)(2,1)} async-done(((bf16[4,128,2048]{2,1,0:T(8,128)(2,1)}), bf16[1,128,2048]{2,1,0:T(8,128)(2,1)}) %reduce-scatter.5.cloned.1.call-update) | async-done | bytes 524304 | tf_op jit(solution)/shard_map/reduce_scatter | solution.py:118
  257.0 0.5 broadcast.83
  257.5 2.0 reduce.3
  259.5 1.2 reshape.208
  260.7 16.8 %all-to-all-start.4 = ((bf16[128,2,1024]{2,1,0:T(2,128)(2,1)}), bf16[128,2,1024]{2,1,0:T(2,128)(2,1)S(1)}, u32[]{:S(2)}, u32[]{:S(2)}) async-start(bf16[128,2,1024]{2,1,0:T(2,128)(2,1)} %reshape.208), calls=%async_computation.6 | async-start | bytes 1048576 | tf_op jit(solution)/shard_map/all_to_all | solution.py:121
  277.5 19.6 %reduce-scatter.3.cloned.1.call-done = bf16[1,128,2048]{2,1,0:T(8,128)(2,1)} async-done(((bf16[4,128,2048]{2,1,0:T(8,128)(2,1)}), bf16[1,128,2048]{2,1,0:T(8,128)(2,1)}) %reduce-scatter.3.cloned.1.call-update) | async-done | bytes 524304 | tf_op jit(solution)/shard_map/reduce_scatter | solution.py:118
  297.0 2.0 reduce.2
  299.0 1.2 reshape.206
  300.2 10.4 %all-to-all-done.4 = bf16[128,2,1024]{2,1,0:T(2,128)(2,1)S(1)} async-done(((bf16[128,2,1024]{2,1,0:T(2,128)(2,1)}), bf16[128,2,1024]{2,1,0:T(2,128)(2,1)S(1)}, u32[]{:S(2)}, u32[]{:S(2)}) %all-to-all-start.4) | async-done | bytes 524320 | tf_op jit(solution)/shard_map/all_to_all | solution.py:121
  310.7 7.1 %all-to-all-start.1 = ((bf16[128,2,1024]{2,1,0:T(2,128)(2,1)}), bf16[128,2,1024]{2,1,0:T(2,128)(2,1)S(1)}, u32[]{:S(2)}, u32[]{:S(2)}) async-start(bf16[128,2,1024]{2,1,0:T(2,128)(2,1)} %reshape.206), calls=%async_computation.2 | async-start | bytes 1048576 | tf_op jit(solution)/shard_map/all_to_all | solution.py:121
  317.8 0.7 fusion.63
  318.6 0.9 copy.76
  319.6 2.3 fusion.18
  321.9 1.5 fusion.6
  323.4 1.0 copy-done.13
  324.4 0.6 fusion.17
  325.3 1.5 fusion.5
  326.8 0.6 fusion.8
  327.4 1.0 copy-done.10
  328.5 1.5 fusion.4
  330.5 20.5 %all-to-all-done.1 = bf16[128,2,1024]{2,1,0:T(2,128)(2,1)S(1)} async-done(((bf16[128,2,1024]{2,1,0:T(2,128)(2,1)}), bf16[128,2,1024]{2,1,0:T(2,128)(2,1)S(1)}, u32[]{:S(2)}, u32[]{:S(2)}) %all-to-all-start.1) | async-done | bytes 524320 | tf_op jit(solution)/shard_map/all_to_all | solution.py:121
  351.9 1.0 fusion.7
  (123 shorter events, 6.3 us)
Async XLA Ops:
  7.2 5.3 %copy-start = (bf16[24,2048]{1,0:T(8,128)(2,1)S(1)}, bf16[24,2048]{1,0:T(8,128)(2,1)}, u32[]{:S(2)}) copy-start(bf16[24,2048]{1,0:T(8,128)(2,1)} %param.11) | copy-start | bytes 294916
  7.2 1.6 copy-start.2
  10.4 2.6 copy-start.29
  12.4 0.6 copy-start.15
  15.8 74.8 %all-to-all-start = ((bf16[2,128,2048]{2,0,1:T(2,128)(2,1)}), bf16[2,128,2048]{2,0,1:T(2,128)(2,1)S(1)}, u32[]{:S(2)}, u32[]{:S(2)}) async-start(bf16[2,128,2048]{2,0,1:T(2,128)(2,1)} %copy.73), calls=%async_computation | async-start | bytes 2097152 | tf_op jit(solution)/shard_map/all_to_all | solution.py:106
  90.6 62.9 %all-to-all-start.2 = ((bf16[2,128,2048]{2,0,1:T(2,128)(2,1)}), bf16[2,128,2048]{2,0,1:T(2,128)(2,1)}, u32[]{:S(2)}, u32[]{:S(2)}) async-start(bf16[2,128,2048]{2,0,1:T(2,128)(2,1)} %copy.77), calls=%async_computation.3 | async-start | bytes 2097152 | tf_op jit(solution)/shard_map/all_to_all | solution.py:106
  99.5 121.6 %all-gather.2.cloned.1.call-start = ((), (), s32[]{:S(2)}) async-start(), calls=%async_computation.7 | async-start | bytes 5242880 | tf_op jit(solution)/shard_map/all_gather | solution.py:108
  99.5 2.5 copy-start.19
  102.1 53.0 %copy-start.11 = (bf16[3,192,2048]{2,1,0:T(8,128)(2,1)}, bf16[3,192,2048]{2,1,0:T(8,128)(2,1)S(1)}, u32[]{:S(2)}) copy-start(bf16[3,192,2048]{2,1,0:T(8,128)(2,1)S(1)} %constant_dynamic-update-slice_fusion) | copy-start | bytes 7077892
  102.1 66.9 %collective-permute-start = (bf16[3,192,2048]{2,1,0:T(8,128)(2,1)S(1)}, bf16[3,192,2048]{2,1,0:T(8,128)(2,1)}, u32[]{:S(2)}, u32[]{:S(2)}) collective-permute-start(bf16[3,192,2048]{2,1,0:T(8,128)(2,1)S(1)} %constant_dynamic-update-slice_fusion), channel_id=1, source_target_pairs={{0,64},{64,0},{1,65},{65,1},{2,66},{66,2},{3,67},{67,3},{4,68},{68... | collective-permute-start | bytes 7077896 | tf_op jit(solution)/shard_map/ppermute | solution.py:14
  157.7 5.1 %copy-start.30 = (f32[1,3,16]{2,0,1:T(1,128)S(1)}, f32[1,3,16]{2,0,1:T(1,128)}, u32[]{:S(2)}) copy-start(f32[1,3,16]{2,0,1:T(1,128)} %param.21) | copy-start | bytes 580
  157.7 5.1 %copy-start.31 = (f32[1,3,16]{2,0,1:T(1,128)S(1)}, f32[1,3,16]{2,0,1:T(1,128)}, u32[]{:S(2)}) copy-start(f32[1,3,16]{2,0,1:T(1,128)} %param.20) | copy-start | bytes 580
  157.7 5.1 %copy-start.32 = (f32[1,3,16]{2,0,1:T(1,128)S(1)}, f32[1,3,16]{2,0,1:T(1,128)}, u32[]{:S(2)}) copy-start(f32[1,3,16]{2,0,1:T(1,128)} %param.19) | copy-start | bytes 580
  157.7 52.3 %all-to-all-start.3 = ((bf16[4,2,128,2048]{3,2,1,0:T(8,128)(2,1)}), bf16[4,2,128,2048]{3,2,1,0:T(8,128)(2,1)}, u32[]{:S(2)}, u32[]{:S(2)}) async-start(bf16[4,2,128,2048]{3,2,1,0:T(8,128)(2,1)} %broadcast_in_dim.57), calls=%async_computation.4 | async-start | bytes 8388608 | tf_op jit(solution)/shard_map/all_to_all | solution.py:111
  162.7 94.2 %reduce-scatter.5.cloned.1.call-start = ((), (), s32[]{:S(2)}) async-start(), calls=%async_computation.9 | async-start | bytes 2621440 | tf_op jit(solution)/shard_map/reduce_scatter | solution.py:118
  162.8 6.1 %collective-permute-start.1 = (f32[3,3,16]{2,0,1:T(4,128)S(1)}, f32[3,3,16]{2,0,1:T(4,128)S(1)}, u32[]{:S(2)}, u32[]{:S(2)}) collective-permute-start(f32[3,3,16]{2,0,1:T(4,128)S(1)} %pad_maximum_fusion.2), channel_id=1, source_target_pairs={{0,64},{64,0},{1,65},{65,1},{2,66},{66,2},{3,67},{67,3},{4,68},{68... | collective-permute-start | bytes 1736 | tf_op jit(solution)/shard_map/ppermute | solution.py:14
  212.7 2.6 copy-start.3
  212.7 2.6 copy-start.9
  212.7 1.7 copy-start.20
  213.6 2.7 copy-start.25
  213.6 1.8 copy-start.21
  215.3 1.0 copy-start.27
  216.3 2.1 copy-start.17
  216.8 1.2 copy-start.7
  218.4 2.4 copy-start.5
  220.8 76.2 %reduce-scatter.3.cloned.1.call-start = ((), (), s32[]{:S(2)}) async-start(), calls=%async_computation.8 | async-start | bytes 2621440 | tf_op jit(solution)/shard_map/reduce_scatter | solution.py:118
  221.1 2.8 copy-start.12
  224.0 2.2 copy-start.33
  224.0 2.2 copy-start.22
  226.1 1.0 copy-start.35
  226.1 1.6 copy-start.8
  227.1 1.5 copy-start.14
  227.1 1.5 copy-start.23
  227.7 1.4 copy-start.6
  260.7 57.2 %copy-start.16 = (bf16[24,256]{0,1:T(8,128)(2,1)S(1)}, bf16[24,256]{0,1:T(8,128)(2,1)}, u32[]{:S(2)}) copy-start(bf16[24,256]{0,1:T(8,128)(2,1)} %copy-done.15) | copy-start | bytes 36868
  260.7 50.0 %all-to-all-start.4 = ((bf16[128,2,1024]{2,1,0:T(2,128)(2,1)}), bf16[128,2,1024]{2,1,0:T(2,128)(2,1)S(1)}, u32[]{:S(2)}, u32[]{:S(2)}) async-start(bf16[128,2,1024]{2,1,0:T(2,128)(2,1)} %reshape.208), calls=%async_computation.6 | async-start | bytes 1048576 | tf_op jit(solution)/shard_map/all_to_all | solution.py:121
  310.7 40.3 %all-to-all-start.1 = ((bf16[128,2,1024]{2,1,0:T(2,128)(2,1)}), bf16[128,2,1024]{2,1,0:T(2,128)(2,1)S(1)}, u32[]{:S(2)}, u32[]{:S(2)}) async-start(bf16[128,2,1024]{2,1,0:T(2,128)(2,1)} %reshape.206), calls=%async_computation.2 | async-start | bytes 1048576 | tf_op jit(solution)/shard_map/all_to_all | solution.py:121
  317.8 4.0 %copy-start.4 = (bf16[1,4,128,2048]{3,2,0,1:T(8,128)(2,1)S(1)}, bf16[1,4,128,2048]{3,2,0,1:T(8,128)(2,1)}, u32[]{:S(2)}) copy-start(bf16[1,4,128,2048]{3,2,0,1:T(8,128)(2,1)} %copy-done.3) | copy-start | bytes 6291460
  321.9 2.5 copy-start.13
  321.9 2.5 copy-start.24
  324.4 0.9 copy-start.18
  325.3 1.5 copy-start.34
  325.3 1.5 copy-start.36
  326.8 1.6 copy-start.10
  326.8 1.6 copy-start.26
  326.8 1.7 copy-start.28
  328.5 24.4 %copy-start.1 = (bf16[24,2048]{1,0:T(8,128)(2,1)S(1)}, bf16[24,2048]{1,0:T(8,128)(2,1)}, u32[]{:S(2)}) copy-start(bf16[24,2048]{1,0:T(8,128)(2,1)} %param.11) | copy-start | bytes 294916
Sparse Core Ops, SparseCore 0:
  108.7 54.5 all-gather.1
  221.0 35.9 reduce-scatter.4
  259.8 37.1 reduce-scatter.2

commit v7 on v2

--- a/solution.py
+++ b/solution.py
@@ -110,10 +110,11 @@
         )
         part = (gate_grad, up_grad, down_grad)
         sums = part if sums is None else tuple(a + b for a, b in zip(sums, part))
-        summed_rows = lax.psum_scatter(
-            row_grads.reshape(replicas, experts, features), "dp", scatter_dimension=0, tiled=True
+        pieces = lax.all_to_all(
+            row_grads.reshape(replicas, experts, features), "dp", split_axis=0, concat_axis=0, tiled=True
         )
-        returned = lax.all_to_all(summed_rows[0], "expert", split_axis=0, concat_axis=0, tiled=True)
+        summed_rows = jnp.sum(pieces.astype(jnp.float32), axis=0).astype(jnp.bfloat16)
+        returned = lax.all_to_all(summed_rows, "expert", split_axis=0, concat_axis=0, tiled=True)
         token_sum = token_sum + jnp.einsum(
             "re,ed->rd", dispatch[:, :, chunk], returned, preferred_element_type=jnp.float32
         )

time: 365 us -> 382 us (1.047)
  waiting for transfers between devices: 172 us -> 183 us
  starting transfers between devices: 39.7 us -> 45.6 us
    all_to_all x2 -> x4, waiting for transfers between devices: 32.5 us -> 84.7 us  [the longest x2 52.2 us: on_device(): lax.all_to_all(summed_rows, 'expert', split_axis=0, concat_axis=0, tiled=...]
    reduce_scatter x2 -> x0, waiting for transfers between devices: 41.7 us -> none  [on_device(): lax.psum_scatter(row_grads.reshape(replicas, experts, features), 'dp', sc...]
    all_to_all x2 -> x4, starting transfers between devices: 23.9 us -> 30.2 us  [the longest x2 21.8 us: on_device(): lax.all_to_all(summed_rows, 'expert', split_axis=0, concat_axis=0, tiled=...]
    unnamed x75 -> x83, local copies, waits for them, and re-layouts: 10.2 us -> 10.2 us
  transfers between devices with their start and end apart: 9 -> 9, of which waited for: 6 -> 6; matrix products, arithmetic and copies ran while one was open for 14% -> 13% of each run, Pallas kernels for 0% -> 0%
where the time goes in v7:
time: 382 us; the launch traced here: 381 us
  waiting for transfers between devices  183 us (48%)
  blocking collectives  74.6 us (20%)
  starting transfers between devices  45.6 us (12%)
  matrix products  28.8 us (8%)
  local copies, waits for them, and re-layouts  21.4 us (6%)
  between operations  15.5 us (4%)
  other arithmetic  12.4 us (3%)
    all_to_all x1, blocking collectives, on_device(): lax.all_to_all(both, 'expert', split_axis=1, concat_axis=1, tiled=True)  74.6 us
    all_to_all x2, waiting for transfers between devices, on_device(): lax.all_to_all(summed_rows, 'expert', split_axis=0, concat_axis=0, tiled=...  52.2 us
    all_to_all x1, waiting for transfers between devices, on_device(): lax.all_to_all(both, 'expert', split_axis=1, concat_axis=1, tiled=True)  51.8 us
    ppermute x2, waiting for transfers between devices, swapped(): return lax.ppermute(block, axis, route)  46.4 us
    all_to_all x2, waiting for transfers between devices, on_device(): lax.all_to_all(row_grads.reshape(replicas, experts, features), 'dp', spli...  32.5 us
    all_to_all x2, starting transfers between devices, on_device(): lax.all_to_all(summed_rows, 'expert', split_axis=0, concat_axis=0, tiled=...  21.8 us
    dot_general x12, matrix products, contract(): lax.dot_general(left, right, (((left_dim,), (right_dim,)), ((), ())), pre...  19.9 us
    unnamed x83, local copies, waits for them, and re-layouts  10.2 us
  transfers between devices with their start and end apart: 9, of which 6 were waited for; matrix products, arithmetic and copies ran while one was open for 13% of the time, Pallas kernels for 0%

profile of v7, /device:TPU:1, one launch (start us, length us, event | category | flops | bytes accessed | tf_op | source)
XLA Modules:
  0.0 381.2 jit_solution(13283050494027761139)
XLA Ops:
  7.3 0.8 copy.62
  8.1 1.6 gather_fusion
  11.0 0.7 select_reduce_fusion
  11.8 0.5 convolution_convert_fusion
  12.3 0.5 fusion
  13.1 1.1 copy.72
  14.2 74.6 %all_to_all.44 = bf16[2,128,2048]{2,0,1:T(2,128)(2,1)S(1)} all-to-all(bf16[2,128,2048]{2,0,1:T(2,128)(2,1)S(1)} %copy.72), channel_id=1, replica_groups=mesh['dp'=4,'expert'=128] {'expert'}, dimensions={1} | all-to-all | bytes 2097152 | tf_op jit(solution)/shard_map/all_to_all | solution.py:106
  88.7 1.3 copy.73
  90.2 2.1 copy.76
  92.3 8.4 %all-to-all-start.3 = ((bf16[2,128,2048]{2,0,1:T(2,128)(2,1)}), bf16[2,128,2048]{2,0,1:T(2,128)(2,1)S(1)}, u32[]{:S(2)}, u32[]{:S(2)}) async-start(bf16[2,128,2048]{2,0,1:T(2,128)(2,1)} %copy.76), calls=%async_computation.3 | async-start | bytes 2097152 | tf_op jit(solution)/shard_map/all_to_all | solution.py:106
  100.7 1.3 constant_dynamic-update-slice_fusion.2
  102.0 1.2 constant_dynamic-update-slice_fusion.1
  103.3 51.8 %all-to-all-done.3 = bf16[2,128,2048]{2,0,1:T(2,128)(2,1)S(1)} async-done(((bf16[2,128,2048]{2,0,1:T(2,128)(2,1)}), bf16[2,128,2048]{2,0,1:T(2,128)(2,1)S(1)}, u32[]{:S(2)}, u32[]{:S(2)}) %all-to-all-start.3) | async-done | bytes 1048608 | tf_op jit(solution)/shard_map/all_to_all | solution.py:106
  155.1 1.4 copy.77
  156.5 1.2 constant_dynamic-update-slice_fusion
  157.7 4.4 %collective-permute-start = (bf16[3,192,2048]{2,1,0:T(8,128)(2,1)S(1)}, bf16[3,192,2048]{2,1,0:T(8,128)(2,1)}, u32[]{:S(2)}, u32[]{:S(2)}) collective-permute-start(bf16[3,192,2048]{2,1,0:T(8,128)(2,1)S(1)} %constant_dynamic-update-slice_fusion), channel_id=1, source_target_pairs={{0,64},{64,0},{1,65},{65,1},{2,66},{66,2},{3,67},{67,3},{4,68},{68... | collective-permute-start | bytes 7077896 | tf_op jit(solution)/shard_map/ppermute | solution.py:14
  162.2 2.5 collective-permute-start.1
  164.7 0.6 fusion.53
  166.0 46.4 %collective-permute-done.1 = f32[3,3,16]{2,0,1:T(4,128)S(1)} collective-permute-done((f32[3,3,16]{2,0,1:T(4,128)S(1)}, f32[3,3,16]{2,0,1:T(4,128)S(1)}, u32[]{:S(2)}, u32[]{:S(2)}) %collective-permute-start.1) | collective-permute-done | bytes 608 | tf_op jit(solution)/shard_map/ppermute | solution.py:14
  212.5 1.9 broadcast_select_fusion
  214.4 0.6 convert_bitcast_fusion.3
  215.9 0.5 fusion.16
  216.4 1.4 fusion.15
  217.8 1.4 fusion.17
  219.2 2.6 fusion.21
  222.0 2.1 fusion.20
  224.1 0.9 multiply_convert_fusion.4
  225.0 0.5 broadcast_in_dim.50
  225.5 0.9 fusion.58
  226.7 0.5 broadcast_in_dim.48
  227.1 2.4 add_convert_fusion.1
  229.5 4.5 %all-to-all-start.1 = ((bf16[4,128,2048]{2,1,0:T(8,128)(2,1)}), bf16[4,128,2048]{2,1,0:T(8,128)(2,1)}, u32[]{:S(2)}, u32[]{:S(2)}) async-start(bf16[4,128,2048]{2,1,0:T(8,128)(2,1)} %bitcast.168), calls=%async_computation.1 | async-start | bytes 4194304 | tf_op jit(solution)/shard_map/all_to_all | solution.py:113
  234.1 2.8 fusion.22
  237.2 0.8 fusion.23
  238.0 0.4 copy-done.19
  238.4 0.9 multiply_convert_fusion.2
  239.4 0.6 copy-done.4
  240.0 0.9 fusion.56
  240.9 0.5 copy-done.6
  241.4 2.3 add_convert_fusion
  243.7 14.3 %all-to-all-done.1 = bf16[4,128,2048]{2,1,0:T(8,128)(2,1)} async-done(((bf16[4,128,2048]{2,1,0:T(8,128)(2,1)}), bf16[4,128,2048]{2,1,0:T(8,128)(2,1)}, u32[]{:S(2)}, u32[]{:S(2)}) %all-to-all-start.1) | async-done | bytes 2097184 | tf_op jit(solution)/shard_map/all_to_all | solution.py:113
  258.0 3.8 %all-to-all-start.4 = ((bf16[4,128,2048]{2,1,0:T(8,128)(2,1)}), bf16[4,128,2048]{2,1,0:T(8,128)(2,1)S(1)}, u32[]{:S(2)}, u32[]{:S(2)}) async-start(bf16[4,128,2048]{2,1,0:T(8,128)(2,1)} %bitcast.169), calls=%async_computation.4 | async-start | bytes 4194304 | tf_op jit(solution)/shard_map/all_to_all | solution.py:113
  261.9 2.0 reduce_sum.57
  263.9 0.5 broadcast.82
  264.4 0.9 reduce.4
  265.3 1.2 reshape.198
  266.5 18.2 %all-to-all-done.4 = bf16[4,128,2048]{2,1,0:T(8,128)(2,1)S(1)} async-done(((bf16[4,128,2048]{2,1,0:T(8,128)(2,1)}), bf16[4,128,2048]{2,1,0:T(8,128)(2,1)S(1)}, u32[]{:S(2)}, u32[]{:S(2)}) %all-to-all-start.4) | async-done | bytes 2097184 | tf_op jit(solution)/shard_map/all_to_all | solution.py:113
  284.7 14.5 %all-to-all-start.2 = ((bf16[128,2,1024]{2,1,0:T(2,128)(2,1)}), bf16[128,2,1024]{2,1,0:T(2,128)(2,1)S(1)}, u32[]{:S(2)}, u32[]{:S(2)}) async-start(bf16[128,2,1024]{2,1,0:T(2,128)(2,1)} %reshape.198), calls=%async_computation.2 | async-start | bytes 1048576 | tf_op jit(solution)/shard_map/all_to_all | solution.py:117
  299.5 0.4 reduce_sum.58
  300.0 0.9 reduce.5
  300.9 1.3 reshape.200
  302.2 30.3 %all-to-all-done.2 = bf16[128,2,1024]{2,1,0:T(2,128)(2,1)S(1)} async-done(((bf16[128,2,1024]{2,1,0:T(2,128)(2,1)}), bf16[128,2,1024]{2,1,0:T(2,128)(2,1)S(1)}, u32[]{:S(2)}, u32[]{:S(2)}) %all-to-all-start.2) | async-done | bytes 524320 | tf_op jit(solution)/shard_map/all_to_all | solution.py:117
  332.4 7.3 %all-to-all-start.5 = ((bf16[128,2,1024]{2,1,0:T(2,128)(2,1)}), bf16[128,2,1024]{2,1,0:T(2,128)(2,1)S(1)}, u32[]{:S(2)}, u32[]{:S(2)}) async-start(bf16[128,2,1024]{2,1,0:T(2,128)(2,1)} %reshape.200), calls=%async_computation.5 | async-start | bytes 1048576 | tf_op jit(solution)/shard_map/all_to_all | solution.py:117
  339.7 2.3 fusion.18
  342.1 3.2 fusion.5
  345.3 0.6 fusion.19
  346.0 1.5 fusion.6
  347.5 0.6 fusion.8
  348.6 1.5 fusion.4
  350.1 0.4 reshape.199
  350.6 0.4 fusion.38
  350.9 22.0 %all-to-all-done.5 = bf16[128,2,1024]{2,1,0:T(2,128)(2,1)S(1)} async-done(((bf16[128,2,1024]{2,1,0:T(2,128)(2,1)}), bf16[128,2,1024]{2,1,0:T(2,128)(2,1)S(1)}, u32[]{:S(2)}, u32[]{:S(2)}) %all-to-all-start.5) | async-done | bytes 524320 | tf_op jit(solution)/shard_map/all_to_all | solution.py:117
  372.9 0.4 reshape.201
  373.3 1.0 fusion.7
  (117 shorter events, 4.4 us)
Async XLA Ops:
  7.2 4.6 %copy-start = (bf16[24,2048]{1,0:T(8,128)(2,1)S(1)}, bf16[24,2048]{1,0:T(8,128)(2,1)}, u32[]{:S(2)}) copy-start(bf16[24,2048]{1,0:T(8,128)(2,1)} %param.11) | copy-start | bytes 294916
  7.2 0.9 copy-start.2
  7.2 212.0 %all-gather.3.cloned.1.call-start = ((), (), s32[]{:S(2)}) async-start(), calls=%async_computation.6 | async-start | bytes 5242880 | tf_op jit(solution)/shard_map/all_gather | solution.py:107
  8.1 2.9 copy-start.26
  9.7 2.6 copy-start.22
  10.8 1.5 copy-start.14
  92.3 62.8 %all-to-all-start.3 = ((bf16[2,128,2048]{2,0,1:T(2,128)(2,1)}), bf16[2,128,2048]{2,0,1:T(2,128)(2,1)S(1)}, u32[]{:S(2)}, u32[]{:S(2)}) async-start(bf16[2,128,2048]{2,0,1:T(2,128)(2,1)} %copy.76), calls=%async_computation.3 | async-start | bytes 2097152 | tf_op jit(solution)/shard_map/all_to_all | solution.py:106
  100.7 133.4 %all-gather.5.cloned.1.call-start = ((), (), s32[]{:S(2)}) async-start(), calls=%async_computation.7 | async-start | bytes 5242880 | tf_op jit(solution)/shard_map/all_gather | solution.py:107
  103.2 58.9 %copy-start.23 = (f32[1,3,16]{2,0,1:T(1,128)S(1)}, f32[1,3,16]{2,0,1:T(1,128)}, u32[]{:S(2)}) copy-start(f32[1,3,16]{2,0,1:T(1,128)} %param.21) | copy-start | bytes 580
  103.2 58.9 %copy-start.24 = (f32[1,3,16]{2,0,1:T(1,128)S(1)}, f32[1,3,16]{2,0,1:T(1,128)}, u32[]{:S(2)}) copy-start(f32[1,3,16]{2,0,1:T(1,128)} %param.20) | copy-start | bytes 580
  103.2 58.9 %copy-start.25 = (f32[1,3,16]{2,0,1:T(1,128)S(1)}, f32[1,3,16]{2,0,1:T(1,128)}, u32[]{:S(2)}) copy-start(f32[1,3,16]{2,0,1:T(1,128)} %param.19) | copy-start | bytes 580
  157.7 54.8 %copy-start.7 = (bf16[3,192,2048]{2,1,0:T(8,128)(2,1)}, bf16[3,192,2048]{2,1,0:T(8,128)(2,1)S(1)}, u32[]{:S(2)}) copy-start(bf16[3,192,2048]{2,1,0:T(8,128)(2,1)S(1)} %constant_dynamic-update-slice_fusion) | copy-start | bytes 7077892
  157.7 54.8 %collective-permute-start = (bf16[3,192,2048]{2,1,0:T(8,128)(2,1)S(1)}, bf16[3,192,2048]{2,1,0:T(8,128)(2,1)}, u32[]{:S(2)}, u32[]{:S(2)}) collective-permute-start(bf16[3,192,2048]{2,1,0:T(8,128)(2,1)S(1)} %constant_dynamic-update-slice_fusion), channel_id=1, source_target_pairs={{0,64},{64,0},{1,65},{65,1},{2,66},{66,2},{3,67},{67,3},{4,68},{68... | collective-permute-start | bytes 7077896 | tf_op jit(solution)/shard_map/ppermute | solution.py:14
  162.2 50.2 %collective-permute-start.1 = (f32[3,3,16]{2,0,1:T(4,128)S(1)}, f32[3,3,16]{2,0,1:T(4,128)S(1)}, u32[]{:S(2)}, u32[]{:S(2)}) collective-permute-start(f32[3,3,16]{2,0,1:T(4,128)S(1)} %pad_maximum_fusion.2), channel_id=1, source_target_pairs={{0,64},{64,0},{1,65},{65,1},{2,66},{66,2},{3,67},{67,3},{4,68},{68... | collective-permute-start | bytes 1736 | tf_op jit(solution)/shard_map/ppermute | solution.py:14
  219.2 2.8 copy-start.10
  221.8 2.3 copy-start.31
  222.0 2.1 copy-start.18
  224.0 1.0 copy-start.33
  225.0 1.4 copy-start.12
  225.0 2.1 copy-start.20
  225.5 1.2 copy-start.3
  227.1 2.4 copy-start.5
  229.5 28.5 %all-to-all-start.1 = ((bf16[4,128,2048]{2,1,0:T(8,128)(2,1)}), bf16[4,128,2048]{2,1,0:T(8,128)(2,1)}, u32[]{:S(2)}, u32[]{:S(2)}) async-start(bf16[4,128,2048]{2,1,0:T(8,128)(2,1)} %bitcast.168), calls=%async_computation.1 | async-start | bytes 4194304 | tf_op jit(solution)/shard_map/all_to_all | solution.py:113
  234.1 3.1 copy-start.8
  237.1 0.9 copy-start.27
  237.2 1.3 copy-start.19
  238.4 0.9 copy-start.29
  238.4 1.5 copy-start.4
  239.4 1.5 copy-start.16
  240.0 1.4 copy-start.6
  258.0 26.6 %all-to-all-start.4 = ((bf16[4,128,2048]{2,1,0:T(8,128)(2,1)}), bf16[4,128,2048]{2,1,0:T(8,128)(2,1)S(1)}, u32[]{:S(2)}, u32[]{:S(2)}) async-start(bf16[4,128,2048]{2,1,0:T(8,128)(2,1)} %bitcast.169), calls=%async_computation.4 | async-start | bytes 4194304 | tf_op jit(solution)/shard_map/all_to_all | solution.py:113
  263.9 35.3 %copy-start.15 = (bf16[24,256]{0,1:T(8,128)(2,1)S(1)}, bf16[24,256]{0,1:T(8,128)(2,1)}, u32[]{:S(2)}) copy-start(bf16[24,256]{0,1:T(8,128)(2,1)} %copy-done.14) | copy-start | bytes 36868
  284.7 47.8 %all-to-all-start.2 = ((bf16[128,2,1024]{2,1,0:T(2,128)(2,1)}), bf16[128,2,1024]{2,1,0:T(2,128)(2,1)S(1)}, u32[]{:S(2)}, u32[]{:S(2)}) async-start(bf16[128,2,1024]{2,1,0:T(2,128)(2,1)} %reshape.198), calls=%async_computation.2 | async-start | bytes 1048576 | tf_op jit(solution)/shard_map/all_to_all | solution.py:117
  300.0 39.8 %copy-start.21 = (bf16[512,192]{0,1:T(8,128)(2,1)S(1)}, bf16[512,192]{0,1:T(8,128)(2,1)}, u32[]{:S(2)}) copy-start(bf16[512,192]{0,1:T(8,128)(2,1)} %copy-done.20) | copy-start | bytes 589828
  332.4 9.6 %copy-start.17 = (bf16[512,192]{0,1:T(8,128)(2,1)S(1)}, bf16[512,192]{0,1:T(8,128)(2,1)}, u32[]{:S(2)}) copy-start(bf16[512,192]{0,1:T(8,128)(2,1)} %copy-done.16) | copy-start | bytes 589828
  332.4 40.5 %all-to-all-start.5 = ((bf16[128,2,1024]{2,1,0:T(2,128)(2,1)}), bf16[128,2,1024]{2,1,0:T(2,128)(2,1)S(1)}, u32[]{:S(2)}, u32[]{:S(2)}) async-start(bf16[128,2,1024]{2,1,0:T(2,128)(2,1)} %reshape.200), calls=%async_computation.5 | async-start | bytes 1048576 | tf_op jit(solution)/shard_map/all_to_all | solution.py:117
  339.7 5.6 %copy-start.11 = (bf16[2,512,2048]{2,1,0:T(8,128)(2,1)S(1)}, bf16[2,512,2048]{2,1,0:T(8,128)(2,1)}, u32[]{:S(2)}) copy-start(bf16[2,512,2048]{2,1,0:T(8,128)(2,1)} %all-gather.3.cloned.1.call-done) | copy-start | bytes 12582916
  339.7 5.6 %copy-start.13 = (bf16[512,192]{0,1:T(8,128)(2,1)S(1)}, bf16[512,192]{0,1:T(8,128)(2,1)}, u32[]{:S(2)}) copy-start(bf16[512,192]{0,1:T(8,128)(2,1)} %copy-done.12) | copy-start | bytes 589828
  342.1 3.9 %copy-start.9 = (bf16[2,512,2048]{2,1,0:T(8,128)(2,1)S(1)}, bf16[2,512,2048]{2,1,0:T(8,128)(2,1)}, u32[]{:S(2)}) copy-start(bf16[2,512,2048]{2,1,0:T(8,128)(2,1)} %all-gather.5.cloned.1.call-done) | copy-start | bytes 12582916
  346.0 1.5 copy-start.32
  346.0 1.5 copy-start.34
  347.5 1.0 copy-start.28
  347.5 1.1 copy-start.30
  348.6 25.8 %copy-start.1 = (bf16[24,2048]{1,0:T(8,128)(2,1)S(1)}, bf16[24,2048]{1,0:T(8,128)(2,1)}, u32[]{:S(2)}) copy-start(bf16[24,2048]{1,0:T(8,128)(2,1)} %param.11) | copy-start | bytes 294916
Sparse Core Ops, SparseCore 0:
  90.2 49.0 all-gather.2
  156.6 49.0 all-gather.4

commit v8 on v4

--- a/solution.py
+++ b/solution.py
@@ -97,6 +97,15 @@
     dispatch = jnp.any(position[..., None] == slots, axis=1).astype(jnp.bfloat16).reshape(
         tok_count, experts, capacity
     )
+    gate_pick = jnp.sum(
+        jnp.where(position[..., None] == slots, gates[..., None], jnp.zeros((), gates.dtype)), axis=1
+    ).reshape(tok_count, experts, capacity)
+    first_tok = jnp.einsum(
+        "re,rd->ed", dispatch[:, :, 0], tokens, preferred_element_type=jnp.float32
+    ).astype(jnp.bfloat16)
+    first_cot = jnp.einsum(
+        "re,rd->ed", gate_pick[:, :, 0], cotangent, preferred_element_type=jnp.float32
+    ).astype(jnp.bfloat16)
     pad = jnp.zeros((tok_count, 128 - 2 * position.shape[1]), jnp.bfloat16)
     packed = jnp.concatenate(
         [tokens, cotangent, position.astype(jnp.bfloat16), gates, pad], axis=1
@@ -107,32 +116,40 @@
     ring_gates = ring_rows[:, 2 * features + top:2 * features + 2 * top]
     my_z = lax.axis_index("ez")
     target = (
-        ((jnp.arange(n_x, dtype=jnp.int32)[:, None, None] * n_z + my_z) * n_c
-         + jnp.arange(n_c, dtype=jnp.int32)[None, :, None]) * capacity
-        + jnp.arange(capacity, dtype=jnp.int32)
-    )
-    match = ring_position[:, :, None, None, None] == target
-    picked = jnp.any(match, axis=1).astype(jnp.bfloat16).reshape(n_z, tok_count, n_x, n_c, capacity)
+        (jnp.arange(n_x, dtype=jnp.int32)[:, None] * n_z + my_z) * n_c
+        + jnp.arange(n_c, dtype=jnp.int32)
+    ) * capacity + 1
+    match = ring_position[:, :, None, None] == target
+    picked = jnp.any(match, axis=1).astype(jnp.bfloat16).reshape(n_z, tok_count, n_x, n_c)
     picked_gate = jnp.sum(
-        jnp.where(match, ring_gates[:, :, None, None, None], jnp.zeros((), ring_gates.dtype)), axis=1
-    ).reshape(n_z, tok_count, n_x, n_c, capacity)
+        jnp.where(match, ring_gates[:, :, None, None], jnp.zeros((), ring_gates.dtype)), axis=1
+    ).reshape(n_z, tok_count, n_x, n_c)
     ring_rows = ring_rows.reshape(n_z, tok_count, ring_rows.shape[-1])
     relay_tok = jnp.einsum(
-        "zrxcs,zrd->sxczd", picked, ring_rows[:, :, :features], preferred_element_type=jnp.float32
-    ).astype(jnp.bfloat16).reshape(capacity, n_x * n_c, n_z, features)
+        "zrxc,zrd->xczd", picked, ring_rows[:, :, :features], preferred_element_type=jnp.float32
+    ).astype(jnp.bfloat16).reshape(n_x * n_c, n_z, features)
     relay_cot = jnp.einsum(
-        "zrxcs,zrd->sxczd", picked_gate, ring_rows[:, :, features:2 * features],
+        "zrxc,zrd->xczd", picked_gate, ring_rows[:, :, features:2 * features],
         preferred_element_type=jnp.float32,
-    ).astype(jnp.bfloat16).reshape(capacity, n_x * n_c, n_z, features)
-    dispatch = dispatch.reshape(tok_count, n_x, n_z, n_c, capacity).transpose(0, 1, 3, 2, 4).reshape(
-        tok_count, experts, capacity
+    ).astype(jnp.bfloat16).reshape(n_x * n_c, n_z, features)
+    relay_tok, relay_cot, w_gate, w_up, w_down = lax.optimization_barrier(
+        (relay_tok, relay_cot, w_gate, w_up, w_down)
+    )
+    dispatch_relay = dispatch[:, :, 1].reshape(tok_count, n_x, n_z, n_c).transpose(0, 1, 3, 2).reshape(
+        tok_count, experts
     )
 
     token_sum = jnp.zeros((tok_count, features), jnp.float32)
     sums = None
     for chunk in range(capacity):
-        both = jnp.stack([relay_tok[chunk], relay_cot[chunk]], axis=0)
-        arrived = lax.all_to_all(both, ("ex", "ec"), split_axis=1, concat_axis=1, tiled=True)
+        if chunk == 0:
+            both = jnp.stack([first_tok, first_cot], axis=0)
+            arrived = lax.all_to_all(both, EXPERT_AXES, split_axis=1, concat_axis=1, tiled=True)
+            back_axes, back_dispatch = EXPERT_AXES, dispatch[:, :, 0]
+        else:
+            both = jnp.stack([relay_tok, relay_cot], axis=0)
+            arrived = lax.all_to_all(both, ("ex", "ec"), split_axis=1, concat_axis=1, tiled=True)
+            back_axes, back_dispatch = ("ex", "ec", "ez"), dispatch_relay
         arrived = arrived.reshape(2, experts, features)
         gathered = lax.all_gather(arrived, "dp", axis=1, tiled=True)
         row_grads, gate_grad, up_grad, down_grad = expert_work(
@@ -143,11 +160,9 @@
         summed_rows = lax.psum_scatter(
             row_grads.reshape(replicas, experts, features), "dp", scatter_dimension=0, tiled=True
         )
-        returned = lax.all_to_all(
-            summed_rows[0], ("ex", "ec", "ez"), split_axis=0, concat_axis=0, tiled=True
-        )
+        returned = lax.all_to_all(summed_rows[0], back_axes, split_axis=0, concat_axis=0, tiled=True)
         token_sum = token_sum + jnp.einsum(
-            "re,ed->rd", dispatch[:, :, chunk], returned, preferred_element_type=jnp.float32
+            "re,ed->rd", back_dispatch, returned, preferred_element_type=jnp.float32
         )
     token_grads = token_sum.astype(jnp.bfloat16)
     gate_grad, up_grad, down_grad = (x.astype(jnp.bfloat16) for x in sums)

time: 373 us -> 384 us (1.029)
  starting transfers between devices: 36.2 us -> 51.6 us
  waiting for transfers between devices: 226 us -> 235 us
  blocking collectives: 28.6 us -> 21.8 us
    all_gather x1, waiting for transfers between devices: 72 us -> 0.02 us  [on_device(): ring_rows = lax.all_gather(packed, 'ez', axis=0, tiled=True)]
    all_to_all x3, waiting for transfers between devices: 43.3 us -> 96.1 us  [the longest x1 65.6 us: on_device(): lax.all_to_all(both, EXPERT_AXES, split_axis=1, concat_axis=1, tiled=True)]
    all_gather x2, waiting for transfers between devices: 13.2 us -> 39.3 us  [on_device(): gathered = lax.all_gather(arrived, 'dp', axis=1, tiled=True)]
    all_to_all x3, starting transfers between devices: 28.9 us -> 44.2 us  [the longest x2 23.8 us: on_device(): lax.all_to_all(summed_rows[0], back_axes, split_axis=0, concat_axis=0, ti...]
    all_to_all x1, blocking collectives: 28.6 us -> 21.8 us  [on_device(): lax.all_to_all(both, ('ex', 'ec'), split_axis=1, concat_axis=1, tiled=True)]
    unnamed x71 -> x52, local copies, waits for them, and re-layouts: 10.3 us -> 8.73 us
  transfers between devices with their start and end apart: 10 -> 10, of which waited for: 8 -> 7; matrix products, arithmetic and copies ran while one was open for 13% -> 14% of each run, Pallas kernels for 0% -> 0%
where the time goes in v8:
time: 384 us; the launch traced here: 383 us
  waiting for transfers between devices  235 us (61%)
  starting transfers between devices  51.6 us (13%)
  matrix products  30.1 us (8%)
  blocking collectives  21.8 us (6%)
  local copies, waits for them, and re-layouts  20.7 us (5%)
  between operations  15.1 us (4%)
  other arithmetic  9.02 us (2%)
    all_to_all x1, waiting for transfers between devices, on_device(): lax.all_to_all(both, EXPERT_AXES, split_axis=1, concat_axis=1, tiled=True)  65.6 us
    reduce_scatter x2, waiting for transfers between devices, on_device(): lax.psum_scatter(row_grads.reshape(replicas, experts, features), 'dp', sc...  52.5 us
    ppermute x2, waiting for transfers between devices, swapped(): return lax.ppermute(block, axis, route)  47 us
    all_gather x2, waiting for transfers between devices, on_device(): gathered = lax.all_gather(arrived, 'dp', axis=1, tiled=True)  39.3 us
    all_to_all x2, waiting for transfers between devices, on_device(): lax.all_to_all(summed_rows[0], back_axes, split_axis=0, concat_axis=0, ti...  30.6 us
    all_to_all x2, starting transfers between devices, on_device(): lax.all_to_all(summed_rows[0], back_axes, split_axis=0, concat_axis=0, ti...  23.8 us
    all_to_all x1, blocking collectives, on_device(): lax.all_to_all(both, ('ex', 'ec'), split_axis=1, concat_axis=1, tiled=True)  21.8 us
    all_to_all x1, starting transfers between devices, on_device(): lax.all_to_all(both, EXPERT_AXES, split_axis=1, concat_axis=1, tiled=True)  20.4 us
  transfers between devices with their start and end apart: 10, of which 7 were waited for; matrix products, arithmetic and copies ran while one was open for 14% of the time, Pallas kernels for 0%

profile of v8, /device:TPU:1, one launch (start us, length us, event | category | flops | bytes accessed | tf_op | source)
XLA Modules:
  0.0 383.4 jit_solution(1843240284090528320)
XLA Ops:
  7.2 0.8 copy.149
  8.1 1.6 gather_fusion
  10.6 0.8 concatenate.9
  11.8 0.3 slice_reduce_fusion
  12.5 0.4 fusion.6
  12.9 0.3 fusion.9
  13.3 2.1 copy.159
  15.4 20.4 %all-to-all-start = ((bf16[2,128,2048]{2,0,1:T(2,128)(2,1)}), bf16[2,128,2048]{2,0,1:T(2,128)(2,1)S(1)}, u32[]{:S(2)}, u32[]{:S(2)}) async-start(bf16[2,128,2048]{2,0,1:T(2,128)(2,1)} %copy.159), calls=%async_computation | async-start | bytes 2097152 | tf_op jit(solution)/shard_map/all_to_all | solution.py:147
  35.8 1.2 constant_dynamic-update-slice_fusion.2
  37.0 65.6 %all-to-all-done = bf16[2,128,2048]{2,0,1:T(2,128)(2,1)S(1)} async-done(((bf16[2,128,2048]{2,0,1:T(2,128)(2,1)}), bf16[2,128,2048]{2,0,1:T(2,128)(2,1)S(1)}, u32[]{:S(2)}, u32[]{:S(2)}) %all-to-all-start) | async-done | bytes 1048608 | tf_op jit(solution)/shard_map/all_to_all | solution.py:147
  102.6 1.4 copy.160
  104.0 1.2 constant_dynamic-update-slice_fusion.1
  105.4 3.9 %collective-permute-start = (bf16[3,192,2048]{2,1,0:T(8,128)(2,1)S(1)}, bf16[3,192,2048]{2,1,0:T(8,128)(2,1)}, u32[]{:S(2)}, u32[]{:S(2)}) collective-permute-start(bf16[3,192,2048]{2,1,0:T(8,128)(2,1)S(1)} %constant_dynamic-update-slice_fusion), channel_id=1, source_target_pairs={{0,64},{64,0},{1,65},{65,1},{2,66},{66,2},{3,67},{67,3},{4,68},{68... | collective-permute-start | bytes 7077896 | tf_op jit(solution)/shard_map/ppermute | solution.py:17
  109.4 3.0 collective-permute-start.1
  112.5 0.6 fusion.45
  113.8 47.0 %collective-permute-done.1 = f32[3,3,16]{2,0,1:T(4,128)S(1)} collective-permute-done((f32[3,3,16]{2,0,1:T(4,128)S(1)}, f32[3,3,16]{2,0,1:T(4,128)S(1)}, u32[]{:S(2)}, u32[]{:S(2)}) %collective-permute-start.1) | collective-permute-done | bytes 608 | tf_op jit(solution)/shard_map/ppermute | solution.py:17
  160.8 0.3 broadcast_select_fusion
  161.2 0.5 broadcast_in_dim.86
  161.7 0.5 broadcast_in_dim.88
  162.2 0.5 broadcast_in_dim.84
  162.6 2.7 fusion.14
  165.3 1.1 fusion.49
  166.8 1.9 fusion.8
  168.6 0.3 copy.168
  169.2 1.9 fusion.7
  171.0 0.3 copy.165
  171.6 21.8 %all_to_all.34 = bf16[2,8,16,2048]{3,2,0,1:T(8,128)(2,1)S(1)} all-to-all(bf16[2,8,16,2048]{3,2,0,1:T(8,128)(2,1)S(1)} %copy.171), channel_id=1, replica_groups=mesh['dp'=4,'ex'=4,'ez'=16,'ec'=2] {'ex','ec'}, dimensions={1} | all-to-all | bytes 2097152 | tf_op jit(solution)/shard_map/all_to_all | solution.py:151
  193.4 1.0 copy.172
  194.5 2.6 fusion.20
  197.1 0.2 copy-done.3
  197.3 0.9 fusion.19
  198.3 1.0 multiply_convert_fusion.4
  199.2 0.7 fusion.51
  200.0 2.1 add_convert_fusion.1
  202.1 0.3 reduce-scatter.5.cloned.1.call-start
  202.4 39.3 %all-gather.8.cloned.1.call-done = bf16[2,512,2048]{2,1,0:T(8,128)(2,1)} async-done(((bf16[2,128,2048]{2,1,0:T(8,128)(2,1)}), bf16[2,512,2048]{2,1,0:T(8,128)(2,1)}) %all-gather.8.cloned.1.call-update) | async-done | bytes 4194320 | tf_op jit(solution)/shard_map/all_gather | solution.py:154
  241.7 2.6 fusion.22
  244.3 0.2 copy-done.1
  244.5 0.9 fusion.21
  245.4 1.0 multiply_convert_fusion.2
  246.4 0.7 fusion.52
  247.1 2.1 add_convert_fusion
  249.2 33.1 %reduce-scatter.3.cloned.1.call-done = bf16[1,128,2048]{2,1,0:T(8,128)(2,1)} async-done(((bf16[4,128,2048]{2,1,0:T(8,128)(2,1)}), bf16[1,128,2048]{2,1,0:T(8,128)(2,1)}) %reduce-scatter.3.cloned.1.call-update) | async-done | bytes 524304 | tf_op jit(solution)/shard_map/reduce_scatter | solution.py:160
  282.3 0.5 broadcast.116
  282.8 2.0 reduce.4
  284.8 1.2 reshape.182
  286.0 16.7 %all-to-all-start.1 = ((bf16[128,2,1024]{2,1,0:T(2,128)(2,1)}), bf16[128,2,1024]{2,1,0:T(2,128)(2,1)S(1)}, u32[]{:S(2)}, u32[]{:S(2)}) async-start(bf16[128,2,1024]{2,1,0:T(2,128)(2,1)} %reshape.182), calls=%async_computation.2 | async-start | bytes 1048576 | tf_op jit(solution)/shard_map/all_to_all | solution.py:163
  302.8 19.5 %reduce-scatter.5.cloned.1.call-done = bf16[1,128,2048]{2,1,0:T(8,128)(2,1)} async-done(((bf16[4,128,2048]{2,1,0:T(8,128)(2,1)}), bf16[1,128,2048]{2,1,0:T(8,128)(2,1)}) %reduce-scatter.5.cloned.1.call-update) | async-done | bytes 524304 | tf_op jit(solution)/shard_map/reduce_scatter | solution.py:160
  322.2 2.0 reduce.5
  324.2 1.2 reshape.184
  325.4 10.5 %all-to-all-done.1 = bf16[128,2,1024]{2,1,0:T(2,128)(2,1)S(1)} async-done(((bf16[128,2,1024]{2,1,0:T(2,128)(2,1)}), bf16[128,2,1024]{2,1,0:T(2,128)(2,1)S(1)}, u32[]{:S(2)}, u32[]{:S(2)}) %all-to-all-start.1) | async-done | bytes 524320 | tf_op jit(solution)/shard_map/all_to_all | solution.py:163
  335.9 7.2 %all-to-all-start.3 = ((bf16[128,2,1024]{2,1,0:T(2,128)(2,1)}), bf16[128,2,1024]{2,1,0:T(2,128)(2,1)S(1)}, u32[]{:S(2)}, u32[]{:S(2)}) async-start(bf16[128,2,1024]{2,1,0:T(2,128)(2,1)} %reshape.184), calls=%async_computation.5 | async-start | bytes 1048576 | tf_op jit(solution)/shard_map/all_to_all | solution.py:163
  343.1 2.3 fusion.17
  345.4 2.2 fusion.18
  347.7 0.6 fusion.11
  348.3 1.6 copy-done.2
  349.9 1.5 fusion.4
  351.4 1.5 fusion.5
  352.9 1.5 fusion.3
  354.4 0.4 reshape.183
  354.9 0.4 fusion.25
  355.3 20.1 %all-to-all-done.3 = bf16[128,2,1024]{2,1,0:T(2,128)(2,1)S(1)} async-done(((bf16[128,2,1024]{2,1,0:T(2,128)(2,1)}), bf16[128,2,1024]{2,1,0:T(2,128)(2,1)S(1)}, u32[]{:S(2)}, u32[]{:S(2)}) %all-to-all-start.3) | async-done | bytes 524320 | tf_op jit(solution)/shard_map/all_to_all | solution.py:163
  375.3 0.4 reshape.185
  375.8 1.0 fusion.10
  (99 shorter events, 3.4 us)
Async XLA Ops:
  7.2 0.9 copy-start
  7.2 158.1 %all-gather.6.cloned.1.call-start = ((), (), s32[]{:S(2)}) async-start(), calls=%async_computation.7 | async-start | bytes 3446784 | tf_op jit(solution)/shard_map/all_gather | solution.py:113
  8.1 2.4 copy-start.11
  8.1 2.5 copy-start.6
  8.1 2.5 copy-start.7
  15.4 87.2 %all-to-all-start = ((bf16[2,128,2048]{2,0,1:T(2,128)(2,1)}), bf16[2,128,2048]{2,0,1:T(2,128)(2,1)S(1)}, u32[]{:S(2)}, u32[]{:S(2)}) async-start(bf16[2,128,2048]{2,0,1:T(2,128)(2,1)} %copy.159), calls=%async_computation | async-start | bytes 2097152 | tf_op jit(solution)/shard_map/all_to_all | solution.py:147
  35.8 158.7 %all-gather.4.cloned.1.call-start = ((), (), s32[]{:S(2)}) async-start(), calls=%async_computation.6 | async-start | bytes 5242880 | tf_op jit(solution)/shard_map/all_gather | solution.py:154
  103.9 1.4 copy-start.5
  104.0 5.4 %copy-start.8 = (f32[1,3,16]{2,0,1:T(1,128)S(1)}, f32[1,3,16]{2,0,1:T(1,128)}, u32[]{:S(2)}) copy-start(f32[1,3,16]{2,0,1:T(1,128)} %param.21) | copy-start | bytes 580
  104.0 5.4 %copy-start.9 = (f32[1,3,16]{2,0,1:T(1,128)S(1)}, f32[1,3,16]{2,0,1:T(1,128)}, u32[]{:S(2)}) copy-start(f32[1,3,16]{2,0,1:T(1,128)} %param.20) | copy-start | bytes 580
  104.0 5.4 %copy-start.10 = (f32[1,3,16]{2,0,1:T(1,128)S(1)}, f32[1,3,16]{2,0,1:T(1,128)}, u32[]{:S(2)}) copy-start(f32[1,3,16]{2,0,1:T(1,128)} %param.19) | copy-start | bytes 580
  104.0 137.7 %all-gather.8.cloned.1.call-start = ((), (), s32[]{:S(2)}) async-start(), calls=%async_computation.9 | async-start | bytes 5242880 | tf_op jit(solution)/shard_map/all_gather | solution.py:154
  105.4 55.4 %collective-permute-start = (bf16[3,192,2048]{2,1,0:T(8,128)(2,1)S(1)}, bf16[3,192,2048]{2,1,0:T(8,128)(2,1)}, u32[]{:S(2)}, u32[]{:S(2)}) collective-permute-start(bf16[3,192,2048]{2,1,0:T(8,128)(2,1)S(1)} %constant_dynamic-update-slice_fusion), channel_id=1, source_target_pairs={{0,64},{64,0},{1,65},{65,1},{2,66},{66,2},{3,67},{67,3},{4,68},{68... | collective-permute-start | bytes 7077896 | tf_op jit(solution)/shard_map/ppermute | solution.py:17
  109.4 51.4 %collective-permute-start.1 = (f32[3,3,16]{2,0,1:T(4,128)S(1)}, f32[3,3,16]{2,0,1:T(4,128)S(1)}, u32[]{:S(2)}, u32[]{:S(2)}) collective-permute-start(f32[3,3,16]{2,0,1:T(4,128)S(1)} %pad_maximum_fusion.2), channel_id=1, source_target_pairs={{0,64},{64,0},{1,65},{65,1},{2,66},{66,2},{3,67},{67,3},{4,68},{68... | collective-permute-start | bytes 1736 | tf_op jit(solution)/shard_map/ppermute | solution.py:17
  194.4 87.9 %reduce-scatter.3.cloned.1.call-start = ((), (), s32[]{:S(2)}) async-start(), calls=%async_computation.8 | async-start | bytes 2621440 | tf_op jit(solution)/shard_map/reduce_scatter | solution.py:160
  194.5 2.8 copy-start.3
  197.3 0.9 copy-start.16
  198.2 1.0 copy-start.18
  202.1 120.1 %reduce-scatter.5.cloned.1.call-start = ((), (), s32[]{:S(2)}) async-start(), calls=%async_computation.10 | async-start | bytes 2621440 | tf_op jit(solution)/shard_map/reduce_scatter | solution.py:160
  241.7 2.8 copy-start.1
  244.5 0.9 copy-start.12
  245.4 1.0 copy-start.14
  286.0 49.9 %all-to-all-start.1 = ((bf16[128,2,1024]{2,1,0:T(2,128)(2,1)}), bf16[128,2,1024]{2,1,0:T(2,128)(2,1)S(1)}, u32[]{:S(2)}, u32[]{:S(2)}) async-start(bf16[128,2,1024]{2,1,0:T(2,128)(2,1)} %reshape.182), calls=%async_computation.2 | async-start | bytes 1048576 | tf_op jit(solution)/shard_map/all_to_all | solution.py:163
  335.9 39.4 %all-to-all-start.3 = ((bf16[128,2,1024]{2,1,0:T(2,128)(2,1)}), bf16[128,2,1024]{2,1,0:T(2,128)(2,1)S(1)}, u32[]{:S(2)}, u32[]{:S(2)}) async-start(bf16[128,2,1024]{2,1,0:T(2,128)(2,1)} %reshape.184), calls=%async_computation.5 | async-start | bytes 1048576 | tf_op jit(solution)/shard_map/all_to_all | solution.py:163
  343.1 4.6 %copy-start.4 = (bf16[2,512,2048]{2,1,0:T(8,128)(2,1)S(1)}, bf16[2,512,2048]{2,1,0:T(8,128)(2,1)}, u32[]{:S(2)}) copy-start(bf16[2,512,2048]{2,1,0:T(8,128)(2,1)} %all-gather.4.cloned.1.call-done) | copy-start | bytes 12582916
  345.4 2.3 copy-start.17
  345.4 2.3 copy-start.19
  347.7 2.2 copy-start.2
  351.4 1.5 copy-start.13
  351.4 1.5 copy-start.15
Sparse Core Ops, SparseCore 0:
  11.6 112.4 all-gather.5
  126.2 57.0 all-gather.3
  194.6 47.0 all-gather.7
  244.4 37.8 reduce-scatter.2
  285.0 37.1 reduce-scatter.4

commit v9 on v2

--- a/solution.py
+++ b/solution.py
@@ -91,18 +91,21 @@
     dispatch = jnp.sum(selected.astype(jnp.int32), axis=1).reshape(
         tok_count, experts, capacity
     ).astype(jnp.bfloat16)
-    outgoing = jnp.einsum(
-        "rec,rd->ecd", dispatch, tokens, preferred_element_type=jnp.float32
+    slot_gate = jnp.einsum(
+        "rkx,rk->rx", selected.astype(jnp.float32), gates.astype(jnp.float32)
+    ).reshape(tok_count, experts, capacity).astype(jnp.bfloat16)
+    zero = jnp.zeros_like(dispatch)
+    pick = jnp.stack(
+        [jnp.concatenate([dispatch, zero], axis=0), jnp.concatenate([zero, slot_gate], axis=0)], axis=0
+    )
+    sends = jnp.einsum(
+        "srec,rd->csed", pick, jnp.concatenate([tokens, cotangent], axis=0),
+        preferred_element_type=jnp.float32,
     ).astype(jnp.bfloat16)
-    slot_gate = jnp.einsum(
-        "rkx,rk->x", selected.astype(jnp.float32), gates.astype(jnp.float32)
-    ).reshape(experts, capacity)
-    lifted = jnp.einsum("rec,rd->ecd", dispatch, cotangent, preferred_element_type=jnp.float32)
-    cot_out = (lifted * slot_gate[..., None]).astype(jnp.bfloat16)
     token_sum = jnp.zeros((tok_count, features), jnp.float32)
     sums = None
     for chunk in range(capacity):
-        both = jnp.stack([outgoing[:, chunk], cot_out[:, chunk]], axis=0)
+        both = sends[chunk]
         arrived = lax.all_to_all(both, "expert", split_axis=1, concat_axis=1, tiled=True)
         gathered = lax.all_gather(arrived, "dp", axis=1, tiled=True)
         row_grads, gate_grad, up_grad, down_grad = expert_work(

time: 365 us -> 365 us (level)
    unnamed x75 -> x72, local copies, waits for them, and re-layouts: 10.2 us -> 10.4 us
where the time goes in v9:
time: 365 us; the launch traced here: 364 us
  waiting for transfers between devices  172 us (47%)
  blocking collectives  74.6 us (20%)
  starting transfers between devices  39.7 us (11%)
  matrix products  28.8 us (8%)
  local copies, waits for them, and re-layouts  21.6 us (6%)
  between operations  15.1 us (4%)
  other arithmetic  12.2 us (3%)
    all_to_all x1, blocking collectives, on_device(): lax.all_to_all(both, 'expert', split_axis=1, concat_axis=1, tiled=True)  74.6 us
    all_to_all x1, waiting for transfers between devices, on_device(): lax.all_to_all(both, 'expert', split_axis=1, concat_axis=1, tiled=True)  51.8 us
    ppermute x2, waiting for transfers between devices, swapped(): return lax.ppermute(block, axis, route)  46.4 us
    reduce_scatter x2, waiting for transfers between devices, on_device(): lax.psum_scatter(row_grads.reshape(replicas, experts, features), 'dp', sc...  41.6 us
    all_to_all x2, waiting for transfers between devices, on_device(): lax.all_to_all(summed_rows[0], 'expert', split_axis=0, concat_axis=0, til...  32.5 us
    all_to_all x2, starting transfers between devices, on_device(): lax.all_to_all(summed_rows[0], 'expert', split_axis=0, concat_axis=0, til...  23.9 us
    dot_general x12, matrix products, contract(): lax.dot_general(left, right, (((left_dim,), (right_dim,)), ((), ())), pre...  20.1 us
    unnamed x72, local copies, waits for them, and re-layouts  10.4 us
  transfers between devices with their start and end apart: 9, of which 6 were waited for; matrix products, arithmetic and copies ran while one was open for 14% of the time, Pallas kernels for 0%

profile of v9, /device:TPU:1, one launch (start us, length us, event | category | flops | bytes accessed | tf_op | source)
XLA Modules:
  0.0 364.4 jit_solution(17827820829193099093)
XLA Ops:
  7.2 0.8 copy.58
  8.1 1.6 gather_fusion
  11.4 0.7 fusion
  12.3 1.0 copy.67
  13.3 74.6 %all_to_all.34 = bf16[2,128,2048]{2,0,1:T(2,128)(2,1)S(1)} all-to-all(bf16[2,128,2048]{2,0,1:T(2,128)(2,1)S(1)} %copy.67), channel_id=1, replica_groups=mesh['dp'=4,'expert'=128] {'expert'}, dimensions={1} | all-to-all | bytes 2097152 | tf_op jit(solution)/shard_map/all_to_all | solution.py:109
  87.9 1.4 copy.68
  89.3 2.1 copy.71
  91.4 8.4 %all-to-all-start.2 = ((bf16[2,128,2048]{2,0,1:T(2,128)(2,1)}), bf16[2,128,2048]{2,0,1:T(2,128)(2,1)S(1)}, u32[]{:S(2)}, u32[]{:S(2)}) async-start(bf16[2,128,2048]{2,0,1:T(2,128)(2,1)} %copy.71), calls=%async_computation.3 | async-start | bytes 2097152 | tf_op jit(solution)/shard_map/all_to_all | solution.py:109
  99.8 1.3 constant_dynamic-update-slice_fusion.2
  101.1 1.2 constant_dynamic-update-slice_fusion.1
  102.3 51.8 %all-to-all-done.2 = bf16[2,128,2048]{2,0,1:T(2,128)(2,1)S(1)} async-done(((bf16[2,128,2048]{2,0,1:T(2,128)(2,1)}), bf16[2,128,2048]{2,0,1:T(2,128)(2,1)S(1)}, u32[]{:S(2)}, u32[]{:S(2)}) %all-to-all-start.2) | async-done | bytes 1048608 | tf_op jit(solution)/shard_map/all_to_all | solution.py:109
  154.2 1.3 copy.72
  155.6 1.2 constant_dynamic-update-slice_fusion
  156.8 4.4 %collective-permute-start = (bf16[3,192,2048]{2,1,0:T(8,128)(2,1)S(1)}, bf16[3,192,2048]{2,1,0:T(8,128)(2,1)}, u32[]{:S(2)}, u32[]{:S(2)}) collective-permute-start(bf16[3,192,2048]{2,1,0:T(8,128)(2,1)S(1)} %constant_dynamic-update-slice_fusion), channel_id=1, source_target_pairs={{0,64},{64,0},{1,65},{65,1},{2,66},{66,2},{3,67},{67,3},{4,68},{68... | collective-permute-start | bytes 7077896 | tf_op jit(solution)/shard_map/ppermute | solution.py:14
  161.3 2.5 collective-permute-start.1
  163.8 0.6 fusion.56
  165.1 46.4 %collective-permute-done.1 = f32[3,3,16]{2,0,1:T(4,128)S(1)} collective-permute-done((f32[3,3,16]{2,0,1:T(4,128)S(1)}, f32[3,3,16]{2,0,1:T(4,128)S(1)}, u32[]{:S(2)}, u32[]{:S(2)}) %collective-permute-start.1) | collective-permute-done | bytes 608 | tf_op jit(solution)/shard_map/ppermute | solution.py:14
  211.6 1.9 broadcast_select_fusion
  213.5 0.6 convert_bitcast_fusion.3
  214.1 0.3 copy.87
  214.4 0.3 copy.89
  214.7 0.3 copy.85
  215.0 1.4 fusion.16
  216.4 1.4 fusion.15
  217.8 1.4 fusion.17
  219.1 2.8 fusion.21
  221.9 0.3 copy-done.8
  222.2 2.1 fusion.20
  224.3 0.9 multiply_convert_fusion.4
  225.2 0.5 broadcast_in_dim.51
  225.7 0.9 fusion.62
  226.8 0.5 broadcast_in_dim.49
  227.3 2.4 add_convert_fusion.1
  230.1 2.8 fusion.22
  232.8 0.3 copy-done.6
  233.2 0.8 fusion.23
  234.0 0.4 copy-done.12
  234.5 0.9 multiply_convert_fusion.2
  235.4 0.6 copy-done.2
  236.0 0.9 fusion.60
  236.9 0.5 copy-done.4
  237.4 2.3 add_convert_fusion
  239.8 22.5 %reduce-scatter.3.cloned.1.call-done = bf16[1,128,2048]{2,1,0:T(8,128)(2,1)} async-done(((bf16[4,128,2048]{2,1,0:T(8,128)(2,1)}), bf16[1,128,2048]{2,1,0:T(8,128)(2,1)}) %reduce-scatter.3.cloned.1.call-update) | async-done | bytes 524304 | tf_op jit(solution)/shard_map/reduce_scatter | solution.py:116
  262.3 0.5 broadcast.80
  262.8 2.0 reduce.2
  264.8 1.2 reshape.193
  266.0 16.8 %all-to-all-start.1 = ((bf16[128,2,1024]{2,1,0:T(2,128)(2,1)}), bf16[128,2,1024]{2,1,0:T(2,128)(2,1)S(1)}, u32[]{:S(2)}, u32[]{:S(2)}) async-start(bf16[128,2,1024]{2,1,0:T(2,128)(2,1)} %reshape.193), calls=%async_computation.2 | async-start | bytes 1048576 | tf_op jit(solution)/shard_map/all_to_all | solution.py:119
  283.1 19.1 %reduce-scatter.5.cloned.1.call-done = bf16[1,128,2048]{2,1,0:T(8,128)(2,1)} async-done(((bf16[4,128,2048]{2,1,0:T(8,128)(2,1)}), bf16[1,128,2048]{2,1,0:T(8,128)(2,1)}) %reduce-scatter.5.cloned.1.call-update) | async-done | bytes 524304 | tf_op jit(solution)/shard_map/reduce_scatter | solution.py:116
  302.2 2.0 reduce.3
  304.2 1.2 reshape.195
  305.4 10.6 %all-to-all-done.1 = bf16[128,2,1024]{2,1,0:T(2,128)(2,1)S(1)} async-done(((bf16[128,2,1024]{2,1,0:T(2,128)(2,1)}), bf16[128,2,1024]{2,1,0:T(2,128)(2,1)S(1)}, u32[]{:S(2)}, u32[]{:S(2)}) %all-to-all-start.1) | async-done | bytes 524320 | tf_op jit(solution)/shard_map/all_to_all | solution.py:119
  316.0 7.1 %all-to-all-start.3 = ((bf16[128,2,1024]{2,1,0:T(2,128)(2,1)}), bf16[128,2,1024]{2,1,0:T(2,128)(2,1)S(1)}, u32[]{:S(2)}, u32[]{:S(2)}) async-start(bf16[128,2,1024]{2,1,0:T(2,128)(2,1)} %reshape.195), calls=%async_computation.5 | async-start | bytes 1048576 | tf_op jit(solution)/shard_map/all_to_all | solution.py:119
  323.2 2.3 fusion.18
  325.5 3.2 fusion.5
  328.7 0.6 fusion.19
  329.4 1.5 fusion.6
  330.9 0.6 fusion.8
  331.5 0.4 copy-done.22
  332.0 1.5 fusion.4
  333.5 0.4 reshape.194
  334.0 0.4 fusion.38
  334.4 22.0 %all-to-all-done.3 = bf16[128,2,1024]{2,1,0:T(2,128)(2,1)S(1)} async-done(((bf16[128,2,1024]{2,1,0:T(2,128)(2,1)}), bf16[128,2,1024]{2,1,0:T(2,128)(2,1)S(1)}, u32[]{:S(2)}, u32[]{:S(2)}) %all-to-all-start.3) | async-done | bytes 524320 | tf_op jit(solution)/shard_map/all_to_all | solution.py:119
  356.3 0.4 reshape.196
  356.8 1.0 fusion.7
  (102 shorter events, 3.1 us)
Async XLA Ops:
  7.2 0.9 copy-start
  7.2 212.0 %all-gather.3.cloned.1.call-start = ((), (), s32[]{:S(2)}) async-start(), calls=%async_computation.6 | async-start | bytes 5242880 | tf_op jit(solution)/shard_map/all_gather | solution.py:110
  8.1 2.8 copy-start.20
  8.1 3.3 copy-start.15
  8.1 3.3 copy-start.16
  91.4 62.8 %all-to-all-start.2 = ((bf16[2,128,2048]{2,0,1:T(2,128)(2,1)}), bf16[2,128,2048]{2,0,1:T(2,128)(2,1)S(1)}, u32[]{:S(2)}, u32[]{:S(2)}) async-start(bf16[2,128,2048]{2,0,1:T(2,128)(2,1)} %copy.71), calls=%async_computation.3 | async-start | bytes 2097152 | tf_op jit(solution)/shard_map/all_to_all | solution.py:109
  99.8 130.3 %all-gather.5.cloned.1.call-start = ((), (), s32[]{:S(2)}) async-start(), calls=%async_computation.8 | async-start | bytes 5242880 | tf_op jit(solution)/shard_map/all_gather | solution.py:110
  102.3 58.9 %copy-start.17 = (f32[1,3,16]{2,0,1:T(1,128)S(1)}, f32[1,3,16]{2,0,1:T(1,128)}, u32[]{:S(2)}) copy-start(f32[1,3,16]{2,0,1:T(1,128)} %param.21) | copy-start | bytes 580
  102.3 58.9 %copy-start.18 = (f32[1,3,16]{2,0,1:T(1,128)S(1)}, f32[1,3,16]{2,0,1:T(1,128)}, u32[]{:S(2)}) copy-start(f32[1,3,16]{2,0,1:T(1,128)} %param.20) | copy-start | bytes 580
  102.3 58.9 %copy-start.19 = (f32[1,3,16]{2,0,1:T(1,128)S(1)}, f32[1,3,16]{2,0,1:T(1,128)}, u32[]{:S(2)}) copy-start(f32[1,3,16]{2,0,1:T(1,128)} %param.19) | copy-start | bytes 580
  155.5 106.8 %reduce-scatter.3.cloned.1.call-start = ((), (), s32[]{:S(2)}) async-start(), calls=%async_computation.7 | async-start | bytes 2621440 | tf_op jit(solution)/shard_map/reduce_scatter | solution.py:116
  156.8 54.8 %copy-start.5 = (bf16[3,192,2048]{2,1,0:T(8,128)(2,1)}, bf16[3,192,2048]{2,1,0:T(8,128)(2,1)S(1)}, u32[]{:S(2)}) copy-start(bf16[3,192,2048]{2,1,0:T(8,128)(2,1)S(1)} %constant_dynamic-update-slice_fusion) | copy-start | bytes 7077892
  156.8 54.8 %collective-permute-start = (bf16[3,192,2048]{2,1,0:T(8,128)(2,1)S(1)}, bf16[3,192,2048]{2,1,0:T(8,128)(2,1)}, u32[]{:S(2)}, u32[]{:S(2)}) collective-permute-start(bf16[3,192,2048]{2,1,0:T(8,128)(2,1)S(1)} %constant_dynamic-update-slice_fusion), channel_id=1, source_target_pairs={{0,64},{64,0},{1,65},{65,1},{2,66},{66,2},{3,67},{67,3},{4,68},{68... | collective-permute-start | bytes 7077896 | tf_op jit(solution)/shard_map/ppermute | solution.py:14
  161.3 50.2 %collective-permute-start.1 = (f32[3,3,16]{2,0,1:T(4,128)S(1)}, f32[3,3,16]{2,0,1:T(4,128)S(1)}, u32[]{:S(2)}, u32[]{:S(2)}) collective-permute-start(f32[3,3,16]{2,0,1:T(4,128)S(1)} %pad_maximum_fusion), channel_id=1, source_target_pairs={{0,64},{64,0},{1,65},{65,1},{2,66},{66,2},{3,67},{67,3},{4,68},{68... | collective-permute-start | bytes 1736 | tf_op jit(solution)/shard_map/ppermute | solution.py:14
  219.1 3.1 copy-start.8
  221.9 2.4 copy-start.25
  222.2 2.1 copy-start.11
  224.2 1.0 copy-start.27
  225.2 2.1 copy-start.13
  225.7 1.1 copy-start.1
  227.3 2.4 copy-start.3
  229.7 3.1 copy-start.10
  229.8 72.4 %reduce-scatter.5.cloned.1.call-start = ((), (), s32[]{:S(2)}) async-start(), calls=%async_computation.9 | async-start | bytes 2621440 | tf_op jit(solution)/shard_map/reduce_scatter | solution.py:116
  230.1 3.1 copy-start.6
  233.2 0.9 copy-start.21
  233.2 1.3 copy-start.12
  234.4 0.9 copy-start.23
  234.5 1.5 copy-start.2
  236.0 1.4 copy-start.4
  266.0 57.2 %copy-start.14 = (bf16[512,192]{0,1:T(8,128)(2,1)S(1)}, bf16[512,192]{0,1:T(8,128)(2,1)}, u32[]{:S(2)}) copy-start(bf16[512,192]{0,1:T(8,128)(2,1)} %copy-done.13) | copy-start | bytes 589828
  266.0 50.0 %all-to-all-start.1 = ((bf16[128,2,1024]{2,1,0:T(2,128)(2,1)}), bf16[128,2,1024]{2,1,0:T(2,128)(2,1)S(1)}, u32[]{:S(2)}, u32[]{:S(2)}) async-start(bf16[128,2,1024]{2,1,0:T(2,128)(2,1)} %reshape.193), calls=%async_computation.2 | async-start | bytes 1048576 | tf_op jit(solution)/shard_map/all_to_all | solution.py:119
  316.0 40.3 %all-to-all-start.3 = ((bf16[128,2,1024]{2,1,0:T(2,128)(2,1)}), bf16[128,2,1024]{2,1,0:T(2,128)(2,1)S(1)}, u32[]{:S(2)}, u32[]{:S(2)}) async-start(bf16[128,2,1024]{2,1,0:T(2,128)(2,1)} %reshape.195), calls=%async_computation.5 | async-start | bytes 1048576 | tf_op jit(solution)/shard_map/all_to_all | solution.py:119
  323.2 5.6 %copy-start.9 = (bf16[2,512,2048]{2,1,0:T(8,128)(2,1)S(1)}, bf16[2,512,2048]{2,1,0:T(8,128)(2,1)}, u32[]{:S(2)}) copy-start(bf16[2,512,2048]{2,1,0:T(8,128)(2,1)} %all-gather.3.cloned.1.call-done) | copy-start | bytes 12582916
  325.5 3.9 %copy-start.7 = (bf16[2,512,2048]{2,1,0:T(8,128)(2,1)S(1)}, bf16[2,512,2048]{2,1,0:T(8,128)(2,1)}, u32[]{:S(2)}) copy-start(bf16[2,512,2048]{2,1,0:T(8,128)(2,1)} %all-gather.5.cloned.1.call-done) | copy-start | bytes 12582916
  329.4 1.5 copy-start.26
  329.4 1.5 copy-start.28
  330.9 1.0 copy-start.22
  330.9 1.1 copy-start.24
Sparse Core Ops, SparseCore 0:
  89.4 49.0 all-gather.2
  155.6 49.0 all-gather.4
  229.9 32.3 reduce-scatter.2
  265.0 37.1 reduce-scatter.4

commit v10 on v9

--- a/solution.py
+++ b/solution.py
@@ -113,13 +113,19 @@
         )
         part = (gate_grad, up_grad, down_grad)
         sums = part if sums is None else tuple(a + b for a, b in zip(sums, part))
-        summed_rows = lax.psum_scatter(
-            row_grads.reshape(replicas, experts, features), "dp", scatter_dimension=0, tiled=True
-        )
-        returned = lax.all_to_all(summed_rows[0], "expert", split_axis=0, concat_axis=0, tiled=True)
-        token_sum = token_sum + jnp.einsum(
-            "re,ed->rd", dispatch[:, :, chunk], returned, preferred_element_type=jnp.float32
-        )
+        halves = 2 if chunk == capacity - 1 else 1
+        width = features // halves
+        pieces = []
+        for half in range(halves):
+            cols = slice(half * width, (half + 1) * width)
+            summed_rows = lax.psum_scatter(
+                row_grads[:, cols].reshape(replicas, experts, width), "dp", scatter_dimension=0, tiled=True
+            )
+            returned = lax.all_to_all(summed_rows[0], "expert", split_axis=0, concat_axis=0, tiled=True)
+            pieces.append(jnp.einsum(
+                "re,ed->rd", dispatch[:, :, chunk], returned, preferred_element_type=jnp.float32
+            ))
+        token_sum = token_sum + jnp.concatenate(pieces, axis=1)
     token_grads = token_sum.astype(jnp.bfloat16)
     gate_grad, up_grad, down_grad = (x.astype(jnp.bfloat16) for x in sums)
     return (token_grads, gate_grad[None], up_grad[None], down_grad[None])

time: 365 us -> 376 us (1.030)
  starting transfers between devices: 39.7 us -> 64.2 us
  waiting for transfers between devices: 172 us -> 153 us
    ppermute x2, waiting for transfers between devices: 46.4 us -> 7 us  [swapped(): return lax.ppermute(block, axis, route)]
    all_to_all x2 -> x3, starting transfers between devices: 23.9 us -> 45.8 us  [on_device(): lax.all_to_all(summed_rows[0], 'expert', split_axis=0, concat_axis=0, til...]
    all_gather x2, waiting for transfers between devices: 0.02 us -> 16.8 us  [on_device(): gathered = lax.all_gather(arrived, 'dp', axis=1, tiled=True)]
    reduce_scatter x2 -> x3, waiting for transfers between devices: 41.6 us -> 53.6 us  [on_device(): lax.psum_scatter(row_grads[:, cols].reshape(replicas, experts, width), 'd...]
    all_to_all x1, waiting for transfers between devices: 51.8 us -> 46.5 us  [on_device(): lax.all_to_all(both, 'expert', split_axis=1, concat_axis=1, tiled=True)]
    all_to_all x2 -> x3, waiting for transfers between devices: 32.5 us -> 29 us  [on_device(): lax.all_to_all(summed_rows[0], 'expert', split_axis=0, concat_axis=0, til...]
    unnamed x72 -> x70, local copies, waits for them, and re-layouts: 10.4 us -> 11.8 us
  transfers between devices with their start and end apart: 9 -> 11, of which waited for: 6 -> 8; matrix products, arithmetic and copies ran while one was open for 14% -> 15% of each run, Pallas kernels for 0% -> 0%
where the time goes in v10:
time: 376 us; the launch traced here: 375 us
  waiting for transfers between devices  153 us (41%)
  blocking collectives  74.6 us (20%)
  starting transfers between devices  64.2 us (17%)
  matrix products  30.2 us (8%)
  local copies, waits for them, and re-layouts  23.2 us (6%)
  between operations  15.1 us (4%)
  other arithmetic  13.8 us (4%)
    all_to_all x1, blocking collectives, on_device(): lax.all_to_all(both, 'expert', split_axis=1, concat_axis=1, tiled=True)  74.6 us
    reduce_scatter x3, waiting for transfers between devices, on_device(): lax.psum_scatter(row_grads[:, cols].reshape(replicas, experts, width), 'd...  53.6 us
    all_to_all x1, waiting for transfers between devices, on_device(): lax.all_to_all(both, 'expert', split_axis=1, concat_axis=1, tiled=True)  46.5 us
    all_to_all x3, starting transfers between devices, on_device(): lax.all_to_all(summed_rows[0], 'expert', split_axis=0, concat_axis=0, til...  45.8 us
    all_to_all x3, waiting for transfers between devices, on_device(): lax.all_to_all(summed_rows[0], 'expert', split_axis=0, concat_axis=0, til...  29 us
    dot_general x12, matrix products, contract(): lax.dot_general(left, right, (((left_dim,), (right_dim,)), ((), ())), pre...  22.9 us
    all_gather x2, waiting for transfers between devices, on_device(): gathered = lax.all_gather(arrived, 'dp', axis=1, tiled=True)  16.8 us
    unnamed x70, local copies, waits for them, and re-layouts  11.8 us
  transfers between devices with their start and end apart: 11, of which 8 were waited for; matrix products, arithmetic and copies ran while one was open for 15% of the time, Pallas kernels for 0%

profile of v10, /device:TPU:1, one launch (start us, length us, event | category | flops | bytes accessed | tf_op | source)
XLA Modules:
  0.0 374.5 jit_solution(5694359513112575059)
XLA Ops:
  7.2 0.8 copy.59
  8.1 1.6 gather_fusion
  11.4 0.7 fusion
  12.3 1.0 copy.72
  13.3 74.6 %all_to_all.46 = bf16[2,128,2048]{2,0,1:T(2,128)(2,1)S(1)} all-to-all(bf16[2,128,2048]{2,0,1:T(2,128)(2,1)S(1)} %copy.72), channel_id=1, replica_groups=mesh['dp'=4,'expert'=128] {'expert'}, dimensions={1} | all-to-all | bytes 2097152 | tf_op jit(solution)/shard_map/all_to_all | solution.py:109
  87.9 1.3 copy.73
  89.2 2.1 copy.68
  91.3 8.4 %all-to-all-start = ((bf16[2,128,2048]{2,0,1:T(2,128)(2,1)}), bf16[2,128,2048]{2,0,1:T(2,128)(2,1)S(1)}, u32[]{:S(2)}, u32[]{:S(2)}) async-start(bf16[2,128,2048]{2,0,1:T(2,128)(2,1)} %copy.68), calls=%async_computation | async-start | bytes 2097152 | tf_op jit(solution)/shard_map/all_to_all | solution.py:109
  99.8 1.3 constant_dynamic-update-slice_fusion.2
  101.1 1.2 constant_dynamic-update-slice_fusion.1
  102.4 5.1 %collective-permute-start = (bf16[3,192,2048]{2,1,0:T(8,128)(2,1)S(1)}, bf16[3,192,2048]{2,1,0:T(8,128)(2,1)}, u32[]{:S(2)}, u32[]{:S(2)}) collective-permute-start(bf16[3,192,2048]{2,1,0:T(8,128)(2,1)S(1)} %constant_dynamic-update-slice_fusion), channel_id=1, source_target_pairs={{0,64},{64,0},{1,65},{65,1},{2,66},{66,2},{3,67},{67,3},{4,68},{68... | collective-permute-start | bytes 7077896 | tf_op jit(solution)/shard_map/ppermute | solution.py:14
  107.6 46.5 %all-to-all-done = bf16[2,128,2048]{2,0,1:T(2,128)(2,1)S(1)} async-done(((bf16[2,128,2048]{2,0,1:T(2,128)(2,1)}), bf16[2,128,2048]{2,0,1:T(2,128)(2,1)S(1)}, u32[]{:S(2)}, u32[]{:S(2)}) %all-to-all-start) | async-done | bytes 1048608 | tf_op jit(solution)/shard_map/all_to_all | solution.py:109
  154.1 1.3 copy.69
  155.6 4.6 %collective-permute-start.1 = (f32[3,3,16]{2,0,1:T(4,128)S(1)}, f32[3,3,16]{2,0,1:T(4,128)S(1)}, u32[]{:S(2)}, u32[]{:S(2)}) collective-permute-start(f32[3,3,16]{2,0,1:T(4,128)S(1)} %pad_maximum_fusion), channel_id=1, source_target_pairs={{0,64},{64,0},{1,65},{65,1},{2,66},{66,2},{3,67},{67,3},{4,68},{68... | collective-permute-start | bytes 1736 | tf_op jit(solution)/shard_map/ppermute | solution.py:14
  160.2 0.6 fusion.60
  161.5 7.0 %collective-permute-done.1 = f32[3,3,16]{2,0,1:T(4,128)S(1)} collective-permute-done((f32[3,3,16]{2,0,1:T(4,128)S(1)}, f32[3,3,16]{2,0,1:T(4,128)S(1)}, u32[]{:S(2)}, u32[]{:S(2)}) %collective-permute-start.1) | collective-permute-done | bytes 608 | tf_op jit(solution)/shard_map/ppermute | solution.py:14
  168.5 2.1 broadcast_select_fusion
  170.6 0.6 convert_bitcast_fusion.3
  172.1 1.4 fusion.16
  173.5 1.4 fusion.15
  174.9 1.4 fusion.17
  176.3 2.8 fusion.22
  179.1 0.3 copy-done.6
  179.5 2.1 fusion.23
  181.6 0.9 multiply_convert_fusion.2
  182.5 0.5 broadcast_in_dim.51
  183.0 0.9 fusion.64
  184.1 0.5 broadcast_in_dim.49
  184.6 1.0 add_convert_fusion
  185.8 1.5 fusion.70
  187.4 0.5 reduce-scatter.8.cloned.1.call-update
  187.9 16.8 %all-gather.3.cloned.1.call-done = bf16[2,512,2048]{2,1,0:T(8,128)(2,1)} async-done(((bf16[2,128,2048]{2,1,0:T(8,128)(2,1)}), bf16[2,512,2048]{2,1,0:T(8,128)(2,1)}) %all-gather.3.cloned.1.call-update) | async-done | bytes 4194320 | tf_op jit(solution)/shard_map/all_gather | solution.py:110
  204.8 2.8 fusion.21
  207.8 2.1 fusion.20
  210.0 0.9 multiply_convert_fusion.4
  211.0 0.6 copy-done.2
  211.6 0.9 fusion.66
  212.5 0.5 copy-done.4
  213.0 2.3 add_convert_fusion.1
  215.3 22.9 %reduce-scatter.6.cloned.1.call-done = bf16[1,128,1024]{2,1,0:T(8,128)(2,1)} async-done(((bf16[4,128,1024]{2,1,0:T(8,128)(2,1)}), bf16[1,128,1024]{2,1,0:T(8,128)(2,1)}) %reduce-scatter.6.cloned.1.call-update) | async-done | bytes 262160 | tf_op jit(solution)/shard_map/reduce_scatter | solution.py:121
  238.2 0.5 broadcast.80
  238.7 1.7 reduce.4
  240.4 0.9 reshape.204
  241.3 18.3 %all-to-all-start.3 = ((bf16[128,2,512]{2,1,0:T(2,128)(2,1)}), bf16[128,2,512]{2,1,0:T(2,128)(2,1)S(1)}, u32[]{:S(2)}, u32[]{:S(2)}) async-start(bf16[128,2,512]{2,1,0:T(2,128)(2,1)} %reshape.204), calls=%async_computation.5 | async-start | bytes 524288 | tf_op jit(solution)/shard_map/all_to_all | solution.py:124
  259.6 12.5 %reduce-scatter.8.cloned.1.call-done = bf16[1,128,1024]{2,1,0:T(8,128)(2,1)} async-done(((bf16[4,128,1024]{2,1,0:T(8,128)(2,1)}), bf16[1,128,1024]{2,1,0:T(8,128)(2,1)}) %reduce-scatter.8.cloned.1.call-update) | async-done | bytes 262160 | tf_op jit(solution)/shard_map/reduce_scatter | solution.py:121
  272.2 1.7 reduce.3
  273.9 0.9 reshape.202
  274.8 7.2 %all-to-all-done.3 = bf16[128,2,512]{2,1,0:T(2,128)(2,1)S(1)} async-done(((bf16[128,2,512]{2,1,0:T(2,128)(2,1)}), bf16[128,2,512]{2,1,0:T(2,128)(2,1)S(1)}, u32[]{:S(2)}, u32[]{:S(2)}) %all-to-all-start.3) | async-done | bytes 262176 | tf_op jit(solution)/shard_map/all_to_all | solution.py:124
  282.0 10.8 %all-to-all-start.4 = ((bf16[128,2,512]{2,1,0:T(2,128)(2,1)}), bf16[128,2,512]{2,1,0:T(2,128)(2,1)S(1)}, u32[]{:S(2)}, u32[]{:S(2)}) async-start(bf16[128,2,512]{2,1,0:T(2,128)(2,1)} %reshape.202), calls=%async_computation.7 | async-start | bytes 524288 | tf_op jit(solution)/shard_map/all_to_all | solution.py:124
  293.1 2.2 fusion.18
  295.3 18.1 %reduce-scatter.4.cloned.1.call-done = bf16[1,128,2048]{2,1,0:T(8,128)(2,1)} async-done(((bf16[4,128,2048]{2,1,0:T(8,128)(2,1)}), bf16[1,128,2048]{2,1,0:T(8,128)(2,1)}) %reduce-scatter.4.cloned.1.call-update) | async-done | bytes 524304 | tf_op jit(solution)/shard_map/reduce_scatter | solution.py:121
  313.4 2.0 reduce.2
  315.5 1.2 reshape.200
  316.6 16.7 %all-to-all-start.1 = ((bf16[128,2,1024]{2,1,0:T(2,128)(2,1)}), bf16[128,2,1024]{2,1,0:T(2,128)(2,1)S(1)}, u32[]{:S(2)}, u32[]{:S(2)}) async-start(bf16[128,2,1024]{2,1,0:T(2,128)(2,1)} %reshape.200), calls=%async_computation.2 | async-start | bytes 1048576 | tf_op jit(solution)/shard_map/all_to_all | solution.py:124
  333.3 3.2 fusion.5
  336.5 2.2 fusion.19
  338.8 1.5 fusion.6
  340.3 0.9 copy-done.9
  341.3 0.6 fusion.8
  341.9 0.4 copy-done.20
  342.4 1.5 fusion.4
  344.8 21.7 %all-to-all-done.1 = bf16[128,2,1024]{2,1,0:T(2,128)(2,1)S(1)} async-done(((bf16[128,2,1024]{2,1,0:T(2,128)(2,1)}), bf16[128,2,1024]{2,1,0:T(2,128)(2,1)S(1)}, u32[]{:S(2)}, u32[]{:S(2)}) %all-to-all-start.1) | async-done | bytes 524320 | tf_op jit(solution)/shard_map/all_to_all | solution.py:124
  366.5 0.4 reshape.201
  367.0 1.0 fusion.7
  (108 shorter events, 5.1 us)
Async XLA Ops:
  7.2 0.9 copy-start
  7.2 169.2 %all-gather.5.cloned.1.call-start = ((), (), s32[]{:S(2)}) async-start(), calls=%async_computation.10 | async-start | bytes 5242880 | tf_op jit(solution)/shard_map/all_gather | solution.py:110
  8.1 2.8 copy-start.18
  8.1 3.3 copy-start.13
  8.1 3.3 copy-start.14
  91.3 62.8 %all-to-all-start = ((bf16[2,128,2048]{2,0,1:T(2,128)(2,1)}), bf16[2,128,2048]{2,0,1:T(2,128)(2,1)S(1)}, u32[]{:S(2)}, u32[]{:S(2)}) async-start(bf16[2,128,2048]{2,0,1:T(2,128)(2,1)} %copy.68), calls=%async_computation | async-start | bytes 2097152 | tf_op jit(solution)/shard_map/all_to_all | solution.py:109
  99.7 105.1 %all-gather.3.cloned.1.call-start = ((), (), s32[]{:S(2)}) async-start(), calls=%async_computation.8 | async-start | bytes 5242880 | tf_op jit(solution)/shard_map/all_gather | solution.py:110
  99.8 2.6 copy-start.10
  102.3 53.2 %copy-start.15 = (f32[1,3,16]{2,0,1:T(1,128)S(1)}, f32[1,3,16]{2,0,1:T(1,128)}, u32[]{:S(2)}) copy-start(f32[1,3,16]{2,0,1:T(1,128)} %param.21) | copy-start | bytes 580
  102.4 53.2 %copy-start.16 = (f32[1,3,16]{2,0,1:T(1,128)S(1)}, f32[1,3,16]{2,0,1:T(1,128)}, u32[]{:S(2)}) copy-start(f32[1,3,16]{2,0,1:T(1,128)} %param.20) | copy-start | bytes 580
  102.4 53.2 %copy-start.17 = (f32[1,3,16]{2,0,1:T(1,128)S(1)}, f32[1,3,16]{2,0,1:T(1,128)}, u32[]{:S(2)}) copy-start(f32[1,3,16]{2,0,1:T(1,128)} %param.19) | copy-start | bytes 580
  102.4 66.1 %copy-start.5 = (bf16[3,192,2048]{2,1,0:T(8,128)(2,1)}, bf16[3,192,2048]{2,1,0:T(8,128)(2,1)S(1)}, u32[]{:S(2)}) copy-start(bf16[3,192,2048]{2,1,0:T(8,128)(2,1)S(1)} %constant_dynamic-update-slice_fusion) | copy-start | bytes 7077892
  102.4 66.1 %collective-permute-start = (bf16[3,192,2048]{2,1,0:T(8,128)(2,1)S(1)}, bf16[3,192,2048]{2,1,0:T(8,128)(2,1)}, u32[]{:S(2)}, u32[]{:S(2)}) collective-permute-start(bf16[3,192,2048]{2,1,0:T(8,128)(2,1)S(1)} %constant_dynamic-update-slice_fusion), channel_id=1, source_target_pairs={{0,64},{64,0},{1,65},{65,1},{2,66},{66,2},{3,67},{67,3},{4,68},{68... | collective-permute-start | bytes 7077896 | tf_op jit(solution)/shard_map/ppermute | solution.py:14
  155.5 82.7 %reduce-scatter.6.cloned.1.call-start = ((), (), s32[]{:S(2)}) async-start(), calls=%async_computation.11 | async-start | bytes 1310720 | tf_op jit(solution)/shard_map/reduce_scatter | solution.py:121
  155.6 12.9 %collective-permute-start.1 = (f32[3,3,16]{2,0,1:T(4,128)S(1)}, f32[3,3,16]{2,0,1:T(4,128)S(1)}, u32[]{:S(2)}, u32[]{:S(2)}) collective-permute-start(f32[3,3,16]{2,0,1:T(4,128)S(1)} %pad_maximum_fusion), channel_id=1, source_target_pairs={{0,64},{64,0},{1,65},{65,1},{2,66},{66,2},{3,67},{67,3},{4,68},{68... | collective-permute-start | bytes 1736 | tf_op jit(solution)/shard_map/ppermute | solution.py:14
  176.3 3.1 copy-start.6
  179.1 2.4 copy-start.19
  179.5 2.1 copy-start.11
  181.5 1.0 copy-start.21
  183.0 1.2 copy-start.1
  184.6 1.2 copy-start.3
  187.3 84.9 %reduce-scatter.8.cloned.1.call-start = ((), (), s32[]{:S(2)}) async-start(), calls=%async_computation.12 | async-start | bytes 1310720 | tf_op jit(solution)/shard_map/reduce_scatter | solution.py:121
  187.9 125.6 %reduce-scatter.4.cloned.1.call-start = ((), (), s32[]{:S(2)}) async-start(), calls=%async_computation.9 | async-start | bytes 2621440 | tf_op jit(solution)/shard_map/reduce_scatter | solution.py:121
  204.8 3.1 copy-start.8
  207.8 2.2 copy-start.23
  207.8 2.2 copy-start.12
  210.0 1.0 copy-start.25
  210.0 1.6 copy-start.2
  211.6 1.4 copy-start.4
  241.3 40.7 %all-to-all-start.3 = ((bf16[128,2,512]{2,1,0:T(2,128)(2,1)}), bf16[128,2,512]{2,1,0:T(2,128)(2,1)S(1)}, u32[]{:S(2)}, u32[]{:S(2)}) async-start(bf16[128,2,512]{2,1,0:T(2,128)(2,1)} %reshape.204), calls=%async_computation.5 | async-start | bytes 524288 | tf_op jit(solution)/shard_map/all_to_all | solution.py:124
  282.0 34.6 %all-to-all-start.4 = ((bf16[128,2,512]{2,1,0:T(2,128)(2,1)}), bf16[128,2,512]{2,1,0:T(2,128)(2,1)S(1)}, u32[]{:S(2)}, u32[]{:S(2)}) async-start(bf16[128,2,512]{2,1,0:T(2,128)(2,1)} %reshape.202), calls=%async_computation.7 | async-start | bytes 524288 | tf_op jit(solution)/shard_map/all_to_all | solution.py:124
  316.6 49.9 %all-to-all-start.1 = ((bf16[128,2,1024]{2,1,0:T(2,128)(2,1)}), bf16[128,2,1024]{2,1,0:T(2,128)(2,1)S(1)}, u32[]{:S(2)}, u32[]{:S(2)}) async-start(bf16[128,2,1024]{2,1,0:T(2,128)(2,1)} %reshape.200), calls=%async_computation.2 | async-start | bytes 1048576 | tf_op jit(solution)/shard_map/all_to_all | solution.py:124
  333.3 5.4 %copy-start.7 = (bf16[2,512,2048]{2,1,0:T(8,128)(2,1)S(1)}, bf16[2,512,2048]{2,1,0:T(8,128)(2,1)}, u32[]{:S(2)}) copy-start(bf16[2,512,2048]{2,1,0:T(8,128)(2,1)} %all-gather.5.cloned.1.call-done) | copy-start | bytes 12582916
  336.5 3.8 %copy-start.26 = (f32[512,192]{0,1:T(8,128)S(1)}, f32[512,192]{0,1:T(8,128)}, u32[]{:S(2)}) copy-start(f32[512,192]{0,1:T(8,128)} %copy-done.25) | copy-start | bytes 1179652
  338.8 2.5 copy-start.9
  338.8 2.5 copy-start.24
  341.3 1.0 copy-start.20
  341.3 1.1 copy-start.22
Sparse Core Ops, SparseCore 0:
  89.3 49.0 all-gather.4
  155.6 49.1 all-gather.2
  207.6 30.5 reduce-scatter.5
  240.9 31.2 reduce-scatter.7
  274.9 38.5 reduce-scatter.3
